TPU v7x, 128 devices: a whole 4x4x4 slice. The times are simulated.
128 devices in a mesh: dp: 16 (over z, x_lo, core), mp: 8 (over y, x_hi).
Axes of the slice: x: 4 (x_hi: 2, x_lo: 2; x = x_hi * 2 + x_lo), y: 4, z: 4, core: 2. Of those that a mesh axis runs over, the one named last changes fastest.
Arguments:
- frozen_input_states: bfloat16 [8192, 8192], P('dp'), may hold values from -6 to 6
- updated_input_states: bfloat16 [8192, 8192], P('dp'), may hold values from -6 to 6
- weight: bfloat16 [8192, 8192], P('dp', 'mp'), may hold values from -0.0625 to 0.0625
- adapter_down_weight: bfloat16 [8192, 64], P('mp'), may hold values from -0.0625 to 0.0625
- adapter_up_weight: bfloat16 [64, 8192], P(None, 'mp'), may hold values from -0.75 to 0.75
- flags: int32 [8192], P('dp'), may hold values from 0 to 1, as said below
- control: float32 [8192], replicated, may hold values from 0.1 to 1
Outputs:
- h_upd: bfloat16 [8192, 8192], P(('dp', 'mp'))
- grad_a: float32 [8192, 64], P('mp')
- grad_b: float32 [64, 8192], P(None, 'mp')
- loss: float32 [1], replicated
Inputs may be any that keep to these rules, and one draw needn't show every extreme that they name: `flags`: each data group's share of forget tokens is its own and may lie anywhere between a twentieth and nineteen twentieths.
All inputs are finite; a program needn't handle non-finite values.
Results may differ from a plain program's by a relative error of at most 0.0049.
Values may be sent and summed in bfloat16 or wider, within the bound.
No kernel may reach another device: no remote copies, remote signals or barrier semaphores. Data moves between devices by JAX's collectives and lax.ppermute only.
A program may use at most 128 MiB of HBM per device.

v0:
```python
import jax
import jax.numpy as jnp
from jax import lax
from jax.sharding import PartitionSpec as P

adapter_gain = 0.5
steer = 90.0
retain_weight = 1.2
loss_multiplier = 65536.0


def row_adder(source, piece):
    return jnp.dot(source, piece, preferred_element_type=jnp.float32)


def per_device(
    frozen_input_states,
    updated_input_states,
    weight,
    adapter_down_weight,
    adapter_up_weight,
    flags,
    control,
):
    group = frozen_input_states.shape[0]
    hidden_width = frozen_input_states.shape[1]
    parts = lax.axis_size("mp")
    share = group // parts
    mine_at = lax.axis_index("mp") * share
    ref_total = row_adder(frozen_input_states, lax.all_gather(weight, "dp", axis=0, tiled=True))
    base_total = row_adder(updated_input_states, lax.all_gather(weight, "dp", axis=0, tiled=True))
    unit = control * lax.rsqrt(jnp.sum(control * control) + 1e-06)
    forget_total = lax.psum(jnp.sum(flags).astype(jnp.float32), "dp")
    all_tokens = jnp.asarray(group * lax.axis_size("dp"), jnp.float32)
    n_forget = jnp.maximum(forget_total, 1.0)
    n_retain = jnp.maximum(all_tokens - forget_total, 1.0)
    stacked = jnp.stack([ref_total.astype(jnp.bfloat16), base_total.astype(jnp.bfloat16)])
    landed = lax.all_to_all(stacked, "mp", split_axis=1, concat_axis=2, tiled=True)
    ref_rows = landed[0]
    frozen_layer_rows = landed[1]
    complete_down_map = lax.all_gather(adapter_down_weight, "mp", axis=0, tiled=True)
    complete_up_map = lax.all_gather(adapter_up_weight, "mp", axis=1, tiled=True)
    mine = lax.dynamic_slice_in_dim(updated_input_states, mine_at, share, 0)
    flag_rows = lax.dynamic_slice_in_dim(flags, mine_at, share, 0)
    rank_projection = jnp.dot(mine, complete_down_map, preferred_element_type=jnp.float32).astype(
        jnp.bfloat16
    )
    updated_output = frozen_layer_rows.astype(jnp.float32) + adapter_gain * jnp.dot(
        rank_projection, complete_up_map, preferred_element_type=jnp.float32
    )
    is_forget = flag_rows.astype(jnp.float32)[:, None]
    target = is_forget * steer * unit[None, :] + (1.0 - is_forget) * ref_rows.astype(jnp.float32)
    state_difference = updated_output - target
    token_weight = is_forget / n_forget + retain_weight * (1.0 - is_forget) / n_retain
    local_loss = jnp.sum(
        token_weight * jnp.mean(state_difference * state_difference, axis=1, keepdims=True)
    )
    output_gradient = (
        loss_multiplier * 2.0 * adapter_gain / hidden_width * token_weight * state_difference
    ).astype(jnp.bfloat16)
    up_grad_t = jnp.dot(output_gradient.T, rank_projection, preferred_element_type=jnp.float32)
    middle_gradient = jnp.dot(
        output_gradient, complete_up_map.T, preferred_element_type=jnp.float32
    ).astype(jnp.bfloat16)
    down_grad = jnp.dot(mine.T, middle_gradient, preferred_element_type=jnp.float32)
    rows_mine = hidden_width // parts
    down_all, up_all, total_loss = lax.psum((down_grad, up_grad_t, local_loss), ("dp", "mp"))
    row_start = lax.axis_index("mp") * rows_mine
    down_part = lax.dynamic_slice_in_dim(down_all, row_start, rows_mine, 0)
    up_part = lax.dynamic_slice_in_dim(up_all, row_start, rows_mine, 0)
    return (updated_output.astype(jnp.bfloat16), down_part, up_part.T, total_loss.reshape(1))


def solution(mesh):
    in_specs = (
        P("dp", None),
        P("dp", None),
        P("dp", "mp"),
        P("mp", None),
        P(None, "mp"),
        P("dp"),
        P(),
    )
    out_specs = (P(("dp", "mp"), None), P("mp", None), P(None, "mp"), P())
    return jax.shard_map(
        per_device, mesh=mesh, in_specs=in_specs, out_specs=out_specs, check_vma=False
    )
```

profile of v0, /device:TPU:4, one launch (start us, length us, event | category | flops | bytes accessed | tf_op | source)
XLA Modules:
  0.0 386.3 jit_solution(11633589092768668788)
XLA Ops:
  7.2 0.0 all-gather.4.cloned.1.call-start
  7.2 0.7 all-gather.4.cloned.1.call-update
  7.9 0.0 all-gather.6.cloned.1.call-start
  7.9 0.7 all-gather.6.cloned.1.call-update
  8.6 95.0 %all-gather.4.cloned.1.call-done = bf16[8192,1024]{1,0:T(8,128)(2,1)} async-done(((bf16[512,1024]{1,0:T(8,128)(2,1)}), bf16[8192,1024]{1,0:T(8,128)(2,1)}) %all-gather.4.cloned.1.call-update) | async-done | bytes 16777232 | tf_op jit(solution)/shard_map/all_gather | solution.py:30
  103.6 0.0 copy-start.3
  103.6 14.9 %fusion.2 = bf16[1,512,1024]{2,1,0:T(8,128)(2,1)S(1)} fusion(bf16[512,8192]{1,0:T(8,128)(2,1)} %param.8, bf16[8192,1024]{1,0:T(8,128)(2,1)} %all-gather.4.cloned.1.call-done), kind=kOutput, calls=%fused_computation.10 | convolution fusion | flops 8590458880 | bytes 26214400 | tf_op jit(solution)/shard_map/dot_general | solution.py:13
  118.6 0.0 copy-done.3
  118.6 11.2 %fusion.1 = bf16[1,512,1024]{2,1,0:T(8,128)(2,1)S(1)} fusion(bf16[512,8192]{1,0:T(8,128)(2,1)} %param.7, bf16[8192,1024]{1,0:T(8,128)(2,1)S(1)} %copy-done.3), kind=kOutput, calls=%fused_computation.9 | convolution fusion | flops 8590458880 | bytes 26214400 | tf_op jit(solution)/shard_map/dot_general | solution.py:13
  129.8 0.2 pad_maximum_fusion
  130.0 3.5 copy.13
  133.5 0.0 copy-start.2
  133.5 0.0 copy-start.1
  133.5 7.4 %all-to-all-start = ((bf16[2,512,1024]{2,0,1:T(2,128)(2,1)}), bf16[2,512,1024]{2,0,1:T(2,128)(2,1)S(1)}, u32[]{:S(2)}, u32[]{:S(2)}) async-start(bf16[2,512,1024]{2,0,1:T(2,128)(2,1)} %copy.13), calls=%async_computation | async-start | bytes 4194304 | tf_op jit(solution)/shard_map/all_to_all | solution.py:38
  140.8 0.0 all-gather.8.cloned.1.call-start
  140.8 0.7 all-gather.8.cloned.1.call-update
  141.6 0.0 all-reduce.3.cloned.1.call-start
  141.6 0.0 copy-done.2
  141.6 0.6 reduce_sum.36
  142.9 49.1 %psum.28 = f32[]{:T(128)} all-reduce(f32[]{:T(128)S(6)} %convert_element_type.43), channel_id=1, replica_groups=mesh['dp'=16,'mp'=8] {'dp'}, use_global_device_ids=true, to_apply=%region_1.0 | all-reduce | flops 1 | bytes 8 | tf_op jit(solution)/shard_map/psum | solution.py:33
  192.0 0.0 copy-done.1
  192.0 0.6 multiply_reduce_fusion.1
  194.6 0.1 convert_multiply_fusion
  194.7 0.0 all-gather.6.cloned.1.call-done
  194.7 2.0 convolution_convert_fusion.3
  196.6 0.0 all-to-all-done
  196.6 1.2 copy.18
  197.8 0.5 slice_convert_fusion
  198.3 2.5 copy.16
  200.8 2.5 copy.15
  203.3 7.7 %all-gather.8.cloned.1.call-done = bf16[64,8192]{1,0:T(8,128)(2,1)} async-done(((bf16[64,1024]{1,0:T(8,128)(2,1)}), bf16[64,8192]{1,0:T(8,128)(2,1)}) %all-gather.8.cloned.1.call-update) | async-done | bytes 1048592 | tf_op jit(solution)/shard_map/all_gather | solution.py:42
  211.0 4.4 %multiply_reduce_fusion = (f32[64]{0:T(128)S(1)}, f32[64,8192]{1,0:T(8,128)S(1)}, bf16[64,8192]{1,0:T(8,128)(2,1)}) fusion(f32[64,8192]{1,0:T(8,128)} %bitcast.26, f32[64]{0:T(128)S(1)} %get-tuple-element.14, f32[8192]{0:T(1024)S(1)} %broadcast_multiply_fusion, f32[64]{0:T(128)S(1)} %get-tuple-element.13, f32[64,8192]{1,0:T(8,128)} %bitcast.27, ...), kind=kOutput, calls=%fused_computation.4 | convolution fusion | flops 71827392 | bytes 8430336 | tf_op jit(solution)/shard_map/dot_general | solution.py:48
  215.4 0.7 multiply_reduce_fusion.2
  216.1 0.0 copy-start
  216.1 1.8 fusion.8
  217.9 0.0 copy-done
  217.9 4.0 %fusion.3 = f32[8192,64]{0,1:T(8,128)} fusion(bf16[64,8192]{1,0:T(8,128)(2,1)S(1)} %copy-done, bf16[512,8192]{1,0:T(8,128)(2,1)} %param.8, s32[]{:T(128)S(6)} %select_n.8, f32[64,8192]{1,0:T(8,128)S(1)} %get-tuple-element.9, f32[64]{0:T(128)S(1)} %broadcast_multiply_fusion.1), kind=kOutput, calls=%fused_computation.13 | convolution fusion | flops 135270400 | bytes 6291716 | tf_op jit(solution)/shard_map/dot_general | solution.py:65
  221.9 0.0 all-reduce.3.cloned.1.call-update
  221.9 66.1 %psum.31 = f32[1]{0:T(128)} all-reduce(f32[1]{0:T(128)} %bitcast.5), channel_id=1, replica_groups=mesh['dp'=16,'mp'=8] {'dp','mp'}, use_global_device_ids=true, to_apply=%region_7.0 | all-reduce | flops 1 | bytes 8 | tf_op jit(solution)/shard_map/psum | solution.py:67
  288.0 89.8 %all-reduce.3.cloned.1.call-done = (f32[8192,64]{0,1:T(8,128)}, f32[8192,64]{0,1:T(8,128)}) async-done(((f32[8192,64]{0,1:T(8,128)}, f32[8192,64]{0,1:T(8,128)}), (f32[8192,64]{0,1:T(8,128)}, f32[8192,64]{0,1:T(8,128)})) %all-reduce.3.cloned.1.call-update) | async-done | bytes 4194320 | tf_op jit(solution)/shard_map/psum | solution.py:67
  377.9 1.9 dynamic-slice_bitcast_fusion
  (2 shorter events, 0.0 us)
Async XLA Ops:
  7.2 96.5 %all-gather.4.cloned.1.call-start = ((), (), s32[]{:S(2)}) async-start(), calls=%async_computation.1 | async-start | bytes 17825792 | tf_op jit(solution)/shard_map/all_gather | solution.py:30
  7.9 186.8 %all-gather.6.cloned.1.call-start = ((), (), s32[]{:S(2)}) async-start(), calls=%async_computation.2 | async-start | bytes 1179648 | tf_op jit(solution)/shard_map/all_gather | solution.py:41
  103.6 14.9 %copy-start.3 = (bf16[8192,1024]{1,0:T(8,128)(2,1)S(1)}, bf16[8192,1024]{1,0:T(8,128)(2,1)}, u32[]{:S(2)}) copy-start(bf16[8192,1024]{1,0:T(8,128)(2,1)} %all-gather.4.cloned.1.call-done) | copy-start | bytes 50331652
  133.5 8.2 %copy-start.2 = (s32[512]{0:T(512)S(1)}, s32[512]{0:T(512)}, u32[]{:S(2)}) copy-start(s32[512]{0:T(512)} %param.12) | copy-start | bytes 6148
  133.5 58.5 %copy-start.1 = (f32[8192]{0:T(1024)S(1)}, f32[8192]{0:T(1024)}, u32[]{:S(2)}) copy-start(f32[8192]{0:T(1024)} %param.13) | copy-start | bytes 98308
  133.5 63.2 %all-to-all-start = ((bf16[2,512,1024]{2,0,1:T(2,128)(2,1)}), bf16[2,512,1024]{2,0,1:T(2,128)(2,1)S(1)}, u32[]{:S(2)}, u32[]{:S(2)}) async-start(bf16[2,512,1024]{2,0,1:T(2,128)(2,1)} %copy.13), calls=%async_computation | async-start | bytes 4194304 | tf_op jit(solution)/shard_map/all_to_all | solution.py:38
  140.8 70.1 %all-gather.8.cloned.1.call-start = ((), (), s32[]{:S(2)}) async-start(), calls=%async_computation.3 | async-start | bytes 1179648 | tf_op jit(solution)/shard_map/all_gather | solution.py:42
  141.6 236.3 %all-reduce.3.cloned.1.call-start = ((), (), s32[]{:S(2)}) async-start(), calls=%async_computation.4 | async-start | bytes 8388608 | tf_op jit(solution)/shard_map/psum | solution.py:67
  216.1 1.8 copy-start
Sparse Core Ops, SparseCore 0:
  9.7 93.9 all-gather.3
  105.9 58.2 all-gather.5
  166.6 44.3 all-gather.7
  222.0 155.8 all-reduce.2
where the time goes:
time: 388 us; the launch traced here: 386 us
  waiting for transfers between devices  195 us (50%)
  blocking collectives  115 us (30%)
  matrix products  38.3 us (10%)
  between operations  16.5 us (4%)
  local copies, waits for them, and re-layouts  11.6 us (3%)
  starting transfers between devices  7.5 us (2%)
    all_gather x1, waiting for transfers between devices, per_device(): lax.all_gather(weight, 'dp', axis=0, tiled=True)  95 us
    psum x1, waiting for transfers between devices, per_device(): lax.psum((down_grad, up_grad_t, local_loss), ('dp', 'mp'))  89.8 us
    psum x1, blocking collectives, per_device(): lax.psum((down_grad, up_grad_t, local_loss), ('dp', 'mp'))  66.1 us
    psum x1, blocking collectives, per_device(): forget_total = lax.psum(jnp.sum(flags).astype(jnp.float32), 'dp')  49.1 us
    dot_general x2, matrix products, row_adder(): return jnp.dot(source, piece, preferred_element_type=jnp.float32)  26.1 us
  transfers between devices with their start and end apart: 5, of which 3 were waited for; matrix products, arithmetic and copies ran while one was open for 10% of the time, Pallas kernels for 0%

commit v1 on v0

v1 whole, which is shorter than its diff:
```python
import jax
import jax.numpy as jnp
from jax import lax
from jax.sharding import Mesh
from jax.sharding import PartitionSpec as P

adapter_gain = 0.5
steer = 90.0
retain_weight = 1.2
loss_multiplier = 65536.0

DP = ("chip", "core")


def row_adder(source, piece):
    return jnp.dot(source, piece, preferred_element_type=jnp.float32)


def gather_columns(weight):
    cols = weight.shape[1]
    half = cols // 2
    core = lax.axis_index("core")
    pair = lax.all_gather(weight, "core", axis=0, tiled=True)
    mine = lax.dynamic_slice_in_dim(pair, core * half, half, 1)
    rows_half = lax.all_gather(mine, "chip", axis=0, tiled=True)
    both = lax.all_gather(rows_half, "core", axis=0, tiled=False)
    return both


def per_device(
    frozen_input_states,
    updated_input_states,
    weight,
    adapter_down_weight,
    adapter_up_weight,
    flags,
    control,
):
    group = frozen_input_states.shape[0]
    hidden_width = frozen_input_states.shape[1]
    parts = lax.axis_size("mp")
    share = group // parts
    rows_mine = hidden_width // parts
    m = lax.axis_index("mp")

    all_flags = lax.all_gather(flags, DP, axis=0, tiled=True)
    forget_total = jnp.sum(all_flags).astype(jnp.float32)
    all_tokens = jnp.asarray(all_flags.shape[0], jnp.float32)
    n_forget = jnp.maximum(forget_total, 1.0)
    n_retain = jnp.maximum(all_tokens - forget_total, 1.0)

    halves = gather_columns(weight)
    ref_rows = jnp.concatenate(
        [row_adder(frozen_input_states, halves[h]).astype(jnp.bfloat16) for h in range(2)], axis=1
    )
    base_rows = jnp.concatenate(
        [row_adder(updated_input_states, halves[h]).astype(jnp.bfloat16) for h in range(2)], axis=1
    )

    my_rows = lax.dynamic_slice_in_dim(updated_input_states, m * rows_mine, rows_mine, 1)
    low_part = jnp.dot(my_rows, adapter_down_weight, preferred_element_type=jnp.float32)
    rank_projection = lax.psum(low_part, "mp").astype(jnp.bfloat16)

    updated_output = base_rows.astype(jnp.float32) + adapter_gain * jnp.dot(
        rank_projection, adapter_up_weight, preferred_element_type=jnp.float32
    )
    h_upd = lax.all_to_all(
        updated_output.astype(jnp.bfloat16), "mp", split_axis=0, concat_axis=1, tiled=True
    )

    unit = control * lax.rsqrt(jnp.sum(control * control) + 1e-06)
    unit_mine = lax.dynamic_slice_in_dim(unit, m * rows_mine, rows_mine, 0)
    is_forget = flags.astype(jnp.float32)[:, None]
    target = is_forget * steer * unit_mine[None, :] + (1.0 - is_forget) * ref_rows.astype(jnp.float32)
    state_difference = updated_output - target
    token_weight = is_forget / n_forget + retain_weight * (1.0 - is_forget) / n_retain
    local_loss = jnp.sum(
        token_weight * (jnp.sum(state_difference * state_difference, axis=1, keepdims=True) / hidden_width)
    )
    output_gradient = (
        loss_multiplier * 2.0 * adapter_gain / hidden_width * token_weight * state_difference
    ).astype(jnp.bfloat16)
    up_grad = jnp.dot(rank_projection.T, output_gradient, preferred_element_type=jnp.float32)
    middle_part = jnp.dot(output_gradient, adapter_up_weight.T, preferred_element_type=jnp.float32)
    middle_gradient = lax.psum(middle_part, "mp").astype(jnp.bfloat16)
    down_grad = jnp.dot(my_rows.T, middle_gradient, preferred_element_type=jnp.float32)
    down_part, up_part, loss_dp = lax.psum((down_grad, up_grad, local_loss), DP)
    total_loss = lax.psum(loss_dp, "mp")
    return (h_upd, down_part, up_part, total_loss.reshape(1))


def solution(mesh):
    dp_size, mp_size = mesh.devices.shape
    split = Mesh(mesh.devices.reshape(dp_size // 2, 2, mp_size), ("chip", "core", "mp"))
    in_specs = (
        P(DP, None),
        P(DP, None),
        P(DP, "mp"),
        P("mp", None),
        P(None, "mp"),
        P(DP),
        P(),
    )
    out_specs = (P(DP + ("mp",), None), P("mp", None), P(None, "mp"), P())
    return jax.shard_map(
        per_device, mesh=split, in_specs=in_specs, out_specs=out_specs, check_vma=False
    )
```

time: 388 us -> 515 us (1.33)
  waiting for transfers between devices: 195 us -> 303 us
  blocking collectives: 115 us -> 132 us
    all_gather x3, waiting for transfers between devices: 103 us -> 187 us  [the longest x1 169 us: gather_columns(): rows_half = lax.all_gather(mine, 'chip', axis=0, tiled=True)]
    psum x1, waiting for transfers between devices: 89.8 us -> 116 us  [per_device(): down_part, up_part, loss_dp = lax.psum((down_grad, up_grad, local_loss), DP)]
    all_gather x0 -> x1, blocking collectives: none -> 19 us  [per_device(): all_flags = lax.all_gather(flags, DP, axis=0, tiled=True)]
    dot_general x2 -> x4, matrix products: 26.1 us -> 35.2 us  [row_adder(): return jnp.dot(source, piece, preferred_element_type=jnp.float32)]
    dot_general x4 -> x5, matrix products: 12.2 us -> 6.25 us  [the longest x1 2.23 us: per_device(): jnp.dot(my_rows.T, middle_gradient, preferred_element_type=jnp.float32)]
    psum x2 -> x3, blocking collectives: 115 us -> 113 us  [the longest x1 47 us: per_device(): middle_gradient = lax.psum(middle_part, 'mp').astype(jnp.bfloat16)]
  transfers between devices with their start and end apart: 5 -> 5, of which waited for: 3 -> 3; matrix products, arithmetic and copies ran while one was open for 10% -> 1% of each run, Pallas kernels for 0% -> 0%
where the time goes in v1:
time: 515 us; the launch traced here: 513 us
  waiting for transfers between devices  303 us (59%)
  blocking collectives  132 us (26%)
  matrix products  41.4 us (8%)
  between operations  15.3 us (3%)
  starting transfers between devices  9.52 us (2%)
  local copies, waits for them, and re-layouts  8.87 us (2%)
    all_gather x1, waiting for transfers between devices, gather_columns(): rows_half = lax.all_gather(mine, 'chip', axis=0, tiled=True)  169 us
    psum x1, waiting for transfers between devices, per_device(): down_part, up_part, loss_dp = lax.psum((down_grad, up_grad, local_loss), DP)  116 us
    psum x1, blocking collectives, per_device(): middle_gradient = lax.psum(middle_part, 'mp').astype(jnp.bfloat16)  47 us
    psum x1, blocking collectives, per_device(): rank_projection = lax.psum(low_part, 'mp').astype(jnp.bfloat16)  38.4 us
    dot_general x4, matrix products, row_adder(): return jnp.dot(source, piece, preferred_element_type=jnp.float32)  35.2 us
    psum x1, blocking collectives, per_device(): down_part, up_part, loss_dp = lax.psum((down_grad, up_grad, local_loss), DP)  27.8 us
    all_gather x1, blocking collectives, per_device(): all_flags = lax.all_gather(flags, DP, axis=0, tiled=True)  19 us
    all_gather x1, waiting for transfers between devices, gather_columns(): pair = lax.all_gather(weight, 'core', axis=0, tiled=True)  17.4 us
  transfers between devices with their start and end apart: 5, of which 3 were waited for; matrix products, arithmetic and copies ran while one was open for 1% of the time, Pallas kernels for 0%

profile of v1, /device:TPU:4, one launch (start us, length us, event | category | flops | bytes accessed | tf_op | source)
XLA Modules:
  0.0 513.3 jit_solution(15413785442603175498)
XLA Ops:
  7.2 0.0 copy-start
  7.2 0.0 all-gather.6.cloned.1.call-start
  7.2 0.7 all-gather.6.cloned.1.call-update
  7.9 0.0 all-gather.8.cloned.1.call-start
  8.0 17.4 %all-gather.6.cloned.1.call-done = bf16[1024,1024]{1,0:T(8,128)(2,1)} async-done(((bf16[512,1024]{1,0:T(8,128)(2,1)}), bf16[1024,1024]{1,0:T(8,128)(2,1)}) %all-gather.6.cloned.1.call-update) | async-done | bytes 2097168 | tf_op jit(solution)/shard_map/all_gather | solution.py:23
  25.4 2.3 constant_dynamic-slice_fusion
  27.6 0.0 all-gather.8.cloned.1.call-update
  27.6 0.0 all-gather.10.cloned.1.call-start
  27.7 169.4 %all-gather.8.cloned.1.call-done = bf16[8192,512]{1,0:T(8,128)(2,1)} async-done(((bf16[1024,512]{1,0:T(8,128)(2,1)}), bf16[8192,512]{1,0:T(8,128)(2,1)}) %all-gather.8.cloned.1.call-update) | async-done | bytes 8388624 | tf_op jit(solution)/shard_map/all_gather | solution.py:25
  197.1 0.0 copy-start.1
  197.1 0.0 copy-start.2
  197.1 0.0 copy-start.3
  197.1 0.0 all-gather.10.cloned.1.call-update
  197.1 0.9 copy-done.1
  198.0 1.7 fusion.34
  199.6 0.0 copy-done.2
  199.6 0.6 multiply_reduce_fusion.1
  200.9 0.0 copy-done.3
  200.9 19.0 %all-gather.1 = s32[16,1,512]{2,1,0:T(1,128)S(1)} all-gather(s32[1,1,512]{2,1,0:T(1,128)S(1)} %bitcast.30), channel_id=1, replica_groups=mesh['chip'=8,'core'=2,'mp'=8] {'chip','core'}, dimensions={0}, use_global_device_ids=true | all-gather | bytes 34816 | tf_op jit(solution)/shard_map/all_gather | solution.py:46
  219.9 0.7 reduce_sum.36
  221.3 38.4 %all-reduce.7 = bf16[512,64]{0,1:T(8,128)(2,1)S(1)} all-reduce(f32[512,64]{0,1:T(8,128)S(1)} %fusion.34), channel_id=1, replica_groups=mesh['chip'=8,'core'=2,'mp'=8] {'mp'}, use_global_device_ids=true, to_apply=%region_0.0 | all-reduce | flops 32768 | bytes 196608 | tf_op jit(solution)/shard_map/psum | solution.py:62
  259.7 0.0 all-gather.10.cloned.1.call-done
  259.8 0.0 slice-start
  259.8 10.5 %fusion.23 = bf16[512,512]{0,1:T(8,128)(2,1)S(1)} fusion(bf16[512,8192]{1,0:T(8,128)(2,1)} %param.7, bf16[16384,512]{1,0:T(8,128)(2,1)} %all-gather.10.cloned.1.call-done), kind=kOutput, calls=%fused_computation.17 | convolution fusion | flops 4295229440 | bytes 17301504 | tf_op jit(solution)/shard_map/dot_general | solution.py:16
  270.2 0.0 slice-start.1
  270.3 10.5 %fusion.29 = bf16[512,512]{0,1:T(8,128)(2,1)S(1)} fusion(bf16[512,8192]{1,0:T(8,128)(2,1)} %param.7, bf16[16384,512]{1,0:T(8,128)(2,1)} %all-gather.10.cloned.1.call-done), kind=kOutput, calls=%fused_computation.19 | convolution fusion | flops 4295229440 | bytes 17301504 | tf_op jit(solution)/shard_map/dot_general | solution.py:16
  280.7 0.0 slice-done
  280.7 0.0 slice-done.1
  280.8 7.2 %fusion.20 = bf16[512,512]{0,1:T(8,128)(2,1)S(1)} fusion(bf16[512,8192]{1,0:T(8,128)(2,1)S(1)} %bitcast.29, bf16[16384,512]{1,0:T(8,128)(2,1)} %all-gather.10.cloned.1.call-done), kind=kOutput, calls=%fused_computation.16 | convolution fusion | flops 4295229440 | bytes 17301504 | tf_op jit(solution)/shard_map/dot_general | solution.py:16
  288.0 7.0 %fusion.26 = bf16[512,512]{0,1:T(8,128)(2,1)S(1)} fusion(bf16[512,8192]{1,0:T(8,128)(2,1)S(1)} %bitcast.29, bf16[16384,512]{1,0:T(8,128)(2,1)} %all-gather.10.cloned.1.call-done), kind=kOutput, calls=%fused_computation.18 | convolution fusion | flops 4295229440 | bytes 17301504 | tf_op jit(solution)/shard_map/dot_general | solution.py:16
  295.0 0.0 copy-done
  295.0 0.9 multiply_reduce_fusion
  295.9 0.6 multiply_reduce_fusion.2
  296.6 0.6 multiply_convert_fusion
  297.2 0.3 fusion.42
  297.5 27.8 %psum.46 = f32[]{:T(128)} all-reduce(f32[]{:T(128)} %get-tuple-element.8), channel_id=1, replica_groups=mesh['chip'=8,'core'=2,'mp'=8] {'chip','core'}, use_global_device_ids=true, to_apply=%region_8.0 | all-reduce | flops 1 | bytes 8 | tf_op jit(solution)/shard_map/psum | solution.py:87
  325.2 1.3 copy.19
  326.6 9.4 %all-to-all-start = ((bf16[8,64,1024]{2,1,0:T(8,128)(2,1)}), bf16[8,64,1024]{2,1,0:T(8,128)(2,1)S(1)}, u32[]{:S(2)}, u32[]{:S(2)}) async-start(bf16[8,64,1024]{2,1,0:T(8,128)(2,1)} %bitcast.2), calls=%async_computation | async-start | bytes 2097152 | tf_op jit(solution)/shard_map/all_to_all | solution.py:67
  336.0 0.0 all-reduce.6.cloned.1.call-start
  336.0 47.0 %all-reduce.8 = (bf16[512,64]{0,1:T(8,128)(2,1)S(1)}, f32[1]{0:T(128)}) all-reduce(f32[512,64]{0,1:T(8,128)S(1)} %fusion.42, f32[1]{0:T(128)} %bitcast.7), channel_id=1, replica_groups=mesh['chip'=8,'core'=2,'mp'=8] {'mp'}, use_global_device_ids=true, to_apply=%region_3.0 | all-reduce | flops 32769 | bytes 196616 | tf_op jit(solution)/shard_map/psum | solution.py:85
  383.0 2.2 fusion.32
  385.2 1.1 fusion.43
  386.3 0.0 all-reduce.6.cloned.1.call-update
  386.4 0.0 all-to-all-done
  386.4 1.1 copy.22
  387.4 116.0 %all-reduce.6.cloned.1.call-done = (f32[1024,64]{0,1:T(8,128)}, f32[64,1024]{1,0:T(8,128)}) async-done(((f32[1024,64]{0,1:T(8,128)}, f32[64,1024]{1,0:T(8,128)}), (f32[1024,64]{0,1:T(8,128)}, f32[64,1024]{1,0:T(8,128)})) %all-reduce.6.cloned.1.call-update) | async-done | bytes 524304 | tf_op jit(solution)/shard_map/psum | solution.py:87
  503.4 1.7 copy.30
  505.1 1.7 copy.31
  (4 shorter events, 0.0 us)
Async XLA Ops:
  7.2 287.9 %copy-start = (bf16[64,1024]{1,0:T(8,128)(2,1)S(1)}, bf16[64,1024]{1,0:T(8,128)(2,1)}, u32[]{:S(2)}) copy-start(bf16[64,1024]{1,0:T(8,128)(2,1)} %param.11) | copy-start | bytes 393220
  7.2 18.2 %all-gather.6.cloned.1.call-start = ((), (), s32[]{:S(2)}) async-start(), calls=%async_computation.1 | async-start | bytes 3145728 | tf_op jit(solution)/shard_map/all_gather | solution.py:23
  7.9 189.1 %all-gather.8.cloned.1.call-start = ((), (), s32[]{:S(2)}) async-start(), calls=%async_computation.2 | async-start | bytes 9437184 | tf_op jit(solution)/shard_map/all_gather | solution.py:25
  27.6 232.1 %all-gather.10.cloned.1.call-start = ((), (), s32[]{:S(2)}) async-start(), calls=%async_computation.3 | async-start | bytes 25165824 | tf_op jit(solution)/shard_map/all_gather | solution.py:26
  197.1 0.9 copy-start.1
  197.1 2.6 copy-start.2
  197.1 3.9 copy-start.3
  259.8 21.0 %slice-start = ((s8[8388608]{0:T(1024)(128)(4,1)}), s8[4194304]{0:T(1024)(128)(4,1)S(1)}, s32[]{:S(2)}) async-start(s8[8388608]{0:T(1024)(128)(4,1)} %bitcast.28), calls=%async_computation.5 | async-start | bytes 8388608
  270.2 10.5 %slice-start.1 = ((s8[8388608]{0:T(1024)(128)(4,1)}), s8[4194304]{0:T(1024)(128)(4,1)S(1)}, s32[]{:S(2)}) async-start(s8[8388608]{0:T(1024)(128)(4,1)} %bitcast.28), calls=%async_computation.6 | async-start | bytes 8388608
  326.6 59.8 %all-to-all-start = ((bf16[8,64,1024]{2,1,0:T(8,128)(2,1)}), bf16[8,64,1024]{2,1,0:T(8,128)(2,1)S(1)}, u32[]{:S(2)}, u32[]{:S(2)}) async-start(bf16[8,64,1024]{2,1,0:T(8,128)(2,1)} %bitcast.2), calls=%async_computation | async-start | bytes 2097152 | tf_op jit(solution)/shard_map/all_to_all | solution.py:67
  336.0 167.4 %all-reduce.6.cloned.1.call-start = ((), (), s32[]{:S(2)}) async-start(), calls=%async_computation.4 | async-start | bytes 1048576 | tf_op jit(solution)/shard_map/psum | solution.py:87
Sparse Core Ops, SparseCore 0:
  9.6 15.6 all-gather.5
  27.8 169.2 all-gather.7
  198.7 34.1 all-gather.9
  386.5 116.8 all-reduce.5

commit v2 on v0

v2 whole, which is shorter than its diff:
```python
import jax
import jax.numpy as jnp
from jax import lax
from jax.sharding import PartitionSpec as P

adapter_gain = 0.5
steer = 90.0
retain_weight = 1.2
loss_multiplier = 65536.0

CHUNKS = 2


def row_adder(source, piece):
    return jnp.dot(source, piece, preferred_element_type=jnp.float32)


def per_device(
    frozen_input_states,
    updated_input_states,
    weight,
    adapter_down_weight,
    adapter_up_weight,
    flags,
    control,
):
    group = frozen_input_states.shape[0]
    hidden_width = frozen_input_states.shape[1]
    parts = lax.axis_size("mp")
    rows_mine = hidden_width // parts
    width = rows_mine // CHUNKS
    m = lax.axis_index("mp")

    gathered = [
        lax.all_gather(weight[:, c * width:(c + 1) * width], "dp", axis=0, tiled=True)
        for c in range(CHUNKS)
    ]

    my_rows = lax.dynamic_slice_in_dim(updated_input_states, m * rows_mine, rows_mine, 1)
    low_part = jnp.dot(my_rows, adapter_down_weight, preferred_element_type=jnp.float32)
    rank_projection = lax.psum(low_part, "mp").astype(jnp.bfloat16)

    all_flags = lax.all_gather(flags, "dp", axis=0, tiled=True)
    forget_total = jnp.sum(all_flags).astype(jnp.float32)
    all_tokens = jnp.asarray(all_flags.shape[0], jnp.float32)
    n_forget = jnp.maximum(forget_total, 1.0)
    n_retain = jnp.maximum(all_tokens - forget_total, 1.0)
    is_forget = flags.astype(jnp.float32)[:, None]
    token_weight = is_forget / n_forget + retain_weight * (1.0 - is_forget) / n_retain

    unit = control * lax.rsqrt(jnp.sum(control * control) + 1e-06)
    unit_mine = lax.dynamic_slice_in_dim(unit, m * rows_mine, rows_mine, 0)

    outs, up_grads = [], []
    middle_part = None
    sq_rows = None
    for c in range(CHUNKS):
        cols = slice(c * width, (c + 1) * width)
        up_c = adapter_up_weight[:, cols]
        ref_c = row_adder(frozen_input_states, gathered[c]).astype(jnp.bfloat16)
        base_c = row_adder(updated_input_states, gathered[c]).astype(jnp.bfloat16)
        upd_c = base_c.astype(jnp.float32) + adapter_gain * jnp.dot(
            rank_projection, up_c, preferred_element_type=jnp.float32
        )
        outs.append(upd_c.astype(jnp.bfloat16))
        target = is_forget * steer * unit_mine[None, cols] + (1.0 - is_forget) * ref_c.astype(jnp.float32)
        diff = upd_c - target
        sq = jnp.sum(diff * diff, axis=1, keepdims=True)
        sq_rows = sq if sq_rows is None else sq_rows + sq
        gout = (
            loss_multiplier * 2.0 * adapter_gain / hidden_width * token_weight * diff
        ).astype(jnp.bfloat16)
        up_grads.append(jnp.dot(rank_projection.T, gout, preferred_element_type=jnp.float32))
        mp_c = jnp.dot(gout, up_c.T, preferred_element_type=jnp.float32)
        middle_part = mp_c if middle_part is None else middle_part + mp_c

    h_upd = lax.all_to_all(
        jnp.concatenate(outs, axis=1), "mp", split_axis=0, concat_axis=1, tiled=True
    )
    local_loss = jnp.sum(token_weight * (sq_rows / hidden_width))

    rank = middle_part.shape[1]
    packed = jnp.concatenate(
        [middle_part.reshape(-1), jnp.broadcast_to(local_loss, (128,))]
    )
    packed = lax.psum(packed, "mp")
    middle_gradient = packed[: group * rank].reshape(group, rank).astype(jnp.bfloat16)
    loss_mp = packed[group * rank]

    down_grad = jnp.dot(my_rows.T, middle_gradient, preferred_element_type=jnp.float32)
    up_grad = jnp.concatenate(up_grads, axis=1)
    n_a = down_grad.size
    n_b = up_grad.size
    packed2 = jnp.concatenate(
        [down_grad.reshape(-1), up_grad.reshape(-1), jnp.broadcast_to(loss_mp, (128,))]
    )
    packed2 = lax.psum(packed2, "dp")
    down_part = packed2[:n_a].reshape(down_grad.shape)
    up_part = packed2[n_a:n_a + n_b].reshape(up_grad.shape)
    total_loss = packed2[n_a + n_b]
    return (h_upd, down_part, up_part, total_loss.reshape(1))


def solution(mesh):
    in_specs = (
        P("dp", None),
        P("dp", None),
        P("dp", "mp"),
        P("mp", None),
        P(None, "mp"),
        P("dp"),
        P(),
    )
    out_specs = (P(("dp", "mp"), None), P("mp", None), P(None, "mp"), P())
    return jax.shard_map(
        per_device, mesh=mesh, in_specs=in_specs, out_specs=out_specs, check_vma=False
    )
```

time: 388 us -> 374 us (0.964)
  blocking collectives: 115 us -> 62.7 us
  waiting for transfers between devices: 195 us -> 222 us
  matrix products: 38.3 us -> 47.9 us
    psum x1 -> x2, waiting for transfers between devices: 89.8 us -> 188 us  [the longest x1 107 us: per_device(): packed2 = lax.psum(packed2, 'dp')]
    psum x2 -> x1, blocking collectives: 115 us -> 41.4 us  [per_device(): rank_projection = lax.psum(low_part, 'mp').astype(jnp.bfloat16)]
    all_gather x3 -> x2, waiting for transfers between devices: 103 us -> 33.9 us  [per_device(): lax.all_gather(weight[:, c * width:(c + 1) * width], 'dp', axis=0, tiled=...]
    all_gather x0 -> x1, blocking collectives: none -> 21.3 us  [per_device(): all_flags = lax.all_gather(flags, 'dp', axis=0, tiled=True)]
    dot_general x2 -> x4, matrix products: 26.1 us -> 41 us  [row_adder(): return jnp.dot(source, piece, preferred_element_type=jnp.float32)]
    slice x0 -> x6, local copies, waits for them, and re-layouts: none -> 6.62 us  [the longest x1 2.27 us: per_device(): weight[:, c * width:(c + 1) * width]]
    dot_general x4 -> x8, matrix products: 12.2 us -> 6.85 us  [the longest x1 1.69 us: per_device(): jnp.dot(my_rows.T, middle_gradient, preferred_element_type=jnp.float32)]
    unnamed x10 -> x8, local copies, waits for them, and re-layouts: 5.05 us -> 0.96 us
  transfers between devices with their start and end apart: 5 -> 5, of which waited for: 3 -> 3; matrix products, arithmetic and copies ran while one was open for 10% -> 6% of each run, Pallas kernels for 0% -> 0%
where the time goes in v2:
time: 374 us
  waiting for transfers between devices  222 us (59%)
  blocking collectives  62.7 us (17%)
  matrix products  47.9 us (13%)
  between operations  15.3 us (4%)
  local copies, waits for them, and re-layouts  13.3 us (4%)
  starting transfers between devices  7.37 us (2%)
  other arithmetic  5 us (1%)
    psum x1, waiting for transfers between devices, per_device(): packed2 = lax.psum(packed2, 'dp')  107 us
    psum x1, waiting for transfers between devices, per_device(): packed = lax.psum(packed, 'mp')  80.2 us
    psum x1, blocking collectives, per_device(): rank_projection = lax.psum(low_part, 'mp').astype(jnp.bfloat16)  41.4 us
    dot_general x4, matrix products, row_adder(): return jnp.dot(source, piece, preferred_element_type=jnp.float32)  41 us
    all_gather x2, waiting for transfers between devices, per_device(): lax.all_gather(weight[:, c * width:(c + 1) * width], 'dp', axis=0, tiled=...  33.9 us
    all_gather x1, blocking collectives, per_device(): all_flags = lax.all_gather(flags, 'dp', axis=0, tiled=True)  21.3 us
  transfers between devices with their start and end apart: 5, of which 3 were waited for; matrix products, arithmetic and copies ran while one was open for 6% of the time, Pallas kernels for 0%

profile of v2, /device:TPU:4, one launch (start us, length us, event | category | flops | bytes accessed | tf_op | source)
XLA Modules:
  0.0 373.7 jit_solution(9970122117687859674)
XLA Ops:
  7.2 0.0 all-gather.4.cloned.1.call-start
  7.2 2.3 fusion.25
  9.5 0.0 all-gather.4.cloned.1.call-update
  9.5 0.0 all-gather.6.cloned.1.call-start
  9.6 0.7 all-gather.6.cloned.1.call-update
  10.3 0.0 all-reduce.5.cloned.1.call-start
  10.3 1.7 fusion.14
  12.0 1.4 multiply_reduce_fusion.2
  14.1 21.3 %all-gather = s32[16,1,512]{2,1,0:T(1,128)S(1)} all-gather(s32[1,1,512]{2,1,0:T(1,128)} %bitcast.26), channel_id=1, replica_groups=mesh['dp'=16,'mp'=8] {'dp'}, dimensions={0}, use_global_device_ids=true | all-gather | bytes 34816 | tf_op jit(solution)/shard_map/all_gather | solution.py:43
  35.4 0.7 reduce_sum.45
  36.7 0.7 dynamic-slice_multiply_fusion
  37.4 41.4 %all-reduce.8 = bf16[512,64]{0,1:T(8,128)(2,1)S(1)} all-reduce(f32[512,64]{0,1:T(8,128)S(1)} %fusion.14), channel_id=1, replica_groups=mesh['dp'=16,'mp'=8] {'mp'}, use_global_device_ids=true, to_apply=%region_0.0 | all-reduce | flops 32768 | bytes 196608 | tf_op jit(solution)/shard_map/psum | solution.py:41
  78.8 0.7 convert_multiply_fusion
  79.5 9.8 %fusion.11 = f32[512,512]{0,1:T(8,128)S(1)} fusion(bf16[512,8192]{1,0:T(8,128)(2,1)} %param.8, bf16[8192,512]{1,0:T(8,128)(2,1)} %all-gather.4.cloned.1.call-done), kind=kOutput, calls=%fused_computation.17 | convolution fusion | flops 4295491584 | bytes 17825792 | tf_op jit(solution)/shard_map/dot_general | solution.py:15
  89.4 0.3 fusion.29
  89.7 33.9 %all-gather.6.cloned.1.call-done = bf16[8192,512]{1,0:T(8,128)(2,1)} async-done(((bf16[512,512]{1,0:T(8,128)(2,1)}), bf16[8192,512]{1,0:T(8,128)(2,1)}) %all-gather.6.cloned.1.call-update) | async-done | bytes 8388624 | tf_op jit(solution)/shard_map/all_gather | solution.py:35
  123.6 9.4 %fusion.10 = f32[512,512]{0,1:T(8,128)S(1)} fusion(bf16[512,8192]{1,0:T(8,128)(2,1)} %param.8, bf16[8192,512]{1,0:T(8,128)(2,1)} %all-gather.6.cloned.1.call-done), kind=kOutput, calls=%fused_computation.15 | convolution fusion | flops 4295491584 | bytes 17825792 | tf_op jit(solution)/shard_map/dot_general | solution.py:15
  133.1 1.3 fusion.28
  134.4 11.1 %multiply_reduce_fusion.1 = (f32[512]{0:T(512)S(1)}, f32[512,512]{0,1:T(8,128)S(1)}) fusion(f32[512,512]{0,1:T(8,128)S(1)} %get-tuple-element.29, bf16[512,8192]{1,0:T(8,128)(2,1)} %param.7, bf16[8192,512]{1,0:T(8,128)(2,1)} %all-gather.4.cloned.1.call-done, f32[512]{0:T(512)S(1)} %get-tuple-element.25, f32[512]{0:T(512)S(1)} %get-tuple-element.23, ...), kind=kOutput, calls=%fused_computation.21 | convolution fusion | flops 4297063936 | bytes 18882560 | tf_op jit(solution)/shard_map/dot_general | solution.py:15
  145.5 10.6 %multiply_reduce_fusion = (f32[512]{0:T(512)S(1)}, f32[512,512]{0,1:T(8,128)S(1)}) fusion(f32[512,512]{0,1:T(8,128)} %get-tuple-element.27, bf16[512,8192]{1,0:T(8,128)(2,1)} %param.7, bf16[8192,512]{1,0:T(8,128)(2,1)} %all-gather.6.cloned.1.call-done, f32[512]{0:T(512)S(1)} %get-tuple-element.25, f32[512]{0:T(512)S(1)} %get-tuple-element.22, ...), kind=kOutput, calls=%fused_computation.20 | convolution fusion | flops 4297063936 | bytes 18882560 | tf_op jit(solution)/shard_map/dot_general | solution.py:15
  156.2 0.6 multiply_reduce_fusion.3
  156.8 0.2 fusion.17
  157.0 0.3 fusion.16
  157.3 1.1 convolution_add_fusion
  158.3 0.1 copy.23
  158.5 0.1 reshape.60
  158.6 1.3 concatenate.13
  159.9 0.0 all-reduce.5.cloned.1.call-update
  159.9 0.0 all-reduce.7.cloned.1.call-start
  160.0 0.3 fusion.18
  160.3 80.2 %all-reduce.5.cloned.1.call-done = f32[32896]{0:T(1024)} async-done(((f32[32896]{0:T(1024)}), f32[32896]{0:T(1024)}) %all-reduce.5.cloned.1.call-update) | async-done | bytes 131600 | tf_op jit(solution)/shard_map/psum | solution.py:86
  240.5 0.9 slice.75
  241.4 0.1 convert_element_type.64
  241.6 1.7 fusion.12
  243.3 0.1 reshape.61
  243.4 1.2 slice.62
  244.6 0.6 broadcast_in_dim.2
  245.2 0.8 pad_maximum_fusion.1
  246.1 0.1 pad_maximum_fusion
  246.2 1.3 copy.21
  247.5 7.2 %all-to-all-start = ((bf16[8,64,1024]{2,1,0:T(8,128)(2,1)}), bf16[8,64,1024]{2,1,0:T(8,128)(2,1)S(1)}, u32[]{:S(2)}, u32[]{:S(2)}) async-start(bf16[8,64,1024]{2,1,0:T(8,128)(2,1)} %bitcast), calls=%async_computation | async-start | bytes 2097152 | tf_op jit(solution)/shard_map/all_to_all | solution.py:77
  254.7 107.3 %all-reduce.7.cloned.1.call-done = f32[131200]{0:T(1024)} async-done(((f32[131200]{0:T(1024)}), f32[131200]{0:T(1024)}) %all-reduce.7.cloned.1.call-update) | async-done | bytes 524816 | tf_op jit(solution)/shard_map/psum | solution.py:97
  362.0 1.1 fusion.26
  363.1 0.1 reshape.63
  363.3 0.9 copy.25
  364.1 0.7 reshape.64
  364.9 1.2 slice.65
  366.1 1.1 copy.27
  (13 shorter events, 0.1 us)
Async XLA Ops:
  7.2 3.2 copy-start
  7.2 72.4 %all-gather.4.cloned.1.call-start = ((), (), s32[]{:S(2)}) async-start(), calls=%async_computation.1 | async-start | bytes 8912896 | tf_op jit(solution)/shard_map/all_gather | solution.py:35
  9.5 114.1 %all-gather.6.cloned.1.call-start = ((), (), s32[]{:S(2)}) async-start(), calls=%async_computation.2 | async-start | bytes 8912896 | tf_op jit(solution)/shard_map/all_gather | solution.py:35
  10.3 230.3 %all-reduce.5.cloned.1.call-start = ((), (), s32[]{:S(2)}) async-start(), calls=%async_computation.3 | async-start | bytes 270336 | tf_op jit(solution)/shard_map/psum | solution.py:86
  79.5 9.9 %copy-start.1 = (bf16[64,1024]{1,0:T(8,128)(2,1)S(1)}, bf16[64,1024]{1,0:T(8,128)(2,1)}, u32[]{:S(2)}) copy-start(bf16[64,1024]{1,0:T(8,128)(2,1)} %param.11) | copy-start | bytes 393220
  145.5 10.6 %copy-start.2 = (s32[512]{0:T(512)S(1)}, s32[512]{0:T(512)}, u32[]{:S(2)}) copy-start(s32[512]{0:T(512)} %param.12) | copy-start | bytes 6148
  159.9 202.1 %all-reduce.7.cloned.1.call-start = ((), (), s32[]{:S(2)}) async-start(), calls=%async_computation.4 | async-start | bytes 1056768 | tf_op jit(solution)/shard_map/psum | solution.py:97
  247.5 118.6 %all-to-all-start = ((bf16[8,64,1024]{2,1,0:T(8,128)(2,1)}), bf16[8,64,1024]{2,1,0:T(8,128)(2,1)S(1)}, u32[]{:S(2)}, u32[]{:S(2)}) async-start(bf16[8,64,1024]{2,1,0:T(8,128)(2,1)} %bitcast), calls=%async_computation | async-start | bytes 2097152 | tf_op jit(solution)/shard_map/all_to_all | solution.py:77
Sparse Core Ops, SparseCore 0:
  10.3 57.9 all-gather.3
  70.0 53.5 all-gather.5
  160.0 80.4 all-reduce.4
  246.2 115.7 all-reduce.6

commit v3 on v2

v3 whole, which is shorter than its diff:
```python
import jax
import jax.numpy as jnp
from jax import lax
from jax.sharding import PartitionSpec as P

adapter_gain = 0.5
steer = 90.0
retain_weight = 1.2
loss_multiplier = 65536.0


def row_adder(source, piece):
    return jnp.dot(source, piece, preferred_element_type=jnp.float32)


def butterfly_sum(x, axis):
    n = lax.axis_size(axis)
    step = 1
    while step < n:
        x = x + lax.ppermute(x, axis, [(i, i ^ step) for i in range(n)])
        step *= 2
    return x


def per_device(
    frozen_input_states,
    updated_input_states,
    weight,
    adapter_down_weight,
    adapter_up_weight,
    flags,
    control,
):
    group = frozen_input_states.shape[0]
    hidden_width = frozen_input_states.shape[1]
    parts = lax.axis_size("mp")
    rows_mine = hidden_width // parts
    m = lax.axis_index("mp")

    gathered = lax.all_gather(weight, "dp", axis=0, tiled=True)

    my_rows = lax.dynamic_slice_in_dim(updated_input_states, m * rows_mine, rows_mine, 1)
    low_part = jnp.dot(my_rows, adapter_down_weight, preferred_element_type=jnp.float32)
    rank_projection = lax.psum(low_part, "mp").astype(jnp.bfloat16)

    all_flags = lax.all_gather(flags, "dp", axis=0, tiled=True)
    forget_total = jnp.sum(all_flags).astype(jnp.float32)
    all_tokens = jnp.asarray(all_flags.shape[0], jnp.float32)
    n_forget = jnp.maximum(forget_total, 1.0)
    n_retain = jnp.maximum(all_tokens - forget_total, 1.0)
    is_forget = flags.astype(jnp.float32)[:, None]
    token_weight = is_forget / n_forget + retain_weight * (1.0 - is_forget) / n_retain

    unit = control * lax.rsqrt(jnp.sum(control * control) + 1e-06)
    unit_mine = lax.dynamic_slice_in_dim(unit, m * rows_mine, rows_mine, 0)

    ref_rows = row_adder(frozen_input_states, gathered).astype(jnp.bfloat16)
    base_rows = row_adder(updated_input_states, gathered).astype(jnp.bfloat16)
    updated_output = base_rows.astype(jnp.float32) + adapter_gain * jnp.dot(
        rank_projection, adapter_up_weight, preferred_element_type=jnp.float32
    )
    h_upd = lax.all_to_all(
        updated_output.astype(jnp.bfloat16), "mp", split_axis=0, concat_axis=1, tiled=True
    )
    target = is_forget * steer * unit_mine[None, :] + (1.0 - is_forget) * ref_rows.astype(jnp.float32)
    state_difference = updated_output - target
    local_loss = jnp.sum(
        token_weight * (jnp.sum(state_difference * state_difference, axis=1, keepdims=True) / hidden_width)
    )
    output_gradient = (
        loss_multiplier * 2.0 * adapter_gain / hidden_width * token_weight * state_difference
    ).astype(jnp.bfloat16)
    up_grad = jnp.dot(rank_projection.T, output_gradient, preferred_element_type=jnp.float32)
    middle_part = jnp.dot(output_gradient, adapter_up_weight.T, preferred_element_type=jnp.float32)

    rank = middle_part.shape[1]
    packed = jnp.concatenate([middle_part, jnp.broadcast_to(local_loss, (8, rank))], axis=0)
    packed = butterfly_sum(packed, "mp")
    middle_gradient = packed[:group].astype(jnp.bfloat16)
    loss_mp = packed[group, 0]

    down_grad = jnp.dot(my_rows.T, middle_gradient, preferred_element_type=jnp.float32)
    n_a = down_grad.size
    n_b = up_grad.size
    packed2 = jnp.concatenate(
        [down_grad.reshape(-1), up_grad.reshape(-1), jnp.broadcast_to(loss_mp, (1024,))]
    )
    packed2 = butterfly_sum(packed2, "dp")
    down_part = packed2[:n_a].reshape(down_grad.shape)
    up_part = packed2[n_a:n_a + n_b].reshape(up_grad.shape)
    total_loss = packed2[n_a + n_b]
    return (h_upd, down_part, up_part, total_loss.reshape(1))


def solution(mesh):
    in_specs = (
        P("dp", None),
        P("dp", None),
        P("dp", "mp"),
        P("mp", None),
        P(None, "mp"),
        P("dp"),
        P(),
    )
    out_specs = (P(("dp", "mp"), None), P("mp", None), P(None, "mp"), P())
    return jax.shard_map(
        per_device, mesh=mesh, in_specs=in_specs, out_specs=out_specs, check_vma=False
    )
```

time: 374 us -> 219 us (0.59)
  waiting for transfers between devices: 222 us -> 77 us
  matrix products: 47.9 us -> 35.9 us
  starting transfers between devices: 7.37 us -> 17.2 us
  local copies, waits for them, and re-layouts: 13.3 us -> 5.4 us
    psum x2 -> x0, waiting for transfers between devices: 188 us -> none  [the longest x1 107 us: per_device(): packed2 = lax.psum(packed2, 'dp')]
    ppermute x0 -> x7, waiting for transfers between devices: none -> 40 us  [butterfly_sum(): x = x + lax.ppermute(x, axis, [(i, i ^ step) for i in range(n)])]
    dot_general x4 -> x2, matrix products: 41 us -> 30.2 us  [row_adder(): return jnp.dot(source, piece, preferred_element_type=jnp.float32)]
    ppermute x0 -> x7, starting transfers between devices: none -> 9.88 us  [butterfly_sum(): x = x + lax.ppermute(x, axis, [(i, i ^ step) for i in range(n)])]
    all_to_all x1, waiting for transfers between devices: 0.01 us -> 5.04 us  [per_device(): lax.all_to_all(updated_output.astype(jnp.bfloat16), 'mp', split_axis=0, c...]
    all_gather x2 -> x1, waiting for transfers between devices: 33.9 us -> 31.2 us  [per_device(): gathered = lax.all_gather(weight, 'dp', axis=0, tiled=True)]
  transfers between devices with their start and end apart: 5 -> 9, of which waited for: 3 -> 9; matrix products, arithmetic and copies ran while one was open for 6% -> 2% of each run, Pallas kernels for 0% -> 0%
where the time goes in v3:
time: 219 us
  waiting for transfers between devices  77 us (35%)
  blocking collectives  64.6 us (29%)
  matrix products  35.9 us (16%)
  starting transfers between devices  17.2 us (8%)
  between operations  15.6 us (7%)
  local copies, waits for them, and re-layouts  5.4 us (2%)
  other arithmetic  2.95 us (1%)
    psum x1, blocking collectives, per_device(): rank_projection = lax.psum(low_part, 'mp').astype(jnp.bfloat16)  43.5 us
    ppermute x7, waiting for transfers between devices, butterfly_sum(): x = x + lax.ppermute(x, axis, [(i, i ^ step) for i in range(n)])  40 us
    all_gather x1, waiting for transfers between devices, per_device(): gathered = lax.all_gather(weight, 'dp', axis=0, tiled=True)  31.2 us
    dot_general x2, matrix products, row_adder(): return jnp.dot(source, piece, preferred_element_type=jnp.float32)  30.2 us
    all_gather x1, blocking collectives, per_device(): all_flags = lax.all_gather(flags, 'dp', axis=0, tiled=True)  21.1 us
    ppermute x7, starting transfers between devices, butterfly_sum(): x = x + lax.ppermute(x, axis, [(i, i ^ step) for i in range(n)])  9.88 us
    all_to_all x1, starting transfers between devices, per_device(): lax.all_to_all(updated_output.astype(jnp.bfloat16), 'mp', split_axis=0, c...  7.28 us
    all_to_all x1, waiting for transfers between devices, per_device(): lax.all_to_all(updated_output.astype(jnp.bfloat16), 'mp', split_axis=0, c...  5.04 us
  transfers between devices with their start and end apart: 9, of which 9 were waited for; matrix products, arithmetic and copies ran while one was open for 2% of the time, Pallas kernels for 0%

profile of v3, /device:TPU:4, one launch (start us, length us, event | category | flops | bytes accessed | tf_op | source)
XLA Modules:
  0.0 218.6 jit_solution(1611422867383796019)
XLA Ops:
  7.2 0.0 copy-start
  7.2 0.0 copy-start.1
  7.2 0.0 all-gather.3.cloned.1.call-start
  7.2 0.7 all-gather.3.cloned.1.call-update
  7.9 1.7 fusion.2
  9.6 0.6 multiply_reduce_fusion.1
  10.9 0.0 copy-done.2
  10.9 21.1 %all-gather = s32[16,1,512]{2,1,0:T(1,128)S(1)} all-gather(s32[1,1,512]{2,1,0:T(1,128)S(1)} %bitcast.22), channel_id=1, replica_groups=mesh['dp'=16,'mp'=8] {'dp'}, dimensions={0}, use_global_device_ids=true | all-gather | bytes 34816 | tf_op jit(solution)/shard_map/all_gather | solution.py:46
  32.0 0.7 reduce_sum.36
  33.4 43.5 %all-reduce.2 = bf16[512,64]{0,1:T(8,128)(2,1)S(1)} all-reduce(f32[512,64]{0,1:T(8,128)S(1)} %fusion.2), channel_id=1, replica_groups=mesh['dp'=16,'mp'=8] {'mp'}, use_global_device_ids=true, to_apply=%region_0.0 | all-reduce | flops 32768 | bytes 196608 | tf_op jit(solution)/shard_map/psum | solution.py:44
  76.9 31.2 %all-gather.3.cloned.1.call-done = bf16[8192,1024]{1,0:T(8,128)(2,1)} async-done(((bf16[512,1024]{1,0:T(8,128)(2,1)}), bf16[8192,1024]{1,0:T(8,128)(2,1)}) %all-gather.3.cloned.1.call-update) | async-done | bytes 16777232 | tf_op jit(solution)/shard_map/all_gather | solution.py:40
  108.1 14.8 %convolution_convert_fusion.1 = bf16[512,1024]{1,0:T(8,128)(2,1)S(1)} fusion(bf16[512,8192]{1,0:T(8,128)(2,1)} %param.8, bf16[8192,1024]{1,0:T(8,128)(2,1)} %all-gather.3.cloned.1.call-done), kind=kOutput, calls=%fused_computation.5 | convolution fusion | flops 8590458880 | bytes 26214400 | tf_op jit(solution)/shard_map/dot_general | solution.py:13
  122.9 1.4 fusion.11
  124.4 15.4 %multiply_reduce_fusion = (f32[512]{0:T(512)S(1)}, f32[512,1024]{1,0:T(8,128)S(1)}) fusion(f32[512,1024]{1,0:T(8,128)S(1)} %get-tuple-element.19, bf16[512,8192]{1,0:T(8,128)(2,1)} %param.7, bf16[8192,1024]{1,0:T(8,128)(2,1)} %all-gather.3.cloned.1.call-done, f32[512]{0:T(512)S(1)} %get-tuple-element.17, f32[1024]{0:T(1024)S(1)} %dynamic-slice_multiply_fusion, ...), kind=kOutput, calls=%fused_computation | convolution fusion | flops 8594128896 | bytes 29370368 | tf_op jit(solution)/shard_map/dot_general | solution.py:13
  139.8 0.6 multiply_reduce_fusion.2
  140.4 0.5 fusion.8
  140.9 0.7 concatenate.6
  141.6 0.9 collective-permute-start
  142.5 7.0 %collective-permute-done = f32[520,64]{0,1:T(8,128)S(1)} collective-permute-done((f32[520,64]{0,1:T(8,128)S(1)}, f32[520,64]{0,1:T(8,128)S(1)}, u32[]{:S(2)}, u32[]{:S(2)}) %collective-permute-start) | collective-permute-done | bytes 133152 | tf_op jit(solution)/shard_map/ppermute | solution.py:20
  149.5 0.7 pad_add_fusion
  150.2 1.6 collective-permute-start.1
  151.8 4.0 %collective-permute-done.1 = f32[520,64]{0,1:T(8,128)S(1)} collective-permute-done((f32[520,64]{0,1:T(8,128)S(1)}, f32[520,64]{0,1:T(8,128)S(1)}, u32[]{:S(2)}, u32[]{:S(2)}) %collective-permute-start.1) | collective-permute-done | bytes 133152 | tf_op jit(solution)/shard_map/ppermute | solution.py:20
  155.8 3.1 %collective-permute-start.2 = (f32[520,64]{0,1:T(8,128)S(1)}, f32[520,64]{0,1:T(8,128)S(1)}, u32[]{:S(2)}, u32[]{:S(2)}) collective-permute-start(f32[520,64]{0,1:T(8,128)S(1)} %add.48), channel_id=1, source_target_pairs={{0,4},{1,5},{2,6},{3,7},{4,0},{5,1},{6,2},{7,3},{8,12},{9,13},{10,... | collective-permute-start | bytes 399368 | tf_op jit(solution)/shard_map/ppermute | solution.py:20
  158.9 0.4 convolution_bitcast_fusion
  159.3 3.4 %collective-permute-done.2 = f32[520,64]{0,1:T(8,128)S(1)} collective-permute-done((f32[520,64]{0,1:T(8,128)S(1)}, f32[520,64]{0,1:T(8,128)S(1)}, u32[]{:S(2)}, u32[]{:S(2)}) %collective-permute-start.2) | collective-permute-done | bytes 133152 | tf_op jit(solution)/shard_map/ppermute | solution.py:20
  162.7 0.5 slice.44
  163.2 1.7 fusion
  164.9 0.1 reshape.49
  165.1 0.6 broadcast_in_dim.2
  165.8 0.1 collective-permute-start.3
  165.9 1.9 collective-permute-done.3
  167.8 0.1 fusion.9
  167.8 1.2 collective-permute-start.4
  169.0 13.0 %collective-permute-done.4 = f32[132096]{0:T(1024)S(1)} collective-permute-done((f32[132096]{0:T(1024)S(1)}, f32[132096]{0:T(1024)S(1)}, u32[]{:S(2)}, u32[]{:S(2)}) %collective-permute-start.4) | collective-permute-done | bytes 528416 | tf_op jit(solution)/shard_map/ppermute | solution.py:20
  182.0 0.1 add.51
  182.0 0.1 collective-permute-start.5
  182.1 7.3 %all-to-all-start = ((bf16[8,64,1024]{2,1,0:T(8,128)(2,1)}), bf16[8,64,1024]{2,1,0:T(8,128)(2,1)S(1)}, u32[]{:S(2)}, u32[]{:S(2)}) async-start(bf16[8,64,1024]{2,1,0:T(8,128)(2,1)} %bitcast), calls=%async_computation | async-start | bytes 2097152 | tf_op jit(solution)/shard_map/all_to_all | solution.py:62
  189.4 5.9 %collective-permute-done.5 = f32[132096]{0:T(1024)S(1)} collective-permute-done((f32[132096]{0:T(1024)S(1)}, f32[132096]{0:T(1024)S(1)}, u32[]{:S(2)}, u32[]{:S(2)}) %collective-permute-start.5) | collective-permute-done | bytes 528416 | tf_op jit(solution)/shard_map/ppermute | solution.py:20
  195.3 0.1 add.52
  195.4 3.0 %collective-permute-start.6 = (f32[132096]{0:T(1024)S(1)}, f32[132096]{0:T(1024)S(1)}, u32[]{:S(2)}, u32[]{:S(2)}) collective-permute-start(f32[132096]{0:T(1024)S(1)} %add.52), channel_id=1, source_target_pairs={{0,64},{8,72},{16,80},{24,88},{32,96},{40,104},{48,112},{56,120},{... | collective-permute-start | bytes 1585160 | tf_op jit(solution)/shard_map/ppermute | solution.py:20
  198.3 5.0 %all-to-all-done = bf16[8,64,1024]{2,1,0:T(8,128)(2,1)S(1)} async-done(((bf16[8,64,1024]{2,1,0:T(8,128)(2,1)}), bf16[8,64,1024]{2,1,0:T(8,128)(2,1)S(1)}, u32[]{:S(2)}, u32[]{:S(2)}) %all-to-all-start) | async-done | bytes 1048608 | tf_op jit(solution)/shard_map/all_to_all | solution.py:62
  203.4 1.0 copy.19
  204.4 4.9 %collective-permute-done.6 = f32[132096]{0:T(1024)S(1)} collective-permute-done((f32[132096]{0:T(1024)S(1)}, f32[132096]{0:T(1024)S(1)}, u32[]{:S(2)}, u32[]{:S(2)}) %collective-permute-start.6) | collective-permute-done | bytes 528416 | tf_op jit(solution)/shard_map/ppermute | solution.py:20
  209.3 0.1 add.53
  209.4 0.5 slice.47
  209.9 0.1 slice.39
  210.1 0.9 copy.17
  211.0 0.7 slice.41
  (11 shorter events, 0.2 us)
Async XLA Ops:
  7.2 115.8 %copy-start = (bf16[64,1024]{1,0:T(8,128)(2,1)S(1)}, bf16[64,1024]{1,0:T(8,128)(2,1)}, u32[]{:S(2)}) copy-start(bf16[64,1024]{1,0:T(8,128)(2,1)} %param.11) | copy-start | bytes 393220
  7.2 2.4 %copy-start.1 = (f32[8192]{0:T(1024)S(1)}, f32[8192]{0:T(1024)}, u32[]{:S(2)}) copy-start(f32[8192]{0:T(1024)} %param.13) | copy-start | bytes 98308
  7.2 3.7 %copy-start.2 = (s32[512]{0:T(512)S(1)}, s32[512]{0:T(512)}, u32[]{:S(2)}) copy-start(s32[512]{0:T(512)} %param.12) | copy-start | bytes 6148
  7.2 100.9 %all-gather.3.cloned.1.call-start = ((), (), s32[]{:S(2)}) async-start(), calls=%async_computation.1 | async-start | bytes 17825792 | tf_op jit(solution)/shard_map/all_gather | solution.py:40
  141.6 7.9 %collective-permute-start = (f32[520,64]{0,1:T(8,128)S(1)}, f32[520,64]{0,1:T(8,128)S(1)}, u32[]{:S(2)}, u32[]{:S(2)}) collective-permute-start(f32[520,64]{0,1:T(8,128)S(1)} %concatenate.6), channel_id=1, source_target_pairs={{0,1},{1,0},{2,3},{3,2},{4,5},{5,4},{6,7},{7,6},{8,9},{9,8},{10,11... | collective-permute-start | bytes 399368 | tf_op jit(solution)/shard_map/ppermute | solution.py:20
  150.2 5.6 %collective-permute-start.1 = (f32[520,64]{0,1:T(8,128)S(1)}, f32[520,64]{0,1:T(8,128)S(1)}, u32[]{:S(2)}, u32[]{:S(2)}) collective-permute-start(f32[520,64]{0,1:T(8,128)S(1)} %pad_add_fusion), channel_id=1, source_target_pairs={{0,2},{1,3},{2,0},{3,1},{4,6},{5,7},{6,4},{7,5},{8,10},{9,11},{10,... | collective-permute-start | bytes 399368 | tf_op jit(solution)/shard_map/ppermute | solution.py:20
  155.8 6.9 %collective-permute-start.2 = (f32[520,64]{0,1:T(8,128)S(1)}, f32[520,64]{0,1:T(8,128)S(1)}, u32[]{:S(2)}, u32[]{:S(2)}) collective-permute-start(f32[520,64]{0,1:T(8,128)S(1)} %add.48), channel_id=1, source_target_pairs={{0,4},{1,5},{2,6},{3,7},{4,0},{5,1},{6,2},{7,3},{8,12},{9,13},{10,... | collective-permute-start | bytes 399368 | tf_op jit(solution)/shard_map/ppermute | solution.py:20
  165.8 2.0 collective-permute-start.3
  167.8 14.1 %collective-permute-start.4 = (f32[132096]{0:T(1024)S(1)}, f32[132096]{0:T(1024)S(1)}, u32[]{:S(2)}, u32[]{:S(2)}) collective-permute-start(f32[132096]{0:T(1024)S(1)} %fusion.9), channel_id=1, source_target_pairs={{0,16},{8,24},{16,0},{24,8},{32,48},{40,56},{48,32},{56,40},{64,80... | collective-permute-start | bytes 1585160 | tf_op jit(solution)/shard_map/ppermute | solution.py:20
  182.0 13.3 %collective-permute-start.5 = (f32[132096]{0:T(1024)S(1)}, f32[132096]{0:T(1024)S(1)}, u32[]{:S(2)}, u32[]{:S(2)}) collective-permute-start(f32[132096]{0:T(1024)S(1)} %add.51), channel_id=1, source_target_pairs={{0,32},{8,40},{16,48},{24,56},{32,0},{40,8},{48,16},{56,24},{64,96... | collective-permute-start | bytes 1585160 | tf_op jit(solution)/shard_map/ppermute | solution.py:20
  182.1 21.3 %all-to-all-start = ((bf16[8,64,1024]{2,1,0:T(8,128)(2,1)}), bf16[8,64,1024]{2,1,0:T(8,128)(2,1)S(1)}, u32[]{:S(2)}, u32[]{:S(2)}) async-start(bf16[8,64,1024]{2,1,0:T(8,128)(2,1)} %bitcast), calls=%async_computation | async-start | bytes 2097152 | tf_op jit(solution)/shard_map/all_to_all | solution.py:62
  195.4 13.9 %collective-permute-start.6 = (f32[132096]{0:T(1024)S(1)}, f32[132096]{0:T(1024)S(1)}, u32[]{:S(2)}, u32[]{:S(2)}) collective-permute-start(f32[132096]{0:T(1024)S(1)} %add.52), channel_id=1, source_target_pairs={{0,64},{8,72},{16,80},{24,88},{32,96},{40,104},{48,112},{56,120},{... | collective-permute-start | bytes 1585160 | tf_op jit(solution)/shard_map/ppermute | solution.py:20
Sparse Core Ops, SparseCore 0:
  9.7 98.3 all-gather.2

commit v4 on v3

--- a/solution.py
+++ b/solution.py
@@ -79,16 +79,12 @@
     middle_gradient = packed[:group].astype(jnp.bfloat16)
     loss_mp = packed[group, 0]
 
+    up_part = butterfly_sum(up_grad, "dp")
     down_grad = jnp.dot(my_rows.T, middle_gradient, preferred_element_type=jnp.float32)
-    n_a = down_grad.size
-    n_b = up_grad.size
-    packed2 = jnp.concatenate(
-        [down_grad.reshape(-1), up_grad.reshape(-1), jnp.broadcast_to(loss_mp, (1024,))]
-    )
+    packed2 = jnp.concatenate([down_grad, jnp.broadcast_to(loss_mp, (8, rank))], axis=0)
     packed2 = butterfly_sum(packed2, "dp")
-    down_part = packed2[:n_a].reshape(down_grad.shape)
-    up_part = packed2[n_a:n_a + n_b].reshape(up_grad.shape)
-    total_loss = packed2[n_a + n_b]
+    down_part = packed2[: down_grad.shape[0]]
+    total_loss = packed2[down_grad.shape[0], 0]
     return (h_upd, down_part, up_part, total_loss.reshape(1))
 
 

time: 219 us -> 216 us (0.986)
  matrix products: 35.9 us -> 32.3 us
  other arithmetic: 2.95 us -> 5.16 us
    ppermute x7 -> x11, waiting for transfers between devices: 40 us -> 46.6 us  [butterfly_sum(): x = x + lax.ppermute(x, axis, [(i, i ^ step) for i in range(n)])]
    all_to_all x1, waiting for transfers between devices: 5.04 us -> 0.01 us  [per_device(): lax.all_to_all(updated_output.astype(jnp.bfloat16), 'mp', split_axis=0, c...]
    dot_general x2, matrix products: 30.2 us -> 26.8 us  [row_adder(): return jnp.dot(source, piece, preferred_element_type=jnp.float32)]
    add x7 -> x11, other arithmetic: 0.97 us -> 3.22 us  [butterfly_sum(): x = x + lax.ppermute(x, axis, [(i, i ^ step) for i in range(n)])]
    ppermute x7 -> x11, starting transfers between devices: 9.88 us -> 9.71 us  [butterfly_sum(): x = x + lax.ppermute(x, axis, [(i, i ^ step) for i in range(n)])]
  transfers between devices with their start and end apart: 9 -> 13, of which waited for: 9 -> 9; matrix products, arithmetic and copies ran while one was open for 2% -> 4% of each run, Pallas kernels for 0% -> 0%
where the time goes in v4:
time: 216 us; the launch traced here: 215 us
  waiting for transfers between devices  78.5 us (36%)
  blocking collectives  64.6 us (30%)
  matrix products  32.3 us (15%)
  between operations  15.6 us (7%)
  starting transfers between devices  15.1 us (7%)
  other arithmetic  5.16 us (2%)
  local copies, waits for them, and re-layouts  4.16 us (2%)
    ppermute x11, waiting for transfers between devices, butterfly_sum(): x = x + lax.ppermute(x, axis, [(i, i ^ step) for i in range(n)])  46.6 us
    psum x1, blocking collectives, per_device(): rank_projection = lax.psum(low_part, 'mp').astype(jnp.bfloat16)  43.5 us
    all_gather x1, waiting for transfers between devices, per_device(): gathered = lax.all_gather(weight, 'dp', axis=0, tiled=True)  31.2 us
    dot_general x2, matrix products, row_adder(): return jnp.dot(source, piece, preferred_element_type=jnp.float32)  26.8 us
    all_gather x1, blocking collectives, per_device(): all_flags = lax.all_gather(flags, 'dp', axis=0, tiled=True)  21.1 us
    ppermute x11, starting transfers between devices, butterfly_sum(): x = x + lax.ppermute(x, axis, [(i, i ^ step) for i in range(n)])  9.71 us
    all_to_all x1, starting transfers between devices, per_device(): lax.all_to_all(updated_output.astype(jnp.bfloat16), 'mp', split_axis=0, c...  5.38 us
  transfers between devices with their start and end apart: 13, of which 9 were waited for; matrix products, arithmetic and copies ran while one was open for 4% of the time, Pallas kernels for 0%

profile of v4, /device:TPU:4, one launch (start us, length us, event | category | flops | bytes accessed | tf_op | source)
XLA Modules:
  0.0 215.4 jit_solution(1012862828283223621)
XLA Ops:
  7.2 0.0 copy-start
  7.2 0.0 all-gather.3.cloned.1.call-start
  7.2 0.7 all-gather.3.cloned.1.call-update
  7.9 1.7 fusion.2
  9.6 0.6 multiply_reduce_fusion.1
  10.9 21.1 %all-gather = s32[16,1,512]{2,1,0:T(1,128)S(1)} all-gather(s32[1,1,512]{2,1,0:T(1,128)S(1)} %bitcast.19), channel_id=1, replica_groups=mesh['dp'=16,'mp'=8] {'dp'}, dimensions={0}, use_global_device_ids=true | all-gather | bytes 34816 | tf_op jit(solution)/shard_map/all_gather | solution.py:46
  32.0 0.7 reduce_sum.36
  33.4 43.5 %all-reduce.3 = bf16[512,64]{0,1:T(8,128)(2,1)S(1)} all-reduce(f32[512,64]{0,1:T(8,128)S(1)} %fusion.2), channel_id=1, replica_groups=mesh['dp'=16,'mp'=8] {'mp'}, use_global_device_ids=true, to_apply=%region_0.0 | all-reduce | flops 32768 | bytes 196608 | tf_op jit(solution)/shard_map/psum | solution.py:44
  76.9 31.2 %all-gather.3.cloned.1.call-done = bf16[8192,1024]{1,0:T(8,128)(2,1)} async-done(((bf16[512,1024]{1,0:T(8,128)(2,1)}), bf16[8192,1024]{1,0:T(8,128)(2,1)}) %all-gather.3.cloned.1.call-update) | async-done | bytes 16777232 | tf_op jit(solution)/shard_map/all_gather | solution.py:40
  108.1 14.9 %convolution_convert_fusion.1 = bf16[512,1024]{1,0:T(8,128)(2,1)S(1)} fusion(bf16[512,8192]{1,0:T(8,128)(2,1)} %param.8, bf16[8192,1024]{1,0:T(8,128)(2,1)} %all-gather.3.cloned.1.call-done), kind=kOutput, calls=%fused_computation.5 | convolution fusion | flops 8590458880 | bytes 26214400 | tf_op jit(solution)/shard_map/dot_general | solution.py:13
  123.1 1.4 fusion.10
  124.5 11.9 %multiply_reduce_fusion = (f32[512]{0:T(512)S(1)}, f32[512,1024]{1,0:T(8,128)S(1)}) fusion(f32[512,1024]{1,0:T(8,128)S(1)} %get-tuple-element.9, bf16[512,8192]{1,0:T(8,128)(2,1)} %param.7, bf16[8192,1024]{1,0:T(8,128)(2,1)S(1)} %copy-done.3, f32[512]{0:T(512)S(1)} %get-tuple-element.7, f32[1024]{0:T(1024)S(1)} %dynamic-slice_multiply_fusion, ...), kind=kOutput, calls=%fused_computation | convolution fusion | flops 8594128896 | bytes 29370368 | tf_op jit(solution)/shard_map/dot_general | solution.py:13
  136.4 0.6 multiply_reduce_fusion.2
  137.0 0.5 fusion.9
  137.5 0.7 concatenate.6
  138.2 0.9 collective-permute-start
  139.1 7.0 %collective-permute-done = f32[520,64]{0,1:T(8,128)S(1)} collective-permute-done((f32[520,64]{0,1:T(8,128)S(1)}, f32[520,64]{0,1:T(8,128)S(1)}, u32[]{:S(2)}, u32[]{:S(2)}) %collective-permute-start) | collective-permute-done | bytes 133152 | tf_op jit(solution)/shard_map/ppermute | solution.py:20
  146.1 0.7 pad_add_fusion
  146.8 1.6 collective-permute-start.1
  148.4 4.0 %collective-permute-done.1 = f32[520,64]{0,1:T(8,128)S(1)} collective-permute-done((f32[520,64]{0,1:T(8,128)S(1)}, f32[520,64]{0,1:T(8,128)S(1)}, u32[]{:S(2)}, u32[]{:S(2)}) %collective-permute-start.1) | collective-permute-done | bytes 133152 | tf_op jit(solution)/shard_map/ppermute | solution.py:20
  152.4 3.1 %collective-permute-start.2 = (f32[520,64]{0,1:T(8,128)S(1)}, f32[520,64]{0,1:T(8,128)}, u32[]{:S(2)}, u32[]{:S(2)}) collective-permute-start(f32[520,64]{0,1:T(8,128)S(1)} %add.62), channel_id=1, source_target_pairs={{0,4},{1,5},{2,6},{3,7},{4,0},{5,1},{6,2},{7,3},{8,12},{9,13},{10,... | collective-permute-start | bytes 399368 | tf_op jit(solution)/shard_map/ppermute | solution.py:20
  155.5 5.4 %all-to-all-start = ((bf16[8,64,1024]{2,1,0:T(8,128)(2,1)}), bf16[8,64,1024]{2,1,0:T(8,128)(2,1)S(1)}, u32[]{:S(2)}, u32[]{:S(2)}) async-start(bf16[8,64,1024]{2,1,0:T(8,128)(2,1)} %bitcast.17), calls=%async_computation | async-start | bytes 2097152 | tf_op jit(solution)/shard_map/all_to_all | solution.py:62
  160.9 0.9 add.63
  161.8 1.5 fusion
  163.3 0.5 slice.18
  163.9 0.7 concatenate.7
  164.5 0.1 collective-permute-start.3
  164.6 0.4 fusion.4
  165.0 0.6 collective-permute-start.7
  165.6 0.6 collective-permute-done.3
  166.2 0.7 pad_add_fusion.1
  166.9 1.2 collective-permute-start.4
  168.0 0.0 collective-permute-done.7
  168.1 1.0 collective-permute-start.8
  169.1 11.4 %collective-permute-done.4 = f32[1032,64]{0,1:T(8,128)S(1)} collective-permute-done((f32[1032,64]{0,1:T(8,128)S(1)}, f32[1032,64]{0,1:T(8,128)S(1)}, u32[]{:S(2)}, u32[]{:S(2)}) %collective-permute-start.4) | collective-permute-done | bytes 264224 | tf_op jit(solution)/shard_map/ppermute | solution.py:20
  180.5 0.1 collective-permute-start.5
  180.6 3.2 %collective-permute-done.8 = f32[64,1024]{1,0:T(8,128)S(1)} collective-permute-done((f32[64,1024]{1,0:T(8,128)S(1)}, f32[64,1024]{1,0:T(8,128)S(1)}, u32[]{:S(2)}, u32[]{:S(2)}) %collective-permute-start.8) | collective-permute-done | bytes 262176 | tf_op jit(solution)/shard_map/ppermute | solution.py:20
  183.9 0.1 collective-permute-start.9
  184.0 6.3 %collective-permute-done.5 = f32[1032,64]{0,1:T(8,128)S(1)} collective-permute-done((f32[1032,64]{0,1:T(8,128)S(1)}, f32[1032,64]{0,1:T(8,128)S(1)}, u32[]{:S(2)}, u32[]{:S(2)}) %collective-permute-start.5) | collective-permute-done | bytes 264224 | tf_op jit(solution)/shard_map/ppermute | solution.py:20
  190.3 0.6 collective-permute-start.6
  190.9 5.0 %collective-permute-done.9 = f32[64,1024]{1,0:T(8,128)S(1)} collective-permute-done((f32[64,1024]{1,0:T(8,128)S(1)}, f32[64,1024]{1,0:T(8,128)S(1)}, u32[]{:S(2)}, u32[]{:S(2)}) %collective-permute-start.9) | collective-permute-done | bytes 262176 | tf_op jit(solution)/shard_map/ppermute | solution.py:20
  195.9 0.6 collective-permute-start.10
  196.5 1.1 copy.13
  197.5 9.0 %collective-permute-done.10 = f32[64,1024]{1,0:T(8,128)S(1)} collective-permute-done((f32[64,1024]{1,0:T(8,128)S(1)}, f32[64,1024]{1,0:T(8,128)S(1)}, u32[]{:S(2)}, u32[]{:S(2)}) %collective-permute-start.10) | collective-permute-done | bytes 262176 | tf_op jit(solution)/shard_map/ppermute | solution.py:20
  206.6 0.7 add.71
  207.3 0.0 collective-permute-done.6
  207.3 0.7 slice.19
  208.1 0.5 slice.20
  (19 shorter events, 0.3 us)
Async XLA Ops:
  7.2 115.9 %copy-start = (bf16[64,1024]{1,0:T(8,128)(2,1)S(1)}, bf16[64,1024]{1,0:T(8,128)(2,1)}, u32[]{:S(2)}) copy-start(bf16[64,1024]{1,0:T(8,128)(2,1)} %param.11) | copy-start | bytes 393220
  7.2 2.4 %copy-start.1 = (f32[8192]{0:T(1024)S(1)}, f32[8192]{0:T(1024)}, u32[]{:S(2)}) copy-start(f32[8192]{0:T(1024)} %param.13) | copy-start | bytes 98308
  7.2 3.7 %copy-start.2 = (s32[512]{0:T(512)S(1)}, s32[512]{0:T(512)}, u32[]{:S(2)}) copy-start(s32[512]{0:T(512)} %param.12) | copy-start | bytes 6148
  7.2 100.9 %all-gather.3.cloned.1.call-start = ((), (), s32[]{:S(2)}) async-start(), calls=%async_computation.1 | async-start | bytes 17825792 | tf_op jit(solution)/shard_map/all_gather | solution.py:40
  108.1 16.4 %copy-start.3 = (bf16[8192,1024]{1,0:T(8,128)(2,1)S(1)}, bf16[8192,1024]{1,0:T(8,128)(2,1)}, u32[]{:S(2)}) copy-start(bf16[8192,1024]{1,0:T(8,128)(2,1)} %all-gather.3.cloned.1.call-done) | copy-start | bytes 50331652
  138.2 7.9 %collective-permute-start = (f32[520,64]{0,1:T(8,128)S(1)}, f32[520,64]{0,1:T(8,128)S(1)}, u32[]{:S(2)}, u32[]{:S(2)}) collective-permute-start(f32[520,64]{0,1:T(8,128)S(1)} %concatenate.6), channel_id=1, source_target_pairs={{0,1},{1,0},{2,3},{3,2},{4,5},{5,4},{6,7},{7,6},{8,9},{9,8},{10,11... | collective-permute-start | bytes 399368 | tf_op jit(solution)/shard_map/ppermute | solution.py:20
  146.8 5.6 %collective-permute-start.1 = (f32[520,64]{0,1:T(8,128)S(1)}, f32[520,64]{0,1:T(8,128)S(1)}, u32[]{:S(2)}, u32[]{:S(2)}) collective-permute-start(f32[520,64]{0,1:T(8,128)S(1)} %pad_add_fusion), channel_id=1, source_target_pairs={{0,2},{1,3},{2,0},{3,1},{4,6},{5,7},{6,4},{7,5},{8,10},{9,11},{10,... | collective-permute-start | bytes 399368 | tf_op jit(solution)/shard_map/ppermute | solution.py:20
  152.4 8.5 %collective-permute-start.2 = (f32[520,64]{0,1:T(8,128)S(1)}, f32[520,64]{0,1:T(8,128)}, u32[]{:S(2)}, u32[]{:S(2)}) collective-permute-start(f32[520,64]{0,1:T(8,128)S(1)} %add.62), channel_id=1, source_target_pairs={{0,4},{1,5},{2,6},{3,7},{4,0},{5,1},{6,2},{7,3},{8,12},{9,13},{10,... | collective-permute-start | bytes 399368 | tf_op jit(solution)/shard_map/ppermute | solution.py:20
  155.5 41.0 %all-to-all-start = ((bf16[8,64,1024]{2,1,0:T(8,128)(2,1)}), bf16[8,64,1024]{2,1,0:T(8,128)(2,1)S(1)}, u32[]{:S(2)}, u32[]{:S(2)}) async-start(bf16[8,64,1024]{2,1,0:T(8,128)(2,1)} %bitcast.17), calls=%async_computation | async-start | bytes 2097152 | tf_op jit(solution)/shard_map/all_to_all | solution.py:62
  164.5 1.7 collective-permute-start.3
  165.0 3.0 %collective-permute-start.7 = (f32[64,1024]{1,0:T(8,128)S(1)}, f32[64,1024]{1,0:T(8,128)S(1)}, u32[]{:S(2)}, u32[]{:S(2)}) collective-permute-start(f32[64,1024]{1,0:T(8,128)S(1)} %fusion.4), channel_id=1, source_target_pairs={{0,8},{8,0},{16,24},{24,16},{32,40},{40,32},{48,56},{56,48},{64,72... | collective-permute-start | bytes 786440 | tf_op jit(solution)/shard_map/ppermute | solution.py:20
  166.9 13.6 %collective-permute-start.4 = (f32[1032,64]{0,1:T(8,128)S(1)}, f32[1032,64]{0,1:T(8,128)S(1)}, u32[]{:S(2)}, u32[]{:S(2)}) collective-permute-start(f32[1032,64]{0,1:T(8,128)S(1)} %pad_add_fusion.1), channel_id=1, source_target_pairs={{0,16},{8,24},{16,0},{24,8},{32,48},{40,56},{48,32},{56,40},{64,80... | collective-permute-start | bytes 792584 | tf_op jit(solution)/shard_map/ppermute | solution.py:20
  168.1 15.8 %collective-permute-start.8 = (f32[64,1024]{1,0:T(8,128)S(1)}, f32[64,1024]{1,0:T(8,128)S(1)}, u32[]{:S(2)}, u32[]{:S(2)}) collective-permute-start(f32[64,1024]{1,0:T(8,128)S(1)} %add.68), channel_id=1, source_target_pairs={{0,16},{8,24},{16,0},{24,8},{32,48},{40,56},{48,32},{56,40},{64,80... | collective-permute-start | bytes 786440 | tf_op jit(solution)/shard_map/ppermute | solution.py:20
  180.5 9.7 %collective-permute-start.5 = (f32[1032,64]{0,1:T(8,128)S(1)}, f32[1032,64]{0,1:T(8,128)S(1)}, u32[]{:S(2)}, u32[]{:S(2)}) collective-permute-start(f32[1032,64]{0,1:T(8,128)S(1)} %add.65), channel_id=1, source_target_pairs={{0,32},{8,40},{16,48},{24,56},{32,0},{40,8},{48,16},{56,24},{64,96... | collective-permute-start | bytes 792584 | tf_op jit(solution)/shard_map/ppermute | solution.py:20
  183.9 12.0 %collective-permute-start.9 = (f32[64,1024]{1,0:T(8,128)S(1)}, f32[64,1024]{1,0:T(8,128)S(1)}, u32[]{:S(2)}, u32[]{:S(2)}) collective-permute-start(f32[64,1024]{1,0:T(8,128)S(1)} %add.69), channel_id=1, source_target_pairs={{0,32},{8,40},{16,48},{24,56},{32,0},{40,8},{48,16},{56,24},{64,96... | collective-permute-start | bytes 786440 | tf_op jit(solution)/shard_map/ppermute | solution.py:20
  190.3 17.0 %collective-permute-start.6 = (f32[1032,64]{0,1:T(8,128)S(1)}, f32[1032,64]{0,1:T(8,128)S(1)}, u32[]{:S(2)}, u32[]{:S(2)}) collective-permute-start(f32[1032,64]{0,1:T(8,128)S(1)} %add.66), channel_id=1, source_target_pairs={{0,64},{8,72},{16,80},{24,88},{32,96},{40,104},{48,112},{56,120},{... | collective-permute-start | bytes 792584 | tf_op jit(solution)/shard_map/ppermute | solution.py:20
  195.9 10.7 %collective-permute-start.10 = (f32[64,1024]{1,0:T(8,128)S(1)}, f32[64,1024]{1,0:T(8,128)S(1)}, u32[]{:S(2)}, u32[]{:S(2)}) collective-permute-start(f32[64,1024]{1,0:T(8,128)S(1)} %add.70), channel_id=1, source_target_pairs={{0,64},{8,72},{16,80},{24,88},{32,96},{40,104},{48,112},{56,120},{... | collective-permute-start | bytes 786440 | tf_op jit(solution)/shard_map/ppermute | solution.py:20
Sparse Core Ops, SparseCore 0:
  9.7 98.3 all-gather.2

commit v5 on v4

--- a/solution.py
+++ b/solution.py
@@ -2,6 +2,7 @@
 import jax.numpy as jnp
 from jax import lax
 from jax.sharding import PartitionSpec as P
+
 
 adapter_gain = 0.5
 steer = 90.0
@@ -37,7 +38,10 @@
     rows_mine = hidden_width // parts
     m = lax.axis_index("mp")
 
-    gathered = lax.all_gather(weight, "dp", axis=0, tiled=True)
+    cols = weight.shape[1]
+    split = cols * 3 // 4
+    first = lax.all_gather(weight[:, :split], "dp", axis=0, tiled=True)
+    second = lax.all_gather(weight[:, split:], "dp", axis=0, tiled=True)
 
     my_rows = lax.dynamic_slice_in_dim(updated_input_states, m * rows_mine, rows_mine, 1)
     low_part = jnp.dot(my_rows, adapter_down_weight, preferred_element_type=jnp.float32)
@@ -54,8 +58,12 @@
     unit = control * lax.rsqrt(jnp.sum(control * control) + 1e-06)
     unit_mine = lax.dynamic_slice_in_dim(unit, m * rows_mine, rows_mine, 0)
 
-    ref_rows = row_adder(frozen_input_states, gathered).astype(jnp.bfloat16)
-    base_rows = row_adder(updated_input_states, gathered).astype(jnp.bfloat16)
+    ref_rows = jnp.concatenate(
+        [row_adder(frozen_input_states, w).astype(jnp.bfloat16) for w in (first, second)], axis=1
+    )
+    base_rows = jnp.concatenate(
+        [row_adder(updated_input_states, w).astype(jnp.bfloat16) for w in (first, second)], axis=1
+    )
     updated_output = base_rows.astype(jnp.float32) + adapter_gain * jnp.dot(
         rank_projection, adapter_up_weight, preferred_element_type=jnp.float32
     )
@@ -99,6 +107,5 @@
         P(),
     )
     out_specs = (P(("dp", "mp"), None), P("mp", None), P(None, "mp"), P())
-    return jax.shard_map(
-        per_device, mesh=mesh, in_specs=in_specs, out_specs=out_specs, check_vma=False
-    )
+
+    return jax.shard_map(per_device, mesh=mesh, in_specs=in_specs, out_specs=out_specs, check_vma=False)

time: 216 us -> 241 us (1.12)
  matrix products: 32.3 us -> 40.9 us
  waiting for transfers between devices: 78.5 us -> 86.6 us
  starting transfers between devices: 15.1 us -> 21.9 us
  local copies, waits for them, and re-layouts: 4.16 us -> 7.95 us
  blocking collectives: 64.6 us -> 61.9 us
    dot_general x2 -> x4, matrix products: 26.8 us -> 36.1 us  [row_adder(): return jnp.dot(source, piece, preferred_element_type=jnp.float32)]
    ppermute x11, waiting for transfers between devices: 46.6 us -> 51.9 us  [butterfly_sum(): x = x + lax.ppermute(x, axis, [(i, i ^ step) for i in range(n)])]
    ppermute x11, starting transfers between devices: 9.71 us -> 14.8 us  [butterfly_sum(): x = x + lax.ppermute(x, axis, [(i, i ^ step) for i in range(n)])]
    slice x0 -> x2, local copies, waits for them, and re-layouts: none -> 3.79 us  [the longest x1 2.07 us: per_device(): first = lax.all_gather(weight[:, :split], 'dp', axis=0, tiled=True)]
    all_gather x1 -> x2, waiting for transfers between devices: 31.2 us -> 34.7 us  [the longest x1 34.7 us: per_device(): first = lax.all_gather(weight[:, :split], 'dp', axis=0, tiled=True)]
    psum x1, blocking collectives: 43.5 us -> 41.1 us  [per_device(): rank_projection = lax.psum(low_part, 'mp').astype(jnp.bfloat16)]
  transfers between devices with their start and end apart: 13 -> 14, of which waited for: 9 -> 9; matrix products, arithmetic and copies ran while one was open for 4% -> 9% of each run, Pallas kernels for 0% -> 0%
where the time goes in v5:
time: 241 us
  waiting for transfers between devices  86.6 us (36%)
  blocking collectives  61.9 us (26%)
  matrix products  40.9 us (17%)
  starting transfers between devices  21.9 us (9%)
  between operations  15.6 us (6%)
  local copies, waits for them, and re-layouts  7.95 us (3%)
  other arithmetic  5.92 us (2%)
    ppermute x11, waiting for transfers between devices, butterfly_sum(): x = x + lax.ppermute(x, axis, [(i, i ^ step) for i in range(n)])  51.9 us
    psum x1, blocking collectives, per_device(): rank_projection = lax.psum(low_part, 'mp').astype(jnp.bfloat16)  41.1 us
    dot_general x4, matrix products, row_adder(): return jnp.dot(source, piece, preferred_element_type=jnp.float32)  36.1 us
    all_gather x1, waiting for transfers between devices, per_device(): first = lax.all_gather(weight[:, :split], 'dp', axis=0, tiled=True)  34.7 us
    all_gather x1, blocking collectives, per_device(): all_flags = lax.all_gather(flags, 'dp', axis=0, tiled=True)  20.8 us
    ppermute x11, starting transfers between devices, butterfly_sum(): x = x + lax.ppermute(x, axis, [(i, i ^ step) for i in range(n)])  14.8 us
    all_to_all x1, starting transfers between devices, per_device(): lax.all_to_all(updated_output.astype(jnp.bfloat16), 'mp', split_axis=0, c...  6.97 us
  transfers between devices with their start and end apart: 14, of which 9 were waited for; matrix products, arithmetic and copies ran while one was open for 9% of the time, Pallas kernels for 0%

profile of v5, /device:TPU:4, one launch (start us, length us, event | category | flops | bytes accessed | tf_op | source)
XLA Modules:
  0.0 240.8 jit_solution(1577147540800126035)
XLA Ops:
  7.3 1.7 slice.20
  9.0 0.0 all-gather.4.cloned.1.call-start
  9.1 2.1 slice.19
  11.2 0.6 multiply_reduce_fusion.1
  12.5 20.8 %all-gather = s32[16,1,512]{2,1,0:T(1,128)S(1)} all-gather(s32[1,1,512]{2,1,0:T(1,128)S(1)} %bitcast.24), channel_id=1, replica_groups=mesh['dp'=16,'mp'=8] {'dp'}, dimensions={0}, use_global_device_ids=true | all-gather | bytes 34816 | tf_op jit(solution)/shard_map/all_gather | solution.py:50
  33.3 0.7 reduce_sum.36
  34.6 1.7 fusion.2
  36.3 41.1 %all-reduce.3 = bf16[512,64]{0,1:T(8,128)(2,1)S(1)} all-reduce(f32[512,64]{0,1:T(8,128)S(1)} %fusion.2), channel_id=1, replica_groups=mesh['dp'=16,'mp'=8] {'mp'}, use_global_device_ids=true, to_apply=%region_0.0 | all-reduce | flops 32768 | bytes 196608 | tf_op jit(solution)/shard_map/psum | solution.py:48
  77.5 7.3 %convolution_convert_fusion.3 = bf16[512,256]{1,0:T(8,128)(2,1)S(1)} fusion(bf16[512,8192]{1,0:T(8,128)(2,1)} %param.8, bf16[8192,256]{1,0:T(8,128)(2,1)} %all-gather.6.cloned.1.call-done), kind=kOutput, calls=%fused_computation.7 | convolution fusion | flops 2147614720 | bytes 12845056 | tf_op jit(solution)/shard_map/dot_general | solution.py:14
  84.8 5.9 %convolution_convert_fusion.2 = bf16[512,256]{1,0:T(8,128)(2,1)S(1)} fusion(bf16[512,8192]{1,0:T(8,128)(2,1)} %param.7, bf16[8192,256]{1,0:T(8,128)(2,1)S(1)} %copy-done.5), kind=kOutput, calls=%fused_computation.6 | convolution fusion | flops 2147614720 | bytes 12845056 | tf_op jit(solution)/shard_map/dot_general | solution.py:14
  90.6 34.7 %all-gather.4.cloned.1.call-done = bf16[8192,768]{1,0:T(8,128)(2,1)} async-done(((bf16[512,768]{1,0:T(8,128)(2,1)}), bf16[8192,768]{1,0:T(8,128)(2,1)}) %all-gather.4.cloned.1.call-update) | async-done | bytes 12582928 | tf_op jit(solution)/shard_map/all_gather | solution.py:43
  125.3 13.7 %convolution_convert_fusion = bf16[512,768]{1,0:T(8,128)(2,1)S(1)} fusion(bf16[512,8192]{1,0:T(8,128)(2,1)} %param.7, bf16[8192,768]{1,0:T(8,128)(2,1)} %all-gather.4.cloned.1.call-done), kind=kOutput, calls=%fused_computation.4 | convolution fusion | flops 6442844160 | bytes 21757952 | tf_op jit(solution)/shard_map/dot_general | solution.py:14
  139.0 9.2 %convolution_convert_fusion.1 = bf16[512,768]{1,0:T(8,128)(2,1)S(1)} fusion(bf16[512,8192]{1,0:T(8,128)(2,1)} %param.8, bf16[8192,768]{1,0:T(8,128)(2,1)S(1)} %copy-done.4), kind=kOutput, calls=%fused_computation.5 | convolution fusion | flops 6442844160 | bytes 21757952 | tf_op jit(solution)/shard_map/dot_general | solution.py:14
  148.3 0.9 multiply_reduce_fusion
  149.2 0.6 multiply_reduce_fusion.2
  149.8 1.7 multiply_convert_fusion
  151.5 0.4 fusion.9
  151.9 0.7 concatenate.14
  152.6 1.3 collective-permute-start
  153.9 6.6 %collective-permute-done = f32[520,64]{0,1:T(8,128)S(1)} collective-permute-done((f32[520,64]{0,1:T(8,128)S(1)}, f32[520,64]{0,1:T(8,128)S(1)}, u32[]{:S(2)}, u32[]{:S(2)}) %collective-permute-start) | collective-permute-done | bytes 133152 | tf_op jit(solution)/shard_map/ppermute | solution.py:21
  160.5 0.7 pad_add_fusion
  161.2 1.4 collective-permute-start.1
  162.6 4.3 %collective-permute-done.1 = f32[520,64]{0,1:T(8,128)S(1)} collective-permute-done((f32[520,64]{0,1:T(8,128)S(1)}, f32[520,64]{0,1:T(8,128)S(1)}, u32[]{:S(2)}, u32[]{:S(2)}) %collective-permute-start.1) | collective-permute-done | bytes 133152 | tf_op jit(solution)/shard_map/ppermute | solution.py:21
  166.9 2.8 %collective-permute-start.2 = (f32[520,64]{0,1:T(8,128)S(1)}, f32[520,64]{0,1:T(8,128)S(1)}, u32[]{:S(2)}, u32[]{:S(2)}) collective-permute-start(f32[520,64]{0,1:T(8,128)S(1)} %add.62), channel_id=1, source_target_pairs={{0,4},{1,5},{2,6},{3,7},{4,0},{5,1},{6,2},{7,3},{8,12},{9,13},{10,... | collective-permute-start | bytes 399368 | tf_op jit(solution)/shard_map/ppermute | solution.py:21
  169.7 4.1 %collective-permute-done.2 = f32[520,64]{0,1:T(8,128)S(1)} collective-permute-done((f32[520,64]{0,1:T(8,128)S(1)}, f32[520,64]{0,1:T(8,128)S(1)}, u32[]{:S(2)}, u32[]{:S(2)}) %collective-permute-start.2) | collective-permute-done | bytes 133152 | tf_op jit(solution)/shard_map/ppermute | solution.py:21
  173.9 0.5 slice.26
  174.4 1.5 fusion
  175.9 0.7 concatenate.15
  176.6 0.1 collective-permute-start.3
  176.7 7.0 %all-to-all-start = ((bf16[8,64,1024]{2,1,0:T(8,128)(2,1)}), bf16[8,64,1024]{2,1,0:T(8,128)(2,1)S(1)}, u32[]{:S(2)}, u32[]{:S(2)}) async-start(bf16[8,64,1024]{2,1,0:T(8,128)(2,1)} %bitcast), calls=%async_computation | async-start | bytes 2097152 | tf_op jit(solution)/shard_map/all_to_all | solution.py:70
  183.6 0.3 fusion.10
  183.9 0.1 collective-permute-start.7
  184.0 0.7 pad_add_fusion.1
  184.7 1.4 collective-permute-start.4
  186.2 0.8 collective-permute-start.8
  187.0 17.9 %collective-permute-done.4 = f32[1032,64]{0,1:T(8,128)S(1)} collective-permute-done((f32[1032,64]{0,1:T(8,128)S(1)}, f32[1032,64]{0,1:T(8,128)S(1)}, u32[]{:S(2)}, u32[]{:S(2)}) %collective-permute-start.4) | collective-permute-done | bytes 264224 | tf_op jit(solution)/shard_map/ppermute | solution.py:21
  204.9 1.1 collective-permute-start.5
  206.0 3.7 %collective-permute-done.8 = f32[64,1024]{1,0:T(8,128)S(1)} collective-permute-done((f32[64,1024]{1,0:T(8,128)S(1)}, f32[64,1024]{1,0:T(8,128)S(1)}, u32[]{:S(2)}, u32[]{:S(2)}) %collective-permute-start.8) | collective-permute-done | bytes 262176 | tf_op jit(solution)/shard_map/ppermute | solution.py:21
  209.7 1.1 collective-permute-start.9
  210.8 2.3 collective-permute-done.5
  213.2 2.4 collective-permute-start.6
  215.6 3.4 %collective-permute-done.9 = f32[64,1024]{1,0:T(8,128)S(1)} collective-permute-done((f32[64,1024]{1,0:T(8,128)S(1)}, f32[64,1024]{1,0:T(8,128)S(1)}, u32[]{:S(2)}, u32[]{:S(2)}) %collective-permute-start.9) | collective-permute-done | bytes 262176 | tf_op jit(solution)/shard_map/ppermute | solution.py:21
  219.0 2.4 collective-permute-start.10
  221.4 1.1 copy.19
  222.5 9.4 %collective-permute-done.10 = f32[64,1024]{1,0:T(8,128)S(1)} collective-permute-done((f32[64,1024]{1,0:T(8,128)S(1)}, f32[64,1024]{1,0:T(8,128)S(1)}, u32[]{:S(2)}, u32[]{:S(2)}) %collective-permute-start.10) | collective-permute-done | bytes 262176 | tf_op jit(solution)/shard_map/ppermute | solution.py:21
  231.9 0.7 add.71
  232.7 0.5 slice.28
  233.2 0.7 slice.27
  (31 shorter events, 0.4 us)
Async XLA Ops:
  7.2 141.1 %copy-start = (bf16[64,1024]{1,0:T(8,128)(2,1)S(1)}, bf16[64,1024]{1,0:T(8,128)(2,1)}, u32[]{:S(2)}) copy-start(bf16[64,1024]{1,0:T(8,128)(2,1)} %param.11) | copy-start | bytes 393220
  7.2 4.0 %copy-start.2 = (f32[8192]{0:T(1024)S(1)}, f32[8192]{0:T(1024)}, u32[]{:S(2)}) copy-start(f32[8192]{0:T(1024)} %param.13) | copy-start | bytes 98308
  7.2 5.3 %copy-start.3 = (s32[512]{0:T(512)S(1)}, s32[512]{0:T(512)}, u32[]{:S(2)}) copy-start(s32[512]{0:T(512)} %param.12) | copy-start | bytes 6148
  7.2 27.4 %copy-start.1 = (bf16[1024,64]{0,1:T(8,128)(2,1)S(1)}, bf16[1024,64]{0,1:T(8,128)(2,1)}, u32[]{:S(2)}) copy-start(bf16[1024,64]{0,1:T(8,128)(2,1)} %param.10) | copy-start | bytes 393220
  7.2 70.3 %all-gather.6.cloned.1.call-start = ((), (), s32[]{:S(2)}) async-start(), calls=%async_computation.2 | async-start | bytes 4456448 | tf_op jit(solution)/shard_map/all_gather | solution.py:44
  9.0 116.3 %all-gather.4.cloned.1.call-start = ((), (), s32[]{:S(2)}) async-start(), calls=%async_computation.1 | async-start | bytes 13369344 | tf_op jit(solution)/shard_map/all_gather | solution.py:43
  77.5 7.3 %copy-start.5 = (bf16[8192,256]{1,0:T(8,128)(2,1)S(1)}, bf16[8192,256]{1,0:T(8,128)(2,1)}, u32[]{:S(2)}) copy-start(bf16[8192,256]{1,0:T(8,128)(2,1)} %all-gather.6.cloned.1.call-done) | copy-start | bytes 12582916
  125.3 13.7 %copy-start.4 = (bf16[8192,768]{1,0:T(8,128)(2,1)S(1)}, bf16[8192,768]{1,0:T(8,128)(2,1)}, u32[]{:S(2)}) copy-start(bf16[8192,768]{1,0:T(8,128)(2,1)} %all-gather.4.cloned.1.call-done) | copy-start | bytes 37748740
  152.6 7.9 %collective-permute-start = (f32[520,64]{0,1:T(8,128)S(1)}, f32[520,64]{0,1:T(8,128)S(1)}, u32[]{:S(2)}, u32[]{:S(2)}) collective-permute-start(f32[520,64]{0,1:T(8,128)S(1)} %concatenate.14), channel_id=1, source_target_pairs={{0,1},{1,0},{2,3},{3,2},{4,5},{5,4},{6,7},{7,6},{8,9},{9,8},{10,11... | collective-permute-start | bytes 399368 | tf_op jit(solution)/shard_map/ppermute | solution.py:21
  161.2 5.7 %collective-permute-start.1 = (f32[520,64]{0,1:T(8,128)S(1)}, f32[520,64]{0,1:T(8,128)S(1)}, u32[]{:S(2)}, u32[]{:S(2)}) collective-permute-start(f32[520,64]{0,1:T(8,128)S(1)} %pad_add_fusion), channel_id=1, source_target_pairs={{0,2},{1,3},{2,0},{3,1},{4,6},{5,7},{6,4},{7,5},{8,10},{9,11},{10,... | collective-permute-start | bytes 399368 | tf_op jit(solution)/shard_map/ppermute | solution.py:21
  166.9 6.9 %collective-permute-start.2 = (f32[520,64]{0,1:T(8,128)S(1)}, f32[520,64]{0,1:T(8,128)S(1)}, u32[]{:S(2)}, u32[]{:S(2)}) collective-permute-start(f32[520,64]{0,1:T(8,128)S(1)} %add.62), channel_id=1, source_target_pairs={{0,4},{1,5},{2,6},{3,7},{4,0},{5,1},{6,2},{7,3},{8,12},{9,13},{10,... | collective-permute-start | bytes 399368 | tf_op jit(solution)/shard_map/ppermute | solution.py:21
  176.6 7.5 %collective-permute-start.3 = (f32[1032,64]{0,1:T(8,128)S(1)}, f32[1032,64]{0,1:T(8,128)S(1)}, u32[]{:S(2)}, u32[]{:S(2)}) collective-permute-start(f32[1032,64]{0,1:T(8,128)S(1)} %concatenate.15), channel_id=1, source_target_pairs={{0,8},{8,0},{16,24},{24,16},{32,40},{40,32},{48,56},{56,48},{64,72... | collective-permute-start | bytes 792584 | tf_op jit(solution)/shard_map/ppermute | solution.py:21
  176.7 44.8 %all-to-all-start = ((bf16[8,64,1024]{2,1,0:T(8,128)(2,1)}), bf16[8,64,1024]{2,1,0:T(8,128)(2,1)S(1)}, u32[]{:S(2)}, u32[]{:S(2)}) async-start(bf16[8,64,1024]{2,1,0:T(8,128)(2,1)} %bitcast), calls=%async_computation | async-start | bytes 2097152 | tf_op jit(solution)/shard_map/all_to_all | solution.py:70
  183.9 2.2 collective-permute-start.7
  184.7 20.1 %collective-permute-start.4 = (f32[1032,64]{0,1:T(8,128)S(1)}, f32[1032,64]{0,1:T(8,128)S(1)}, u32[]{:S(2)}, u32[]{:S(2)}) collective-permute-start(f32[1032,64]{0,1:T(8,128)S(1)} %pad_add_fusion.1), channel_id=1, source_target_pairs={{0,16},{8,24},{16,0},{24,8},{32,48},{40,56},{48,32},{56,40},{64,80... | collective-permute-start | bytes 792584 | tf_op jit(solution)/shard_map/ppermute | solution.py:21
  186.2 23.5 %collective-permute-start.8 = (f32[64,1024]{1,0:T(8,128)S(1)}, f32[64,1024]{1,0:T(8,128)S(1)}, u32[]{:S(2)}, u32[]{:S(2)}) collective-permute-start(f32[64,1024]{1,0:T(8,128)S(1)} %add.68), channel_id=1, source_target_pairs={{0,16},{8,24},{16,0},{24,8},{32,48},{40,56},{48,32},{56,40},{64,80... | collective-permute-start | bytes 786440 | tf_op jit(solution)/shard_map/ppermute | solution.py:21
  204.9 8.3 %collective-permute-start.5 = (f32[1032,64]{0,1:T(8,128)S(1)}, f32[1032,64]{0,1:T(8,128)S(1)}, u32[]{:S(2)}, u32[]{:S(2)}) collective-permute-start(f32[1032,64]{0,1:T(8,128)S(1)} %add.65), channel_id=1, source_target_pairs={{0,32},{8,40},{16,48},{24,56},{32,0},{40,8},{48,16},{56,24},{64,96... | collective-permute-start | bytes 792584 | tf_op jit(solution)/shard_map/ppermute | solution.py:21
  209.7 9.3 %collective-permute-start.9 = (f32[64,1024]{1,0:T(8,128)S(1)}, f32[64,1024]{1,0:T(8,128)S(1)}, u32[]{:S(2)}, u32[]{:S(2)}) collective-permute-start(f32[64,1024]{1,0:T(8,128)S(1)} %add.69), channel_id=1, source_target_pairs={{0,32},{8,40},{16,48},{24,56},{32,0},{40,8},{48,16},{56,24},{64,96... | collective-permute-start | bytes 786440 | tf_op jit(solution)/shard_map/ppermute | solution.py:21
  213.2 19.5 %collective-permute-start.6 = (f32[1032,64]{0,1:T(8,128)S(1)}, f32[1032,64]{0,1:T(8,128)S(1)}, u32[]{:S(2)}, u32[]{:S(2)}) collective-permute-start(f32[1032,64]{0,1:T(8,128)S(1)} %add.66), channel_id=1, source_target_pairs={{0,64},{8,72},{16,80},{24,88},{32,96},{40,104},{48,112},{56,120},{... | collective-permute-start | bytes 792584 | tf_op jit(solution)/shard_map/ppermute | solution.py:21
  219.0 12.9 %collective-permute-start.10 = (f32[64,1024]{1,0:T(8,128)S(1)}, f32[64,1024]{1,0:T(8,128)S(1)}, u32[]{:S(2)}, u32[]{:S(2)}) collective-permute-start(f32[64,1024]{1,0:T(8,128)S(1)} %add.70), channel_id=1, source_target_pairs={{0,64},{8,72},{16,80},{24,88},{32,96},{40,104},{48,112},{56,120},{... | collective-permute-start | bytes 786440 | tf_op jit(solution)/shard_map/ppermute | solution.py:21
Sparse Core Ops, SparseCore 0:
  10.3 39.8 all-gather.5
  52.5 72.7 all-gather.3

commit v6 on v4

--- a/solution.py
+++ b/solution.py
@@ -13,12 +13,13 @@
     return jnp.dot(source, piece, preferred_element_type=jnp.float32)
 
 
+MASKS = {"dp": (1, 2, 4, 12), "mp": (1, 2, 6)}
+
+
 def butterfly_sum(x, axis):
     n = lax.axis_size(axis)
-    step = 1
-    while step < n:
-        x = x + lax.ppermute(x, axis, [(i, i ^ step) for i in range(n)])
-        step *= 2
+    for mask in MASKS[axis]:
+        x = x + lax.ppermute(x, axis, [(i, i ^ mask) for i in range(n)])
     return x
 
 

time: 216 us -> 212 us (0.981)
  waiting for transfers between devices: 78.5 us -> 72.3 us
    ppermute x11, waiting for transfers between devices: 46.6 us -> 40.4 us  [butterfly_sum(): x = x + lax.ppermute(x, axis, [(i, i ^ mask) for i in range(n)])]
    ppermute x11, starting transfers between devices: 9.71 us -> 12.1 us  [butterfly_sum(): x = x + lax.ppermute(x, axis, [(i, i ^ mask) for i in range(n)])]
  transfers between devices with their start and end apart: 13 -> 13, of which waited for: 9 -> 9; matrix products, arithmetic and copies ran while one was open for 4% -> 5% of each run, Pallas kernels for 0% -> 0%
where the time goes in v6:
time: 212 us; the launch traced here: 211 us
  waiting for transfers between devices  72.3 us (34%)
  blocking collectives  64.6 us (30%)
  matrix products  32.3 us (15%)
  starting transfers between devices  17.2 us (8%)
  between operations  15.6 us (7%)
  other arithmetic  5.16 us (2%)
  local copies, waits for them, and re-layouts  4.16 us (2%)
    psum x1, blocking collectives, per_device(): rank_projection = lax.psum(low_part, 'mp').astype(jnp.bfloat16)  43.5 us
    ppermute x11, waiting for transfers between devices, butterfly_sum(): x = x + lax.ppermute(x, axis, [(i, i ^ mask) for i in range(n)])  40.4 us
    all_gather x1, waiting for transfers between devices, per_device(): gathered = lax.all_gather(weight, 'dp', axis=0, tiled=True)  31.2 us
    dot_general x2, matrix products, row_adder(): return jnp.dot(source, piece, preferred_element_type=jnp.float32)  26.8 us
    all_gather x1, blocking collectives, per_device(): all_flags = lax.all_gather(flags, 'dp', axis=0, tiled=True)  21.1 us
    ppermute x11, starting transfers between devices, butterfly_sum(): x = x + lax.ppermute(x, axis, [(i, i ^ mask) for i in range(n)])  12.1 us
    all_to_all x1, starting transfers between devices, per_device(): lax.all_to_all(updated_output.astype(jnp.bfloat16), 'mp', split_axis=0, c...  5.03 us
  transfers between devices with their start and end apart: 13, of which 9 were waited for; matrix products, arithmetic and copies ran while one was open for 5% of the time, Pallas kernels for 0%

profile of v6, /device:TPU:4, one launch (start us, length us, event | category | flops | bytes accessed | tf_op | source)
XLA Modules:
  0.0 211.3 jit_solution(5986174039691629683)
XLA Ops:
  7.2 0.0 copy-start
  7.2 0.0 all-gather.3.cloned.1.call-start
  7.2 0.7 all-gather.3.cloned.1.call-update
  7.9 1.7 fusion.2
  9.6 0.6 multiply_reduce_fusion.1
  10.9 21.1 %all-gather = s32[16,1,512]{2,1,0:T(1,128)S(1)} all-gather(s32[1,1,512]{2,1,0:T(1,128)S(1)} %bitcast.19), channel_id=1, replica_groups=mesh['dp'=16,'mp'=8] {'dp'}, dimensions={0}, use_global_device_ids=true | all-gather | bytes 34816 | tf_op jit(solution)/shard_map/all_gather | solution.py:47
  32.0 0.7 reduce_sum.36
  33.4 43.5 %all-reduce.3 = bf16[512,64]{0,1:T(8,128)(2,1)S(1)} all-reduce(f32[512,64]{0,1:T(8,128)S(1)} %fusion.2), channel_id=1, replica_groups=mesh['dp'=16,'mp'=8] {'mp'}, use_global_device_ids=true, to_apply=%region_0.0 | all-reduce | flops 32768 | bytes 196608 | tf_op jit(solution)/shard_map/psum | solution.py:45
  76.9 31.2 %all-gather.3.cloned.1.call-done = bf16[8192,1024]{1,0:T(8,128)(2,1)} async-done(((bf16[512,1024]{1,0:T(8,128)(2,1)}), bf16[8192,1024]{1,0:T(8,128)(2,1)}) %all-gather.3.cloned.1.call-update) | async-done | bytes 16777232 | tf_op jit(solution)/shard_map/all_gather | solution.py:41
  108.1 14.9 %convolution_convert_fusion.1 = bf16[512,1024]{1,0:T(8,128)(2,1)S(1)} fusion(bf16[512,8192]{1,0:T(8,128)(2,1)} %param.8, bf16[8192,1024]{1,0:T(8,128)(2,1)} %all-gather.3.cloned.1.call-done), kind=kOutput, calls=%fused_computation.5 | convolution fusion | flops 8590458880 | bytes 26214400 | tf_op jit(solution)/shard_map/dot_general | solution.py:13
  123.1 1.4 fusion.10
  124.5 11.9 %multiply_reduce_fusion = (f32[512]{0:T(512)S(1)}, f32[512,1024]{1,0:T(8,128)S(1)}) fusion(f32[512,1024]{1,0:T(8,128)S(1)} %get-tuple-element.9, bf16[512,8192]{1,0:T(8,128)(2,1)} %param.7, bf16[8192,1024]{1,0:T(8,128)(2,1)S(1)} %copy-done.3, f32[512]{0:T(512)S(1)} %get-tuple-element.7, f32[1024]{0:T(1024)S(1)} %dynamic-slice_multiply_fusion, ...), kind=kOutput, calls=%fused_computation | convolution fusion | flops 8594128896 | bytes 29370368 | tf_op jit(solution)/shard_map/dot_general | solution.py:13
  136.4 0.6 multiply_reduce_fusion.2
  137.0 0.5 fusion.9
  137.5 0.7 concatenate.6
  138.2 0.9 collective-permute-start
  139.1 7.0 %collective-permute-done = f32[520,64]{0,1:T(8,128)S(1)} collective-permute-done((f32[520,64]{0,1:T(8,128)S(1)}, f32[520,64]{0,1:T(8,128)S(1)}, u32[]{:S(2)}, u32[]{:S(2)}) %collective-permute-start) | collective-permute-done | bytes 133152 | tf_op jit(solution)/shard_map/ppermute | solution.py:22
  146.1 0.7 pad_add_fusion
  146.8 1.6 collective-permute-start.1
  148.4 4.0 %collective-permute-done.1 = f32[520,64]{0,1:T(8,128)S(1)} collective-permute-done((f32[520,64]{0,1:T(8,128)S(1)}, f32[520,64]{0,1:T(8,128)S(1)}, u32[]{:S(2)}, u32[]{:S(2)}) %collective-permute-start.1) | collective-permute-done | bytes 133152 | tf_op jit(solution)/shard_map/ppermute | solution.py:22
  152.4 2.8 %collective-permute-start.2 = (f32[520,64]{0,1:T(8,128)S(1)}, f32[520,64]{0,1:T(8,128)}, u32[]{:S(2)}, u32[]{:S(2)}) collective-permute-start(f32[520,64]{0,1:T(8,128)S(1)} %add.62), channel_id=1, source_target_pairs={{0,6},{1,7},{2,4},{3,5},{4,2},{5,3},{6,0},{7,1},{8,14},{9,15},{10,... | collective-permute-start | bytes 399368 | tf_op jit(solution)/shard_map/ppermute | solution.py:22
  155.2 5.0 %all-to-all-start = ((bf16[8,64,1024]{2,1,0:T(8,128)(2,1)}), bf16[8,64,1024]{2,1,0:T(8,128)(2,1)S(1)}, u32[]{:S(2)}, u32[]{:S(2)}) async-start(bf16[8,64,1024]{2,1,0:T(8,128)(2,1)} %bitcast.17), calls=%async_computation | async-start | bytes 2097152 | tf_op jit(solution)/shard_map/all_to_all | solution.py:63
  160.2 0.0 collective-permute-done.2
  160.3 0.9 add.63
  161.2 1.5 fusion
  162.7 0.5 slice.18
  163.2 0.7 concatenate.7
  163.9 0.1 collective-permute-start.3
  164.0 0.4 fusion.4
  164.4 0.6 collective-permute-start.7
  165.0 0.6 collective-permute-done.3
  165.6 0.7 pad_add_fusion.1
  166.3 1.2 collective-permute-start.4
  167.4 0.0 collective-permute-done.7
  167.5 1.0 collective-permute-start.8
  168.5 11.4 %collective-permute-done.4 = f32[1032,64]{0,1:T(8,128)S(1)} collective-permute-done((f32[1032,64]{0,1:T(8,128)S(1)}, f32[1032,64]{0,1:T(8,128)S(1)}, u32[]{:S(2)}, u32[]{:S(2)}) %collective-permute-start.4) | collective-permute-done | bytes 264224 | tf_op jit(solution)/shard_map/ppermute | solution.py:22
  179.9 0.1 collective-permute-start.5
  180.0 3.2 %collective-permute-done.8 = f32[64,1024]{1,0:T(8,128)S(1)} collective-permute-done((f32[64,1024]{1,0:T(8,128)S(1)}, f32[64,1024]{1,0:T(8,128)S(1)}, u32[]{:S(2)}, u32[]{:S(2)}) %collective-permute-start.8) | collective-permute-done | bytes 262176 | tf_op jit(solution)/shard_map/ppermute | solution.py:22
  183.3 0.1 collective-permute-start.9
  183.4 6.2 %collective-permute-done.5 = f32[1032,64]{0,1:T(8,128)S(1)} collective-permute-done((f32[1032,64]{0,1:T(8,128)S(1)}, f32[1032,64]{0,1:T(8,128)S(1)}, u32[]{:S(2)}, u32[]{:S(2)}) %collective-permute-start.5) | collective-permute-done | bytes 264224 | tf_op jit(solution)/shard_map/ppermute | solution.py:22
  189.6 1.5 collective-permute-start.6
  191.1 1.3 collective-permute-done.9
  192.4 2.3 %collective-permute-start.10 = (f32[64,1024]{1,0:T(8,128)S(1)}, f32[64,1024]{1,0:T(8,128)S(1)}, u32[]{:S(2)}, u32[]{:S(2)}) collective-permute-start(f32[64,1024]{1,0:T(8,128)S(1)} %add.70), channel_id=1, source_target_pairs={{0,96},{8,104},{16,112},{24,120},{32,64},{40,72},{48,80},{56,88},{... | collective-permute-start | bytes 786440 | tf_op jit(solution)/shard_map/ppermute | solution.py:22
  194.7 1.1 copy.13
  195.8 6.7 %collective-permute-done.10 = f32[64,1024]{1,0:T(8,128)S(1)} collective-permute-done((f32[64,1024]{1,0:T(8,128)S(1)}, f32[64,1024]{1,0:T(8,128)S(1)}, u32[]{:S(2)}, u32[]{:S(2)}) %collective-permute-start.10) | collective-permute-done | bytes 262176 | tf_op jit(solution)/shard_map/ppermute | solution.py:22
  202.4 0.7 add.71
  203.2 0.7 slice.19
  203.9 0.5 slice.20
  (19 shorter events, 0.3 us)
Async XLA Ops:
  7.2 115.9 %copy-start = (bf16[64,1024]{1,0:T(8,128)(2,1)S(1)}, bf16[64,1024]{1,0:T(8,128)(2,1)}, u32[]{:S(2)}) copy-start(bf16[64,1024]{1,0:T(8,128)(2,1)} %param.11) | copy-start | bytes 393220
  7.2 2.4 %copy-start.1 = (f32[8192]{0:T(1024)S(1)}, f32[8192]{0:T(1024)}, u32[]{:S(2)}) copy-start(f32[8192]{0:T(1024)} %param.13) | copy-start | bytes 98308
  7.2 3.7 %copy-start.2 = (s32[512]{0:T(512)S(1)}, s32[512]{0:T(512)}, u32[]{:S(2)}) copy-start(s32[512]{0:T(512)} %param.12) | copy-start | bytes 6148
  7.2 100.9 %all-gather.3.cloned.1.call-start = ((), (), s32[]{:S(2)}) async-start(), calls=%async_computation.1 | async-start | bytes 17825792 | tf_op jit(solution)/shard_map/all_gather | solution.py:41
  108.1 16.4 %copy-start.3 = (bf16[8192,1024]{1,0:T(8,128)(2,1)S(1)}, bf16[8192,1024]{1,0:T(8,128)(2,1)}, u32[]{:S(2)}) copy-start(bf16[8192,1024]{1,0:T(8,128)(2,1)} %all-gather.3.cloned.1.call-done) | copy-start | bytes 50331652
  138.2 7.9 %collective-permute-start = (f32[520,64]{0,1:T(8,128)S(1)}, f32[520,64]{0,1:T(8,128)S(1)}, u32[]{:S(2)}, u32[]{:S(2)}) collective-permute-start(f32[520,64]{0,1:T(8,128)S(1)} %concatenate.6), channel_id=1, source_target_pairs={{0,1},{1,0},{2,3},{3,2},{4,5},{5,4},{6,7},{7,6},{8,9},{9,8},{10,11... | collective-permute-start | bytes 399368 | tf_op jit(solution)/shard_map/ppermute | solution.py:22
  146.8 5.6 %collective-permute-start.1 = (f32[520,64]{0,1:T(8,128)S(1)}, f32[520,64]{0,1:T(8,128)S(1)}, u32[]{:S(2)}, u32[]{:S(2)}) collective-permute-start(f32[520,64]{0,1:T(8,128)S(1)} %pad_add_fusion), channel_id=1, source_target_pairs={{0,2},{1,3},{2,0},{3,1},{4,6},{5,7},{6,4},{7,5},{8,10},{9,11},{10,... | collective-permute-start | bytes 399368 | tf_op jit(solution)/shard_map/ppermute | solution.py:22
  152.4 7.9 %collective-permute-start.2 = (f32[520,64]{0,1:T(8,128)S(1)}, f32[520,64]{0,1:T(8,128)}, u32[]{:S(2)}, u32[]{:S(2)}) collective-permute-start(f32[520,64]{0,1:T(8,128)S(1)} %add.62), channel_id=1, source_target_pairs={{0,6},{1,7},{2,4},{3,5},{4,2},{5,3},{6,0},{7,1},{8,14},{9,15},{10,... | collective-permute-start | bytes 399368 | tf_op jit(solution)/shard_map/ppermute | solution.py:22
  155.2 39.5 %all-to-all-start = ((bf16[8,64,1024]{2,1,0:T(8,128)(2,1)}), bf16[8,64,1024]{2,1,0:T(8,128)(2,1)S(1)}, u32[]{:S(2)}, u32[]{:S(2)}) async-start(bf16[8,64,1024]{2,1,0:T(8,128)(2,1)} %bitcast.17), calls=%async_computation | async-start | bytes 2097152 | tf_op jit(solution)/shard_map/all_to_all | solution.py:63
  163.9 1.7 collective-permute-start.3
  164.4 3.0 %collective-permute-start.7 = (f32[64,1024]{1,0:T(8,128)S(1)}, f32[64,1024]{1,0:T(8,128)S(1)}, u32[]{:S(2)}, u32[]{:S(2)}) collective-permute-start(f32[64,1024]{1,0:T(8,128)S(1)} %fusion.4), channel_id=1, source_target_pairs={{0,8},{8,0},{16,24},{24,16},{32,40},{40,32},{48,56},{56,48},{64,72... | collective-permute-start | bytes 786440 | tf_op jit(solution)/shard_map/ppermute | solution.py:22
  166.3 13.6 %collective-permute-start.4 = (f32[1032,64]{0,1:T(8,128)S(1)}, f32[1032,64]{0,1:T(8,128)S(1)}, u32[]{:S(2)}, u32[]{:S(2)}) collective-permute-start(f32[1032,64]{0,1:T(8,128)S(1)} %pad_add_fusion.1), channel_id=1, source_target_pairs={{0,16},{8,24},{16,0},{24,8},{32,48},{40,56},{48,32},{56,40},{64,80... | collective-permute-start | bytes 792584 | tf_op jit(solution)/shard_map/ppermute | solution.py:22
  167.5 15.8 %collective-permute-start.8 = (f32[64,1024]{1,0:T(8,128)S(1)}, f32[64,1024]{1,0:T(8,128)S(1)}, u32[]{:S(2)}, u32[]{:S(2)}) collective-permute-start(f32[64,1024]{1,0:T(8,128)S(1)} %add.68), channel_id=1, source_target_pairs={{0,16},{8,24},{16,0},{24,8},{32,48},{40,56},{48,32},{56,40},{64,80... | collective-permute-start | bytes 786440 | tf_op jit(solution)/shard_map/ppermute | solution.py:22
  179.9 9.6 %collective-permute-start.5 = (f32[1032,64]{0,1:T(8,128)S(1)}, f32[1032,64]{0,1:T(8,128)S(1)}, u32[]{:S(2)}, u32[]{:S(2)}) collective-permute-start(f32[1032,64]{0,1:T(8,128)S(1)} %add.65), channel_id=1, source_target_pairs={{0,32},{8,40},{16,48},{24,56},{32,0},{40,8},{48,16},{56,24},{64,96... | collective-permute-start | bytes 792584 | tf_op jit(solution)/shard_map/ppermute | solution.py:22
  183.3 9.1 %collective-permute-start.9 = (f32[64,1024]{1,0:T(8,128)S(1)}, f32[64,1024]{1,0:T(8,128)S(1)}, u32[]{:S(2)}, u32[]{:S(2)}) collective-permute-start(f32[64,1024]{1,0:T(8,128)S(1)} %add.69), channel_id=1, source_target_pairs={{0,32},{8,40},{16,48},{24,56},{32,0},{40,8},{48,16},{56,24},{64,96... | collective-permute-start | bytes 786440 | tf_op jit(solution)/shard_map/ppermute | solution.py:22
  189.6 13.6 %collective-permute-start.6 = (f32[1032,64]{0,1:T(8,128)S(1)}, f32[1032,64]{0,1:T(8,128)S(1)}, u32[]{:S(2)}, u32[]{:S(2)}) collective-permute-start(f32[1032,64]{0,1:T(8,128)S(1)} %add.66), channel_id=1, source_target_pairs={{0,96},{8,104},{16,112},{24,120},{32,64},{40,72},{48,80},{56,88},{... | collective-permute-start | bytes 792584 | tf_op jit(solution)/shard_map/ppermute | solution.py:22
  192.4 10.0 %collective-permute-start.10 = (f32[64,1024]{1,0:T(8,128)S(1)}, f32[64,1024]{1,0:T(8,128)S(1)}, u32[]{:S(2)}, u32[]{:S(2)}) collective-permute-start(f32[64,1024]{1,0:T(8,128)S(1)} %add.70), channel_id=1, source_target_pairs={{0,96},{8,104},{16,112},{24,120},{32,64},{40,72},{48,80},{56,88},{... | collective-permute-start | bytes 786440 | tf_op jit(solution)/shard_map/ppermute | solution.py:22
Sparse Core Ops, SparseCore 0:
  9.7 98.3 all-gather.2

commit v7 on v6

--- a/solution.py
+++ b/solution.py
@@ -13,7 +13,7 @@
     return jnp.dot(source, piece, preferred_element_type=jnp.float32)
 
 
-MASKS = {"dp": (1, 2, 4, 12), "mp": (1, 2, 6)}
+MASKS = {"dp": (1, 4, 12, 2), "mp": (2, 6, 1)}
 
 
 def butterfly_sum(x, axis):

time: 212 us -> 207 us (0.976)
  waiting for transfers between devices: 72.3 us -> 61 us
  starting transfers between devices: 17.2 us -> 24.2 us
    ppermute x11, waiting for transfers between devices: 40.4 us -> 29.1 us  [butterfly_sum(): x = x + lax.ppermute(x, axis, [(i, i ^ mask) for i in range(n)])]
    ppermute x11, starting transfers between devices: 12.1 us -> 17.2 us  [butterfly_sum(): x = x + lax.ppermute(x, axis, [(i, i ^ mask) for i in range(n)])]
where the time goes in v7:
time: 207 us
  blocking collectives  64.6 us (31%)
  waiting for transfers between devices  61 us (29%)
  matrix products  32.3 us (16%)
  starting transfers between devices  24.2 us (12%)
  between operations  15.6 us (8%)
  other arithmetic  5.16 us (2%)
  local copies, waits for them, and re-layouts  4.16 us (2%)
    psum x1, blocking collectives, per_device(): rank_projection = lax.psum(low_part, 'mp').astype(jnp.bfloat16)  43.5 us
    all_gather x1, waiting for transfers between devices, per_device(): gathered = lax.all_gather(weight, 'dp', axis=0, tiled=True)  31.2 us
    ppermute x11, waiting for transfers between devices, butterfly_sum(): x = x + lax.ppermute(x, axis, [(i, i ^ mask) for i in range(n)])  29.1 us
    dot_general x2, matrix products, row_adder(): return jnp.dot(source, piece, preferred_element_type=jnp.float32)  26.8 us
    all_gather x1, blocking collectives, per_device(): all_flags = lax.all_gather(flags, 'dp', axis=0, tiled=True)  21.1 us
    ppermute x11, starting transfers between devices, butterfly_sum(): x = x + lax.ppermute(x, axis, [(i, i ^ mask) for i in range(n)])  17.2 us
    all_to_all x1, starting transfers between devices, per_device(): lax.all_to_all(updated_output.astype(jnp.bfloat16), 'mp', split_axis=0, c...  6.97 us
  transfers between devices with their start and end apart: 13, of which 9 were waited for; matrix products, arithmetic and copies ran while one was open for 5% of the time, Pallas kernels for 0%

profile of v7, /device:TPU:4, one launch (start us, length us, event | category | flops | bytes accessed | tf_op | source)
XLA Modules:
  0.0 207.0 jit_solution(15332622908893375235)
XLA Ops:
  7.2 0.0 copy-start
  7.2 0.0 all-gather.3.cloned.1.call-start
  7.2 0.7 all-gather.3.cloned.1.call-update
  7.9 1.7 fusion.2
  9.6 0.6 multiply_reduce_fusion.1
  10.9 21.1 %all-gather = s32[16,1,512]{2,1,0:T(1,128)S(1)} all-gather(s32[1,1,512]{2,1,0:T(1,128)S(1)} %bitcast.19), channel_id=1, replica_groups=mesh['dp'=16,'mp'=8] {'dp'}, dimensions={0}, use_global_device_ids=true | all-gather | bytes 34816 | tf_op jit(solution)/shard_map/all_gather | solution.py:47
  32.0 0.7 reduce_sum.36
  33.4 43.5 %all-reduce.3 = bf16[512,64]{0,1:T(8,128)(2,1)S(1)} all-reduce(f32[512,64]{0,1:T(8,128)S(1)} %fusion.2), channel_id=1, replica_groups=mesh['dp'=16,'mp'=8] {'mp'}, use_global_device_ids=true, to_apply=%region_0.0 | all-reduce | flops 32768 | bytes 196608 | tf_op jit(solution)/shard_map/psum | solution.py:45
  76.9 31.2 %all-gather.3.cloned.1.call-done = bf16[8192,1024]{1,0:T(8,128)(2,1)} async-done(((bf16[512,1024]{1,0:T(8,128)(2,1)}), bf16[8192,1024]{1,0:T(8,128)(2,1)}) %all-gather.3.cloned.1.call-update) | async-done | bytes 16777232 | tf_op jit(solution)/shard_map/all_gather | solution.py:41
  108.1 14.9 %convolution_convert_fusion.1 = bf16[512,1024]{1,0:T(8,128)(2,1)S(1)} fusion(bf16[512,8192]{1,0:T(8,128)(2,1)} %param.8, bf16[8192,1024]{1,0:T(8,128)(2,1)} %all-gather.3.cloned.1.call-done), kind=kOutput, calls=%fused_computation.5 | convolution fusion | flops 8590458880 | bytes 26214400 | tf_op jit(solution)/shard_map/dot_general | solution.py:13
  123.1 1.4 fusion.10
  124.5 11.9 %multiply_reduce_fusion = (f32[512]{0:T(512)S(1)}, f32[512,1024]{1,0:T(8,128)S(1)}) fusion(f32[512,1024]{1,0:T(8,128)S(1)} %get-tuple-element.9, bf16[512,8192]{1,0:T(8,128)(2,1)} %param.7, bf16[8192,1024]{1,0:T(8,128)(2,1)S(1)} %copy-done.3, f32[512]{0:T(512)S(1)} %get-tuple-element.7, f32[1024]{0:T(1024)S(1)} %dynamic-slice_multiply_fusion, ...), kind=kOutput, calls=%fused_computation | convolution fusion | flops 8594128896 | bytes 29370368 | tf_op jit(solution)/shard_map/dot_general | solution.py:13
  136.4 0.6 multiply_reduce_fusion.2
  137.0 0.5 fusion.9
  137.5 0.7 concatenate.6
  138.2 1.6 collective-permute-start
  139.8 4.9 %collective-permute-done = f32[520,64]{0,1:T(8,128)S(1)} collective-permute-done((f32[520,64]{0,1:T(8,128)S(1)}, f32[520,64]{0,1:T(8,128)S(1)}, u32[]{:S(2)}, u32[]{:S(2)}) %collective-permute-start) | collective-permute-done | bytes 133152 | tf_op jit(solution)/shard_map/ppermute | solution.py:22
  144.6 0.7 pad_add_fusion
  145.3 2.8 %collective-permute-start.1 = (f32[520,64]{0,1:T(8,128)S(1)}, f32[520,64]{0,1:T(8,128)S(1)}, u32[]{:S(2)}, u32[]{:S(2)}) collective-permute-start(f32[520,64]{0,1:T(8,128)S(1)} %pad_add_fusion), channel_id=1, source_target_pairs={{0,6},{1,7},{2,4},{3,5},{4,2},{5,3},{6,0},{7,1},{8,14},{9,15},{10,... | collective-permute-start | bytes 399368 | tf_op jit(solution)/shard_map/ppermute | solution.py:22
  148.1 4.0 %collective-permute-done.1 = f32[520,64]{0,1:T(8,128)S(1)} collective-permute-done((f32[520,64]{0,1:T(8,128)S(1)}, f32[520,64]{0,1:T(8,128)S(1)}, u32[]{:S(2)}, u32[]{:S(2)}) %collective-permute-start.1) | collective-permute-done | bytes 133152 | tf_op jit(solution)/shard_map/ppermute | solution.py:22
  152.1 0.9 collective-permute-start.2
  153.0 7.0 %all-to-all-start = ((bf16[8,64,1024]{2,1,0:T(8,128)(2,1)}), bf16[8,64,1024]{2,1,0:T(8,128)(2,1)S(1)}, u32[]{:S(2)}, u32[]{:S(2)}) async-start(bf16[8,64,1024]{2,1,0:T(8,128)(2,1)} %bitcast.17), calls=%async_computation | async-start | bytes 2097152 | tf_op jit(solution)/shard_map/all_to_all | solution.py:63
  160.0 0.0 collective-permute-done.2
  160.0 0.9 add.63
  160.9 1.5 fusion
  162.5 0.5 slice.18
  163.0 0.7 concatenate.7
  163.7 0.1 collective-permute-start.3
  163.8 0.4 fusion.4
  164.1 0.6 collective-permute-start.7
  164.7 0.6 collective-permute-done.3
  165.3 0.7 pad_add_fusion.1
  166.0 0.1 collective-permute-start.4
  166.2 2.1 %collective-permute-start.8 = (f32[64,1024]{1,0:T(8,128)S(1)}, f32[64,1024]{1,0:T(8,128)S(1)}, u32[]{:S(2)}, u32[]{:S(2)}) collective-permute-start(f32[64,1024]{1,0:T(8,128)S(1)} %add.68), channel_id=1, source_target_pairs={{0,32},{8,40},{16,48},{24,56},{32,0},{40,8},{48,16},{56,24},{64,96... | collective-permute-start | bytes 786440 | tf_op jit(solution)/shard_map/ppermute | solution.py:22
  168.2 7.7 %collective-permute-done.4 = f32[1032,64]{0,1:T(8,128)S(1)} collective-permute-done((f32[1032,64]{0,1:T(8,128)S(1)}, f32[1032,64]{0,1:T(8,128)S(1)}, u32[]{:S(2)}, u32[]{:S(2)}) %collective-permute-start.4) | collective-permute-done | bytes 264224 | tf_op jit(solution)/shard_map/ppermute | solution.py:22
  176.0 3.2 %collective-permute-start.5 = (f32[1032,64]{0,1:T(8,128)S(1)}, f32[1032,64]{0,1:T(8,128)S(1)}, u32[]{:S(2)}, u32[]{:S(2)}) collective-permute-start(f32[1032,64]{0,1:T(8,128)S(1)} %add.65), channel_id=1, source_target_pairs={{0,96},{8,104},{16,112},{24,120},{32,64},{40,72},{48,80},{56,88},{... | collective-permute-start | bytes 792584 | tf_op jit(solution)/shard_map/ppermute | solution.py:22
  179.2 1.5 collective-permute-done.8
  180.8 3.2 %collective-permute-start.9 = (f32[64,1024]{1,0:T(8,128)S(1)}, f32[64,1024]{1,0:T(8,128)S(1)}, u32[]{:S(2)}, u32[]{:S(2)}) collective-permute-start(f32[64,1024]{1,0:T(8,128)S(1)} %add.69), channel_id=1, source_target_pairs={{0,96},{8,104},{16,112},{24,120},{32,64},{40,72},{48,80},{56,88},{... | collective-permute-start | bytes 786440 | tf_op jit(solution)/shard_map/ppermute | solution.py:22
  184.0 1.5 collective-permute-done.5
  185.6 1.3 collective-permute-start.6
  186.9 3.6 %collective-permute-done.9 = f32[64,1024]{1,0:T(8,128)S(1)} collective-permute-done((f32[64,1024]{1,0:T(8,128)S(1)}, f32[64,1024]{1,0:T(8,128)S(1)}, u32[]{:S(2)}, u32[]{:S(2)}) %collective-permute-start.9) | collective-permute-done | bytes 262176 | tf_op jit(solution)/shard_map/ppermute | solution.py:22
  190.5 1.3 collective-permute-start.10
  191.8 0.0 all-to-all-done
  191.8 1.1 copy.13
  192.9 5.3 %collective-permute-done.10 = f32[64,1024]{1,0:T(8,128)S(1)} collective-permute-done((f32[64,1024]{1,0:T(8,128)S(1)}, f32[64,1024]{1,0:T(8,128)S(1)}, u32[]{:S(2)}, u32[]{:S(2)}) %collective-permute-start.10) | collective-permute-done | bytes 262176 | tf_op jit(solution)/shard_map/ppermute | solution.py:22
  198.1 0.7 add.71
  198.9 0.7 slice.19
  199.6 0.5 slice.20
  (19 shorter events, 0.3 us)
Async XLA Ops:
  7.2 115.9 %copy-start = (bf16[64,1024]{1,0:T(8,128)(2,1)S(1)}, bf16[64,1024]{1,0:T(8,128)(2,1)}, u32[]{:S(2)}) copy-start(bf16[64,1024]{1,0:T(8,128)(2,1)} %param.11) | copy-start | bytes 393220
  7.2 2.4 %copy-start.1 = (f32[8192]{0:T(1024)S(1)}, f32[8192]{0:T(1024)}, u32[]{:S(2)}) copy-start(f32[8192]{0:T(1024)} %param.13) | copy-start | bytes 98308
  7.2 3.7 %copy-start.2 = (s32[512]{0:T(512)S(1)}, s32[512]{0:T(512)}, u32[]{:S(2)}) copy-start(s32[512]{0:T(512)} %param.12) | copy-start | bytes 6148
  7.2 100.9 %all-gather.3.cloned.1.call-start = ((), (), s32[]{:S(2)}) async-start(), calls=%async_computation.1 | async-start | bytes 17825792 | tf_op jit(solution)/shard_map/all_gather | solution.py:41
  108.1 16.4 %copy-start.3 = (bf16[8192,1024]{1,0:T(8,128)(2,1)S(1)}, bf16[8192,1024]{1,0:T(8,128)(2,1)}, u32[]{:S(2)}) copy-start(bf16[8192,1024]{1,0:T(8,128)(2,1)} %all-gather.3.cloned.1.call-done) | copy-start | bytes 50331652
  138.2 6.4 %collective-permute-start = (f32[520,64]{0,1:T(8,128)S(1)}, f32[520,64]{0,1:T(8,128)S(1)}, u32[]{:S(2)}, u32[]{:S(2)}) collective-permute-start(f32[520,64]{0,1:T(8,128)S(1)} %concatenate.6), channel_id=1, source_target_pairs={{0,2},{1,3},{2,0},{3,1},{4,6},{5,7},{6,4},{7,5},{8,10},{9,11},{10,... | collective-permute-start | bytes 399368 | tf_op jit(solution)/shard_map/ppermute | solution.py:22
  145.3 6.8 %collective-permute-start.1 = (f32[520,64]{0,1:T(8,128)S(1)}, f32[520,64]{0,1:T(8,128)S(1)}, u32[]{:S(2)}, u32[]{:S(2)}) collective-permute-start(f32[520,64]{0,1:T(8,128)S(1)} %pad_add_fusion), channel_id=1, source_target_pairs={{0,6},{1,7},{2,4},{3,5},{4,2},{5,3},{6,0},{7,1},{8,14},{9,15},{10,... | collective-permute-start | bytes 399368 | tf_op jit(solution)/shard_map/ppermute | solution.py:22
  152.1 7.9 %collective-permute-start.2 = (f32[520,64]{0,1:T(8,128)S(1)}, f32[520,64]{0,1:T(8,128)}, u32[]{:S(2)}, u32[]{:S(2)}) collective-permute-start(f32[520,64]{0,1:T(8,128)S(1)} %add.62), channel_id=1, source_target_pairs={{0,1},{1,0},{2,3},{3,2},{4,5},{5,4},{6,7},{7,6},{8,9},{9,8},{10,11... | collective-permute-start | bytes 399368 | tf_op jit(solution)/shard_map/ppermute | solution.py:22
  153.0 38.8 %all-to-all-start = ((bf16[8,64,1024]{2,1,0:T(8,128)(2,1)}), bf16[8,64,1024]{2,1,0:T(8,128)(2,1)S(1)}, u32[]{:S(2)}, u32[]{:S(2)}) async-start(bf16[8,64,1024]{2,1,0:T(8,128)(2,1)} %bitcast.17), calls=%async_computation | async-start | bytes 2097152 | tf_op jit(solution)/shard_map/all_to_all | solution.py:63
  163.7 1.7 collective-permute-start.3
  164.1 2.0 collective-permute-start.7
  166.0 10.0 %collective-permute-start.4 = (f32[1032,64]{0,1:T(8,128)S(1)}, f32[1032,64]{0,1:T(8,128)S(1)}, u32[]{:S(2)}, u32[]{:S(2)}) collective-permute-start(f32[1032,64]{0,1:T(8,128)S(1)} %pad_add_fusion.1), channel_id=1, source_target_pairs={{0,32},{8,40},{16,48},{24,56},{32,0},{40,8},{48,16},{56,24},{64,96... | collective-permute-start | bytes 792584 | tf_op jit(solution)/shard_map/ppermute | solution.py:22
  166.2 14.6 %collective-permute-start.8 = (f32[64,1024]{1,0:T(8,128)S(1)}, f32[64,1024]{1,0:T(8,128)S(1)}, u32[]{:S(2)}, u32[]{:S(2)}) collective-permute-start(f32[64,1024]{1,0:T(8,128)S(1)} %add.68), channel_id=1, source_target_pairs={{0,32},{8,40},{16,48},{24,56},{32,0},{40,8},{48,16},{56,24},{64,96... | collective-permute-start | bytes 786440 | tf_op jit(solution)/shard_map/ppermute | solution.py:22
  176.0 9.6 %collective-permute-start.5 = (f32[1032,64]{0,1:T(8,128)S(1)}, f32[1032,64]{0,1:T(8,128)S(1)}, u32[]{:S(2)}, u32[]{:S(2)}) collective-permute-start(f32[1032,64]{0,1:T(8,128)S(1)} %add.65), channel_id=1, source_target_pairs={{0,96},{8,104},{16,112},{24,120},{32,64},{40,72},{48,80},{56,88},{... | collective-permute-start | bytes 792584 | tf_op jit(solution)/shard_map/ppermute | solution.py:22
  180.8 9.7 %collective-permute-start.9 = (f32[64,1024]{1,0:T(8,128)S(1)}, f32[64,1024]{1,0:T(8,128)S(1)}, u32[]{:S(2)}, u32[]{:S(2)}) collective-permute-start(f32[64,1024]{1,0:T(8,128)S(1)} %add.69), channel_id=1, source_target_pairs={{0,96},{8,104},{16,112},{24,120},{32,64},{40,72},{48,80},{56,88},{... | collective-permute-start | bytes 786440 | tf_op jit(solution)/shard_map/ppermute | solution.py:22
  185.6 13.3 %collective-permute-start.6 = (f32[1032,64]{0,1:T(8,128)S(1)}, f32[1032,64]{0,1:T(8,128)S(1)}, u32[]{:S(2)}, u32[]{:S(2)}) collective-permute-start(f32[1032,64]{0,1:T(8,128)S(1)} %add.66), channel_id=1, source_target_pairs={{0,16},{8,24},{16,0},{24,8},{32,48},{40,56},{48,32},{56,40},{64,80... | collective-permute-start | bytes 792584 | tf_op jit(solution)/shard_map/ppermute | solution.py:22
  190.5 7.6 %collective-permute-start.10 = (f32[64,1024]{1,0:T(8,128)S(1)}, f32[64,1024]{1,0:T(8,128)S(1)}, u32[]{:S(2)}, u32[]{:S(2)}) collective-permute-start(f32[64,1024]{1,0:T(8,128)S(1)} %add.70), channel_id=1, source_target_pairs={{0,16},{8,24},{16,0},{24,8},{32,48},{40,56},{48,32},{56,40},{64,80... | collective-permute-start | bytes 786440 | tf_op jit(solution)/shard_map/ppermute | solution.py:22
Sparse Core Ops, SparseCore 0:
  9.7 98.3 all-gather.2

commit v8 on v7

--- a/solution.py
+++ b/solution.py
@@ -80,12 +80,15 @@
     middle_gradient = packed[:group].astype(jnp.bfloat16)
     loss_mp = packed[group, 0]
 
-    up_part = butterfly_sum(up_grad, "dp")
     down_grad = jnp.dot(my_rows.T, middle_gradient, preferred_element_type=jnp.float32)
-    packed2 = jnp.concatenate([down_grad, jnp.broadcast_to(loss_mp, (8, rank))], axis=0)
+    rows_a = down_grad.shape[0]
+    packed2 = jnp.concatenate(
+        [down_grad, up_grad.reshape(-1, rank), jnp.broadcast_to(loss_mp, (8, rank))], axis=0
+    )
     packed2 = butterfly_sum(packed2, "dp")
-    down_part = packed2[: down_grad.shape[0]]
-    total_loss = packed2[down_grad.shape[0], 0]
+    down_part = packed2[:rows_a]
+    up_part = packed2[rows_a:rows_a + up_grad.size // rank].reshape(up_grad.shape)
+    total_loss = packed2[rows_a + up_grad.size // rank, 0]
     return (h_upd, down_part, up_part, total_loss.reshape(1))
 
 

time: 207 us -> 225 us (1.087)
  waiting for transfers between devices: 61 us -> 83.8 us
  starting transfers between devices: 24.2 us -> 16.7 us
  matrix products: 32.3 us -> 35.7 us
    ppermute x11 -> x7, waiting for transfers between devices: 29.1 us -> 44.3 us  [butterfly_sum(): x = x + lax.ppermute(x, axis, [(i, i ^ mask) for i in range(n)])]
    all_to_all x1, waiting for transfers between devices: 0.01 us -> 7.59 us  [per_device(): lax.all_to_all(updated_output.astype(jnp.bfloat16), 'mp', split_axis=0, c...]
    ppermute x11 -> x7, starting transfers between devices: 17.2 us -> 9.67 us  [butterfly_sum(): x = x + lax.ppermute(x, axis, [(i, i ^ mask) for i in range(n)])]
    dot_general x2, matrix products: 26.8 us -> 30.2 us  [row_adder(): return jnp.dot(source, piece, preferred_element_type=jnp.float32)]
    add x11 -> x7, other arithmetic: 3.22 us -> 0.96 us  [butterfly_sum(): x = x + lax.ppermute(x, axis, [(i, i ^ mask) for i in range(n)])]
  transfers between devices with their start and end apart: 13 -> 9, of which waited for: 9 -> 9; matrix products, arithmetic and copies ran while one was open for 5% -> 2% of each run, Pallas kernels for 0% -> 0%
where the time goes in v8:
time: 225 us
  waiting for transfers between devices  83.8 us (37%)
  blocking collectives  64.6 us (29%)
  matrix products  35.7 us (16%)
  starting transfers between devices  16.7 us (7%)
  between operations  15.6 us (7%)
  local copies, waits for them, and re-layouts  5.57 us (2%)
  other arithmetic  2.94 us (1%)
    ppermute x7, waiting for transfers between devices, butterfly_sum(): x = x + lax.ppermute(x, axis, [(i, i ^ mask) for i in range(n)])  44.3 us
    psum x1, blocking collectives, per_device(): rank_projection = lax.psum(low_part, 'mp').astype(jnp.bfloat16)  43.5 us
    all_gather x1, waiting for transfers between devices, per_device(): gathered = lax.all_gather(weight, 'dp', axis=0, tiled=True)  31.2 us
    dot_general x2, matrix products, row_adder(): return jnp.dot(source, piece, preferred_element_type=jnp.float32)  30.2 us
    all_gather x1, blocking collectives, per_device(): all_flags = lax.all_gather(flags, 'dp', axis=0, tiled=True)  21.1 us
    ppermute x7, starting transfers between devices, butterfly_sum(): x = x + lax.ppermute(x, axis, [(i, i ^ mask) for i in range(n)])  9.67 us
    all_to_all x1, waiting for transfers between devices, per_device(): lax.all_to_all(updated_output.astype(jnp.bfloat16), 'mp', split_axis=0, c...  7.59 us
    all_to_all x1, starting transfers between devices, per_device(): lax.all_to_all(updated_output.astype(jnp.bfloat16), 'mp', split_axis=0, c...  6.97 us
  transfers between devices with their start and end apart: 9, of which 9 were waited for; matrix products, arithmetic and copies ran while one was open for 2% of the time, Pallas kernels for 0%

profile of v8, /device:TPU:4, one launch (start us, length us, event | category | flops | bytes accessed | tf_op | source)
XLA Modules:
  0.0 224.9 jit_solution(8542958998387189120)
XLA Ops:
  7.2 0.0 copy-start
  7.2 0.0 all-gather.3.cloned.1.call-start
  7.2 0.7 all-gather.3.cloned.1.call-update
  7.9 1.7 fusion.2
  9.6 0.6 multiply_reduce_fusion.1
  10.9 21.1 %all-gather = s32[16,1,512]{2,1,0:T(1,128)S(1)} all-gather(s32[1,1,512]{2,1,0:T(1,128)S(1)} %bitcast.18), channel_id=1, replica_groups=mesh['dp'=16,'mp'=8] {'dp'}, dimensions={0}, use_global_device_ids=true | all-gather | bytes 34816 | tf_op jit(solution)/shard_map/all_gather | solution.py:47
  32.0 0.7 reduce_sum.36
  33.4 43.5 %all-reduce.2 = bf16[512,64]{0,1:T(8,128)(2,1)S(1)} all-reduce(f32[512,64]{0,1:T(8,128)S(1)} %fusion.2), channel_id=1, replica_groups=mesh['dp'=16,'mp'=8] {'mp'}, use_global_device_ids=true, to_apply=%region_0.0 | all-reduce | flops 32768 | bytes 196608 | tf_op jit(solution)/shard_map/psum | solution.py:45
  76.9 31.2 %all-gather.3.cloned.1.call-done = bf16[8192,1024]{1,0:T(8,128)(2,1)} async-done(((bf16[512,1024]{1,0:T(8,128)(2,1)}), bf16[8192,1024]{1,0:T(8,128)(2,1)}) %all-gather.3.cloned.1.call-update) | async-done | bytes 16777232 | tf_op jit(solution)/shard_map/all_gather | solution.py:41
  108.1 14.8 %convolution_convert_fusion.1 = bf16[512,1024]{1,0:T(8,128)(2,1)S(1)} fusion(bf16[512,8192]{1,0:T(8,128)(2,1)} %param.8, bf16[8192,1024]{1,0:T(8,128)(2,1)} %all-gather.3.cloned.1.call-done), kind=kOutput, calls=%fused_computation.5 | convolution fusion | flops 8590458880 | bytes 26214400 | tf_op jit(solution)/shard_map/dot_general | solution.py:13
  122.9 0.0 copy-done
  122.9 1.4 fusion.12
  124.4 15.4 %multiply_reduce_fusion = (f32[512]{0:T(512)S(1)}, f32[512,1024]{1,0:T(8,128)S(1)}) fusion(f32[512,1024]{1,0:T(8,128)S(1)} %get-tuple-element.11, bf16[512,8192]{1,0:T(8,128)(2,1)} %param.7, bf16[8192,1024]{1,0:T(8,128)(2,1)} %all-gather.3.cloned.1.call-done, f32[512]{0:T(512)S(1)} %get-tuple-element.9, f32[1024]{0:T(1024)S(1)} %dynamic-slice_multiply_fusion, ...), kind=kOutput, calls=%fused_computation | convolution fusion | flops 8594128896 | bytes 29370368 | tf_op jit(solution)/shard_map/dot_general | solution.py:13
  139.8 0.6 multiply_reduce_fusion.2
  140.4 0.5 fusion.9
  140.9 0.7 concatenate.6
  141.6 1.6 collective-permute-start
  143.2 4.9 %collective-permute-done = f32[520,64]{0,1:T(8,128)S(1)} collective-permute-done((f32[520,64]{0,1:T(8,128)S(1)}, f32[520,64]{0,1:T(8,128)S(1)}, u32[]{:S(2)}, u32[]{:S(2)}) %collective-permute-start) | collective-permute-done | bytes 133152 | tf_op jit(solution)/shard_map/ppermute | solution.py:22
  148.0 0.7 pad_add_fusion
  148.7 2.8 %collective-permute-start.1 = (f32[520,64]{0,1:T(8,128)S(1)}, f32[520,64]{0,1:T(8,128)S(1)}, u32[]{:S(2)}, u32[]{:S(2)}) collective-permute-start(f32[520,64]{0,1:T(8,128)S(1)} %pad_add_fusion), channel_id=1, source_target_pairs={{0,6},{1,7},{2,4},{3,5},{4,2},{5,3},{6,0},{7,1},{8,14},{9,15},{10,... | collective-permute-start | bytes 399368 | tf_op jit(solution)/shard_map/ppermute | solution.py:22
  151.5 3.9 %collective-permute-done.1 = f32[520,64]{0,1:T(8,128)S(1)} collective-permute-done((f32[520,64]{0,1:T(8,128)S(1)}, f32[520,64]{0,1:T(8,128)S(1)}, u32[]{:S(2)}, u32[]{:S(2)}) %collective-permute-start.1) | collective-permute-done | bytes 133152 | tf_op jit(solution)/shard_map/ppermute | solution.py:22
  155.5 0.9 collective-permute-start.2
  156.4 0.4 fusion.4
  156.8 0.1 reshape.31
  156.9 0.2 copy.16
  157.1 5.3 %collective-permute-done.2 = f32[520,64]{0,1:T(8,128)S(1)} collective-permute-done((f32[520,64]{0,1:T(8,128)S(1)}, f32[520,64]{0,1:T(8,128)S(1)}, u32[]{:S(2)}, u32[]{:S(2)}) %collective-permute-start.2) | collective-permute-done | bytes 133152 | tf_op jit(solution)/shard_map/ppermute | solution.py:22
  162.4 1.5 fusion
  164.0 0.5 slice.22
  164.5 0.6 broadcast_in_dim.2
  165.2 0.1 collective-permute-start.3
  165.3 1.9 collective-permute-done.3
  167.2 0.1 fusion.10
  167.3 0.1 collective-permute-start.4
  167.4 14.7 %collective-permute-done.4 = f32[2056,64]{0,1:T(8,128)S(1)} collective-permute-done((f32[2056,64]{0,1:T(8,128)S(1)}, f32[2056,64]{0,1:T(8,128)S(1)}, u32[]{:S(2)}, u32[]{:S(2)}) %collective-permute-start.4) | collective-permute-done | bytes 526368 | tf_op jit(solution)/shard_map/ppermute | solution.py:22
  182.1 0.1 add.51
  182.1 3.2 %collective-permute-start.5 = (f32[2056,64]{0,1:T(8,128)S(1)}, f32[2056,64]{0,1:T(8,128)S(1)}, u32[]{:S(2)}, u32[]{:S(2)}) collective-permute-start(f32[2056,64]{0,1:T(8,128)S(1)} %add.51), channel_id=1, source_target_pairs={{0,96},{8,104},{16,112},{24,120},{32,64},{40,72},{48,80},{56,88},{... | collective-permute-start | bytes 1579016 | tf_op jit(solution)/shard_map/ppermute | solution.py:22
  185.4 7.0 %all-to-all-start = ((bf16[8,64,1024]{2,1,0:T(8,128)(2,1)}), bf16[8,64,1024]{2,1,0:T(8,128)(2,1)S(1)}, u32[]{:S(2)}, u32[]{:S(2)}) async-start(bf16[8,64,1024]{2,1,0:T(8,128)(2,1)} %bitcast), calls=%async_computation | async-start | bytes 2097152 | tf_op jit(solution)/shard_map/all_to_all | solution.py:63
  192.3 5.1 %collective-permute-done.5 = f32[2056,64]{0,1:T(8,128)S(1)} collective-permute-done((f32[2056,64]{0,1:T(8,128)S(1)}, f32[2056,64]{0,1:T(8,128)S(1)}, u32[]{:S(2)}, u32[]{:S(2)}) %collective-permute-start.5) | collective-permute-done | bytes 526368 | tf_op jit(solution)/shard_map/ppermute | solution.py:22
  197.4 0.1 add.52
  197.5 0.9 collective-permute-start.6
  198.4 7.6 %all-to-all-done = bf16[8,64,1024]{2,1,0:T(8,128)(2,1)S(1)} async-done(((bf16[8,64,1024]{2,1,0:T(8,128)(2,1)}), bf16[8,64,1024]{2,1,0:T(8,128)(2,1)S(1)}, u32[]{:S(2)}, u32[]{:S(2)}) %all-to-all-start) | async-done | bytes 1048608 | tf_op jit(solution)/shard_map/all_to_all | solution.py:63
  206.0 1.1 copy.18
  207.1 8.6 %collective-permute-done.6 = f32[2056,64]{0,1:T(8,128)S(1)} collective-permute-done((f32[2056,64]{0,1:T(8,128)S(1)}, f32[2056,64]{0,1:T(8,128)S(1)}, u32[]{:S(2)}, u32[]{:S(2)}) %collective-permute-start.6) | collective-permute-done | bytes 526368 | tf_op jit(solution)/shard_map/ppermute | solution.py:22
  215.7 0.1 add.53
  215.7 0.8 fusion.11
  216.5 0.5 slice.25
  217.0 0.2 copy.17
  217.2 0.9 reshape.32
  (11 shorter events, 0.1 us)
Async XLA Ops:
  7.2 115.8 %copy-start = (bf16[64,1024]{1,0:T(8,128)(2,1)S(1)}, bf16[64,1024]{1,0:T(8,128)(2,1)}, u32[]{:S(2)}) copy-start(bf16[64,1024]{1,0:T(8,128)(2,1)} %param.11) | copy-start | bytes 393220
  7.2 2.4 %copy-start.1 = (f32[8192]{0:T(1024)S(1)}, f32[8192]{0:T(1024)}, u32[]{:S(2)}) copy-start(f32[8192]{0:T(1024)} %param.13) | copy-start | bytes 98308
  7.2 3.7 %copy-start.2 = (s32[512]{0:T(512)S(1)}, s32[512]{0:T(512)}, u32[]{:S(2)}) copy-start(s32[512]{0:T(512)} %param.12) | copy-start | bytes 6148
  7.2 100.9 %all-gather.3.cloned.1.call-start = ((), (), s32[]{:S(2)}) async-start(), calls=%async_computation.1 | async-start | bytes 17825792 | tf_op jit(solution)/shard_map/all_gather | solution.py:41
  141.6 6.4 %collective-permute-start = (f32[520,64]{0,1:T(8,128)S(1)}, f32[520,64]{0,1:T(8,128)S(1)}, u32[]{:S(2)}, u32[]{:S(2)}) collective-permute-start(f32[520,64]{0,1:T(8,128)S(1)} %concatenate.6), channel_id=1, source_target_pairs={{0,2},{1,3},{2,0},{3,1},{4,6},{5,7},{6,4},{7,5},{8,10},{9,11},{10,... | collective-permute-start | bytes 399368 | tf_op jit(solution)/shard_map/ppermute | solution.py:22
  148.7 6.8 %collective-permute-start.1 = (f32[520,64]{0,1:T(8,128)S(1)}, f32[520,64]{0,1:T(8,128)S(1)}, u32[]{:S(2)}, u32[]{:S(2)}) collective-permute-start(f32[520,64]{0,1:T(8,128)S(1)} %pad_add_fusion), channel_id=1, source_target_pairs={{0,6},{1,7},{2,4},{3,5},{4,2},{5,3},{6,0},{7,1},{8,14},{9,15},{10,... | collective-permute-start | bytes 399368 | tf_op jit(solution)/shard_map/ppermute | solution.py:22
  155.5 6.9 %collective-permute-start.2 = (f32[520,64]{0,1:T(8,128)S(1)}, f32[520,64]{0,1:T(8,128)S(1)}, u32[]{:S(2)}, u32[]{:S(2)}) collective-permute-start(f32[520,64]{0,1:T(8,128)S(1)} %add.48), channel_id=1, source_target_pairs={{0,1},{1,0},{2,3},{3,2},{4,5},{5,4},{6,7},{7,6},{8,9},{9,8},{10,11... | collective-permute-start | bytes 399368 | tf_op jit(solution)/shard_map/ppermute | solution.py:22
  165.2 2.0 collective-permute-start.3
  167.3 14.7 %collective-permute-start.4 = (f32[2056,64]{0,1:T(8,128)S(1)}, f32[2056,64]{0,1:T(8,128)S(1)}, u32[]{:S(2)}, u32[]{:S(2)}) collective-permute-start(f32[2056,64]{0,1:T(8,128)S(1)} %fusion.10), channel_id=1, source_target_pairs={{0,32},{8,40},{16,48},{24,56},{32,0},{40,8},{48,16},{56,24},{64,96... | collective-permute-start | bytes 1579016 | tf_op jit(solution)/shard_map/ppermute | solution.py:22
  182.1 15.3 %collective-permute-start.5 = (f32[2056,64]{0,1:T(8,128)S(1)}, f32[2056,64]{0,1:T(8,128)S(1)}, u32[]{:S(2)}, u32[]{:S(2)}) collective-permute-start(f32[2056,64]{0,1:T(8,128)S(1)} %add.51), channel_id=1, source_target_pairs={{0,96},{8,104},{16,112},{24,120},{32,64},{40,72},{48,80},{56,88},{... | collective-permute-start | bytes 1579016 | tf_op jit(solution)/shard_map/ppermute | solution.py:22
  185.4 20.7 %all-to-all-start = ((bf16[8,64,1024]{2,1,0:T(8,128)(2,1)}), bf16[8,64,1024]{2,1,0:T(8,128)(2,1)S(1)}, u32[]{:S(2)}, u32[]{:S(2)}) async-start(bf16[8,64,1024]{2,1,0:T(8,128)(2,1)} %bitcast), calls=%async_computation | async-start | bytes 2097152 | tf_op jit(solution)/shard_map/all_to_all | solution.py:63
  197.5 18.2 %collective-permute-start.6 = (f32[2056,64]{0,1:T(8,128)S(1)}, f32[2056,64]{0,1:T(8,128)S(1)}, u32[]{:S(2)}, u32[]{:S(2)}) collective-permute-start(f32[2056,64]{0,1:T(8,128)S(1)} %add.52), channel_id=1, source_target_pairs={{0,16},{8,24},{16,0},{24,8},{32,48},{40,56},{48,32},{56,40},{64,80... | collective-permute-start | bytes 1579016 | tf_op jit(solution)/shard_map/ppermute | solution.py:22
Sparse Core Ops, SparseCore 0:
  9.7 98.3 all-gather.2

commit v9 on v7

--- a/solution.py
+++ b/solution.py
@@ -13,7 +13,7 @@
     return jnp.dot(source, piece, preferred_element_type=jnp.float32)
 
 
-MASKS = {"dp": (1, 4, 12, 2), "mp": (2, 6, 1)}
+MASKS = {"dp": (1, 4, 12, 2), "mp": (1, 2, 6)}
 
 
 def butterfly_sum(x, axis):

time: 207 us -> 208 us (level)
  waiting for transfers between devices: 61 us -> 63.8 us
  starting transfers between devices: 24.2 us -> 21.6 us
    ppermute x11, waiting for transfers between devices: 29.1 us -> 31.9 us  [butterfly_sum(): x = x + lax.ppermute(x, axis, [(i, i ^ mask) for i in range(n)])]
where the time goes in v9:
time: 208 us; the launch traced here: 207 us
  blocking collectives  64.6 us (31%)
  waiting for transfers between devices  63.8 us (31%)
  matrix products  32.3 us (16%)
  starting transfers between devices  21.6 us (10%)
  between operations  15.6 us (8%)
  other arithmetic  5.16 us (2%)
  local copies, waits for them, and re-layouts  4.16 us (2%)
    psum x1, blocking collectives, per_device(): rank_projection = lax.psum(low_part, 'mp').astype(jnp.bfloat16)  43.5 us
    ppermute x11, waiting for transfers between devices, butterfly_sum(): x = x + lax.ppermute(x, axis, [(i, i ^ mask) for i in range(n)])  31.9 us
    all_gather x1, waiting for transfers between devices, per_device(): gathered = lax.all_gather(weight, 'dp', axis=0, tiled=True)  31.2 us
    dot_general x2, matrix products, row_adder(): return jnp.dot(source, piece, preferred_element_type=jnp.float32)  26.8 us
    all_gather x1, blocking collectives, per_device(): all_flags = lax.all_gather(flags, 'dp', axis=0, tiled=True)  21.1 us
    ppermute x11, starting transfers between devices, butterfly_sum(): x = x + lax.ppermute(x, axis, [(i, i ^ mask) for i in range(n)])  16.6 us
    all_to_all x1, starting transfers between devices, per_device(): lax.all_to_all(updated_output.astype(jnp.bfloat16), 'mp', split_axis=0, c...  5.03 us
  transfers between devices with their start and end apart: 13, of which 9 were waited for; matrix products, arithmetic and copies ran while one was open for 5% of the time, Pallas kernels for 0%

profile of v9, /device:TPU:4, one launch (start us, length us, event | category | flops | bytes accessed | tf_op | source)
XLA Modules:
  0.0 207.2 jit_solution(1615080196540938321)
XLA Ops:
  7.2 0.0 copy-start
  7.2 0.0 all-gather.3.cloned.1.call-start
  7.2 0.7 all-gather.3.cloned.1.call-update
  7.9 1.7 fusion.2
  9.6 0.6 multiply_reduce_fusion.1
  10.9 21.1 %all-gather = s32[16,1,512]{2,1,0:T(1,128)S(1)} all-gather(s32[1,1,512]{2,1,0:T(1,128)S(1)} %bitcast.19), channel_id=1, replica_groups=mesh['dp'=16,'mp'=8] {'dp'}, dimensions={0}, use_global_device_ids=true | all-gather | bytes 34816 | tf_op jit(solution)/shard_map/all_gather | solution.py:47
  32.0 0.7 reduce_sum.36
  33.4 43.5 %all-reduce.3 = bf16[512,64]{0,1:T(8,128)(2,1)S(1)} all-reduce(f32[512,64]{0,1:T(8,128)S(1)} %fusion.2), channel_id=1, replica_groups=mesh['dp'=16,'mp'=8] {'mp'}, use_global_device_ids=true, to_apply=%region_0.0 | all-reduce | flops 32768 | bytes 196608 | tf_op jit(solution)/shard_map/psum | solution.py:45
  76.9 31.2 %all-gather.3.cloned.1.call-done = bf16[8192,1024]{1,0:T(8,128)(2,1)} async-done(((bf16[512,1024]{1,0:T(8,128)(2,1)}), bf16[8192,1024]{1,0:T(8,128)(2,1)}) %all-gather.3.cloned.1.call-update) | async-done | bytes 16777232 | tf_op jit(solution)/shard_map/all_gather | solution.py:41
  108.1 14.9 %convolution_convert_fusion.1 = bf16[512,1024]{1,0:T(8,128)(2,1)S(1)} fusion(bf16[512,8192]{1,0:T(8,128)(2,1)} %param.8, bf16[8192,1024]{1,0:T(8,128)(2,1)} %all-gather.3.cloned.1.call-done), kind=kOutput, calls=%fused_computation.5 | convolution fusion | flops 8590458880 | bytes 26214400 | tf_op jit(solution)/shard_map/dot_general | solution.py:13
  123.1 1.4 fusion.10
  124.5 11.9 %multiply_reduce_fusion = (f32[512]{0:T(512)S(1)}, f32[512,1024]{1,0:T(8,128)S(1)}) fusion(f32[512,1024]{1,0:T(8,128)S(1)} %get-tuple-element.9, bf16[512,8192]{1,0:T(8,128)(2,1)} %param.7, bf16[8192,1024]{1,0:T(8,128)(2,1)S(1)} %copy-done.3, f32[512]{0:T(512)S(1)} %get-tuple-element.7, f32[1024]{0:T(1024)S(1)} %dynamic-slice_multiply_fusion, ...), kind=kOutput, calls=%fused_computation | convolution fusion | flops 8594128896 | bytes 29370368 | tf_op jit(solution)/shard_map/dot_general | solution.py:13
  136.4 0.6 multiply_reduce_fusion.2
  137.0 0.5 fusion.9
  137.5 0.7 concatenate.6
  138.2 0.9 collective-permute-start
  139.1 7.0 %collective-permute-done = f32[520,64]{0,1:T(8,128)S(1)} collective-permute-done((f32[520,64]{0,1:T(8,128)S(1)}, f32[520,64]{0,1:T(8,128)S(1)}, u32[]{:S(2)}, u32[]{:S(2)}) %collective-permute-start) | collective-permute-done | bytes 133152 | tf_op jit(solution)/shard_map/ppermute | solution.py:22
  146.1 0.7 pad_add_fusion
  146.8 1.6 collective-permute-start.1
  148.4 4.0 %collective-permute-done.1 = f32[520,64]{0,1:T(8,128)S(1)} collective-permute-done((f32[520,64]{0,1:T(8,128)S(1)}, f32[520,64]{0,1:T(8,128)S(1)}, u32[]{:S(2)}, u32[]{:S(2)}) %collective-permute-start.1) | collective-permute-done | bytes 133152 | tf_op jit(solution)/shard_map/ppermute | solution.py:22
  152.4 2.8 %collective-permute-start.2 = (f32[520,64]{0,1:T(8,128)S(1)}, f32[520,64]{0,1:T(8,128)}, u32[]{:S(2)}, u32[]{:S(2)}) collective-permute-start(f32[520,64]{0,1:T(8,128)S(1)} %add.62), channel_id=1, source_target_pairs={{0,6},{1,7},{2,4},{3,5},{4,2},{5,3},{6,0},{7,1},{8,14},{9,15},{10,... | collective-permute-start | bytes 399368 | tf_op jit(solution)/shard_map/ppermute | solution.py:22
  155.2 5.0 %all-to-all-start = ((bf16[8,64,1024]{2,1,0:T(8,128)(2,1)}), bf16[8,64,1024]{2,1,0:T(8,128)(2,1)S(1)}, u32[]{:S(2)}, u32[]{:S(2)}) async-start(bf16[8,64,1024]{2,1,0:T(8,128)(2,1)} %bitcast.17), calls=%async_computation | async-start | bytes 2097152 | tf_op jit(solution)/shard_map/all_to_all | solution.py:63
  160.2 0.0 collective-permute-done.2
  160.3 0.9 add.63
  161.2 1.5 fusion
  162.7 0.5 slice.18
  163.2 0.7 concatenate.7
  163.9 0.1 collective-permute-start.3
  164.0 0.4 fusion.4
  164.4 0.6 collective-permute-start.7
  165.0 0.6 collective-permute-done.3
  165.6 0.7 pad_add_fusion.1
  166.3 0.1 collective-permute-start.4
  166.4 2.1 %collective-permute-start.8 = (f32[64,1024]{1,0:T(8,128)S(1)}, f32[64,1024]{1,0:T(8,128)S(1)}, u32[]{:S(2)}, u32[]{:S(2)}) collective-permute-start(f32[64,1024]{1,0:T(8,128)S(1)} %add.68), channel_id=1, source_target_pairs={{0,32},{8,40},{16,48},{24,56},{32,0},{40,8},{48,16},{56,24},{64,96... | collective-permute-start | bytes 786440 | tf_op jit(solution)/shard_map/ppermute | solution.py:22
  168.5 7.7 %collective-permute-done.4 = f32[1032,64]{0,1:T(8,128)S(1)} collective-permute-done((f32[1032,64]{0,1:T(8,128)S(1)}, f32[1032,64]{0,1:T(8,128)S(1)}, u32[]{:S(2)}, u32[]{:S(2)}) %collective-permute-start.4) | collective-permute-done | bytes 264224 | tf_op jit(solution)/shard_map/ppermute | solution.py:22
  176.3 3.2 %collective-permute-start.5 = (f32[1032,64]{0,1:T(8,128)S(1)}, f32[1032,64]{0,1:T(8,128)S(1)}, u32[]{:S(2)}, u32[]{:S(2)}) collective-permute-start(f32[1032,64]{0,1:T(8,128)S(1)} %add.65), channel_id=1, source_target_pairs={{0,96},{8,104},{16,112},{24,120},{32,64},{40,72},{48,80},{56,88},{... | collective-permute-start | bytes 792584 | tf_op jit(solution)/shard_map/ppermute | solution.py:22
  179.5 1.5 collective-permute-done.8
  181.0 3.2 %collective-permute-start.9 = (f32[64,1024]{1,0:T(8,128)S(1)}, f32[64,1024]{1,0:T(8,128)S(1)}, u32[]{:S(2)}, u32[]{:S(2)}) collective-permute-start(f32[64,1024]{1,0:T(8,128)S(1)} %add.69), channel_id=1, source_target_pairs={{0,96},{8,104},{16,112},{24,120},{32,64},{40,72},{48,80},{56,88},{... | collective-permute-start | bytes 786440 | tf_op jit(solution)/shard_map/ppermute | solution.py:22
  184.3 1.5 collective-permute-done.5
  185.8 1.0 collective-permute-start.6
  186.8 3.9 %collective-permute-done.9 = f32[64,1024]{1,0:T(8,128)S(1)} collective-permute-done((f32[64,1024]{1,0:T(8,128)S(1)}, f32[64,1024]{1,0:T(8,128)S(1)}, u32[]{:S(2)}, u32[]{:S(2)}) %collective-permute-start.9) | collective-permute-done | bytes 262176 | tf_op jit(solution)/shard_map/ppermute | solution.py:22
  190.8 1.0 collective-permute-start.10
  191.7 1.1 copy.13
  192.8 5.6 %collective-permute-done.10 = f32[64,1024]{1,0:T(8,128)S(1)} collective-permute-done((f32[64,1024]{1,0:T(8,128)S(1)}, f32[64,1024]{1,0:T(8,128)S(1)}, u32[]{:S(2)}, u32[]{:S(2)}) %collective-permute-start.10) | collective-permute-done | bytes 262176 | tf_op jit(solution)/shard_map/ppermute | solution.py:22
  198.4 0.7 add.71
  199.1 0.0 collective-permute-done.6
  199.1 0.7 slice.19
  199.9 0.5 slice.20
  (19 shorter events, 0.3 us)
Async XLA Ops:
  7.2 115.9 %copy-start = (bf16[64,1024]{1,0:T(8,128)(2,1)S(1)}, bf16[64,1024]{1,0:T(8,128)(2,1)}, u32[]{:S(2)}) copy-start(bf16[64,1024]{1,0:T(8,128)(2,1)} %param.11) | copy-start | bytes 393220
  7.2 2.4 %copy-start.1 = (f32[8192]{0:T(1024)S(1)}, f32[8192]{0:T(1024)}, u32[]{:S(2)}) copy-start(f32[8192]{0:T(1024)} %param.13) | copy-start | bytes 98308
  7.2 3.7 %copy-start.2 = (s32[512]{0:T(512)S(1)}, s32[512]{0:T(512)}, u32[]{:S(2)}) copy-start(s32[512]{0:T(512)} %param.12) | copy-start | bytes 6148
  7.2 100.9 %all-gather.3.cloned.1.call-start = ((), (), s32[]{:S(2)}) async-start(), calls=%async_computation.1 | async-start | bytes 17825792 | tf_op jit(solution)/shard_map/all_gather | solution.py:41
  108.1 16.4 %copy-start.3 = (bf16[8192,1024]{1,0:T(8,128)(2,1)S(1)}, bf16[8192,1024]{1,0:T(8,128)(2,1)}, u32[]{:S(2)}) copy-start(bf16[8192,1024]{1,0:T(8,128)(2,1)} %all-gather.3.cloned.1.call-done) | copy-start | bytes 50331652
  138.2 7.9 %collective-permute-start = (f32[520,64]{0,1:T(8,128)S(1)}, f32[520,64]{0,1:T(8,128)S(1)}, u32[]{:S(2)}, u32[]{:S(2)}) collective-permute-start(f32[520,64]{0,1:T(8,128)S(1)} %concatenate.6), channel_id=1, source_target_pairs={{0,1},{1,0},{2,3},{3,2},{4,5},{5,4},{6,7},{7,6},{8,9},{9,8},{10,11... | collective-permute-start | bytes 399368 | tf_op jit(solution)/shard_map/ppermute | solution.py:22
  146.8 5.6 %collective-permute-start.1 = (f32[520,64]{0,1:T(8,128)S(1)}, f32[520,64]{0,1:T(8,128)S(1)}, u32[]{:S(2)}, u32[]{:S(2)}) collective-permute-start(f32[520,64]{0,1:T(8,128)S(1)} %pad_add_fusion), channel_id=1, source_target_pairs={{0,2},{1,3},{2,0},{3,1},{4,6},{5,7},{6,4},{7,5},{8,10},{9,11},{10,... | collective-permute-start | bytes 399368 | tf_op jit(solution)/shard_map/ppermute | solution.py:22
  152.4 7.9 %collective-permute-start.2 = (f32[520,64]{0,1:T(8,128)S(1)}, f32[520,64]{0,1:T(8,128)}, u32[]{:S(2)}, u32[]{:S(2)}) collective-permute-start(f32[520,64]{0,1:T(8,128)S(1)} %add.62), channel_id=1, source_target_pairs={{0,6},{1,7},{2,4},{3,5},{4,2},{5,3},{6,0},{7,1},{8,14},{9,15},{10,... | collective-permute-start | bytes 399368 | tf_op jit(solution)/shard_map/ppermute | solution.py:22
  155.2 36.5 %all-to-all-start = ((bf16[8,64,1024]{2,1,0:T(8,128)(2,1)}), bf16[8,64,1024]{2,1,0:T(8,128)(2,1)S(1)}, u32[]{:S(2)}, u32[]{:S(2)}) async-start(bf16[8,64,1024]{2,1,0:T(8,128)(2,1)} %bitcast.17), calls=%async_computation | async-start | bytes 2097152 | tf_op jit(solution)/shard_map/all_to_all | solution.py:63
  163.9 1.7 collective-permute-start.3
  164.4 2.0 collective-permute-start.7
  166.3 10.0 %collective-permute-start.4 = (f32[1032,64]{0,1:T(8,128)S(1)}, f32[1032,64]{0,1:T(8,128)S(1)}, u32[]{:S(2)}, u32[]{:S(2)}) collective-permute-start(f32[1032,64]{0,1:T(8,128)S(1)} %pad_add_fusion.1), channel_id=1, source_target_pairs={{0,32},{8,40},{16,48},{24,56},{32,0},{40,8},{48,16},{56,24},{64,96... | collective-permute-start | bytes 792584 | tf_op jit(solution)/shard_map/ppermute | solution.py:22
  166.4 14.6 %collective-permute-start.8 = (f32[64,1024]{1,0:T(8,128)S(1)}, f32[64,1024]{1,0:T(8,128)S(1)}, u32[]{:S(2)}, u32[]{:S(2)}) collective-permute-start(f32[64,1024]{1,0:T(8,128)S(1)} %add.68), channel_id=1, source_target_pairs={{0,32},{8,40},{16,48},{24,56},{32,0},{40,8},{48,16},{56,24},{64,96... | collective-permute-start | bytes 786440 | tf_op jit(solution)/shard_map/ppermute | solution.py:22
  176.3 9.6 %collective-permute-start.5 = (f32[1032,64]{0,1:T(8,128)S(1)}, f32[1032,64]{0,1:T(8,128)S(1)}, u32[]{:S(2)}, u32[]{:S(2)}) collective-permute-start(f32[1032,64]{0,1:T(8,128)S(1)} %add.65), channel_id=1, source_target_pairs={{0,96},{8,104},{16,112},{24,120},{32,64},{40,72},{48,80},{56,88},{... | collective-permute-start | bytes 792584 | tf_op jit(solution)/shard_map/ppermute | solution.py:22
  181.0 9.7 %collective-permute-start.9 = (f32[64,1024]{1,0:T(8,128)S(1)}, f32[64,1024]{1,0:T(8,128)S(1)}, u32[]{:S(2)}, u32[]{:S(2)}) collective-permute-start(f32[64,1024]{1,0:T(8,128)S(1)} %add.69), channel_id=1, source_target_pairs={{0,96},{8,104},{16,112},{24,120},{32,64},{40,72},{48,80},{56,88},{... | collective-permute-start | bytes 786440 | tf_op jit(solution)/shard_map/ppermute | solution.py:22
  185.8 13.3 %collective-permute-start.6 = (f32[1032,64]{0,1:T(8,128)S(1)}, f32[1032,64]{0,1:T(8,128)S(1)}, u32[]{:S(2)}, u32[]{:S(2)}) collective-permute-start(f32[1032,64]{0,1:T(8,128)S(1)} %add.66), channel_id=1, source_target_pairs={{0,16},{8,24},{16,0},{24,8},{32,48},{40,56},{48,32},{56,40},{64,80... | collective-permute-start | bytes 792584 | tf_op jit(solution)/shard_map/ppermute | solution.py:22
  190.8 7.6 %collective-permute-start.10 = (f32[64,1024]{1,0:T(8,128)S(1)}, f32[64,1024]{1,0:T(8,128)S(1)}, u32[]{:S(2)}, u32[]{:S(2)}) collective-permute-start(f32[64,1024]{1,0:T(8,128)S(1)} %add.70), channel_id=1, source_target_pairs={{0,16},{8,24},{16,0},{24,8},{32,48},{40,56},{48,32},{56,40},{64,80... | collective-permute-start | bytes 786440 | tf_op jit(solution)/shard_map/ppermute | solution.py:22
Sparse Core Ops, SparseCore 0:
  9.7 98.3 all-gather.2

commit v10 on v7

--- a/solution.py
+++ b/solution.py
@@ -16,9 +16,9 @@
 MASKS = {"dp": (1, 4, 12, 2), "mp": (2, 6, 1)}
 
 
-def butterfly_sum(x, axis):
+def butterfly_sum(x, axis, masks=None):
     n = lax.axis_size(axis)
-    for mask in MASKS[axis]:
+    for mask in masks or MASKS[axis]:
         x = x + lax.ppermute(x, axis, [(i, i ^ mask) for i in range(n)])
     return x
 
@@ -80,7 +80,7 @@
     middle_gradient = packed[:group].astype(jnp.bfloat16)
     loss_mp = packed[group, 0]
 
-    up_part = butterfly_sum(up_grad, "dp")
+    up_part = butterfly_sum(up_grad, "dp", (2, 12, 4, 1))
     down_grad = jnp.dot(my_rows.T, middle_gradient, preferred_element_type=jnp.float32)
     packed2 = jnp.concatenate([down_grad, jnp.broadcast_to(loss_mp, (8, rank))], axis=0)
     packed2 = butterfly_sum(packed2, "dp")

time: 207 us -> 205 us (level)
  starting transfers between devices: 24.2 us -> 18.4 us
  waiting for transfers between devices: 61 us -> 64.7 us
    ppermute x11, starting transfers between devices: 17.2 us -> 11.4 us  [butterfly_sum(): x = x + lax.ppermute(x, axis, [(i, i ^ mask) for i in range(n)])]
    ppermute x11, waiting for transfers between devices: 29.1 us -> 32.8 us  [butterfly_sum(): x = x + lax.ppermute(x, axis, [(i, i ^ mask) for i in range(n)])]
where the time goes in v10:
time: 205 us
  waiting for transfers between devices  64.7 us (32%)
  blocking collectives  64.6 us (32%)
  matrix products  32.3 us (16%)
  starting transfers between devices  18.4 us (9%)
  between operations  15.6 us (8%)
  other arithmetic  5.16 us (3%)
  local copies, waits for them, and re-layouts  4.16 us (2%)
    psum x1, blocking collectives, per_device(): rank_projection = lax.psum(low_part, 'mp').astype(jnp.bfloat16)  43.5 us
    ppermute x11, waiting for transfers between devices, butterfly_sum(): x = x + lax.ppermute(x, axis, [(i, i ^ mask) for i in range(n)])  32.8 us
    all_gather x1, waiting for transfers between devices, per_device(): gathered = lax.all_gather(weight, 'dp', axis=0, tiled=True)  31.2 us
    dot_general x2, matrix products, row_adder(): return jnp.dot(source, piece, preferred_element_type=jnp.float32)  26.8 us
    all_gather x1, blocking collectives, per_device(): all_flags = lax.all_gather(flags, 'dp', axis=0, tiled=True)  21.1 us
    ppermute x11, starting transfers between devices, butterfly_sum(): x = x + lax.ppermute(x, axis, [(i, i ^ mask) for i in range(n)])  11.4 us
    all_to_all x1, starting transfers between devices, per_device(): lax.all_to_all(updated_output.astype(jnp.bfloat16), 'mp', split_axis=0, c...  6.97 us
  transfers between devices with their start and end apart: 13, of which 9 were waited for; matrix products, arithmetic and copies ran while one was open for 5% of the time, Pallas kernels for 0%

profile of v10, /device:TPU:4, one launch (start us, length us, event | category | flops | bytes accessed | tf_op | source)
XLA Modules:
  0.0 204.9 jit_solution(5114002227824492488)
XLA Ops:
  7.2 0.0 copy-start
  7.2 0.0 all-gather.3.cloned.1.call-start
  7.2 0.7 all-gather.3.cloned.1.call-update
  7.9 1.7 fusion.2
  9.6 0.6 multiply_reduce_fusion.1
  10.9 21.1 %all-gather = s32[16,1,512]{2,1,0:T(1,128)S(1)} all-gather(s32[1,1,512]{2,1,0:T(1,128)S(1)} %bitcast.19), channel_id=1, replica_groups=mesh['dp'=16,'mp'=8] {'dp'}, dimensions={0}, use_global_device_ids=true | all-gather | bytes 34816 | tf_op jit(solution)/shard_map/all_gather | solution.py:47
  32.0 0.7 reduce_sum.36
  33.4 43.5 %all-reduce.3 = bf16[512,64]{0,1:T(8,128)(2,1)S(1)} all-reduce(f32[512,64]{0,1:T(8,128)S(1)} %fusion.2), channel_id=1, replica_groups=mesh['dp'=16,'mp'=8] {'mp'}, use_global_device_ids=true, to_apply=%region_0.0 | all-reduce | flops 32768 | bytes 196608 | tf_op jit(solution)/shard_map/psum | solution.py:45
  76.9 31.2 %all-gather.3.cloned.1.call-done = bf16[8192,1024]{1,0:T(8,128)(2,1)} async-done(((bf16[512,1024]{1,0:T(8,128)(2,1)}), bf16[8192,1024]{1,0:T(8,128)(2,1)}) %all-gather.3.cloned.1.call-update) | async-done | bytes 16777232 | tf_op jit(solution)/shard_map/all_gather | solution.py:41
  108.1 14.9 %convolution_convert_fusion.1 = bf16[512,1024]{1,0:T(8,128)(2,1)S(1)} fusion(bf16[512,8192]{1,0:T(8,128)(2,1)} %param.8, bf16[8192,1024]{1,0:T(8,128)(2,1)} %all-gather.3.cloned.1.call-done), kind=kOutput, calls=%fused_computation.5 | convolution fusion | flops 8590458880 | bytes 26214400 | tf_op jit(solution)/shard_map/dot_general | solution.py:13
  123.1 1.4 fusion.10
  124.5 11.9 %multiply_reduce_fusion = (f32[512]{0:T(512)S(1)}, f32[512,1024]{1,0:T(8,128)S(1)}) fusion(f32[512,1024]{1,0:T(8,128)S(1)} %get-tuple-element.9, bf16[512,8192]{1,0:T(8,128)(2,1)} %param.7, bf16[8192,1024]{1,0:T(8,128)(2,1)S(1)} %copy-done.3, f32[512]{0:T(512)S(1)} %get-tuple-element.7, f32[1024]{0:T(1024)S(1)} %dynamic-slice_multiply_fusion, ...), kind=kOutput, calls=%fused_computation | convolution fusion | flops 8594128896 | bytes 29370368 | tf_op jit(solution)/shard_map/dot_general | solution.py:13
  136.4 0.6 multiply_reduce_fusion.2
  137.0 0.5 fusion.9
  137.5 0.7 concatenate.6
  138.2 1.6 collective-permute-start
  139.8 4.9 %collective-permute-done = f32[520,64]{0,1:T(8,128)S(1)} collective-permute-done((f32[520,64]{0,1:T(8,128)S(1)}, f32[520,64]{0,1:T(8,128)S(1)}, u32[]{:S(2)}, u32[]{:S(2)}) %collective-permute-start) | collective-permute-done | bytes 133152 | tf_op jit(solution)/shard_map/ppermute | solution.py:22
  144.6 0.7 pad_add_fusion
  145.3 2.8 %collective-permute-start.1 = (f32[520,64]{0,1:T(8,128)S(1)}, f32[520,64]{0,1:T(8,128)S(1)}, u32[]{:S(2)}, u32[]{:S(2)}) collective-permute-start(f32[520,64]{0,1:T(8,128)S(1)} %pad_add_fusion), channel_id=1, source_target_pairs={{0,6},{1,7},{2,4},{3,5},{4,2},{5,3},{6,0},{7,1},{8,14},{9,15},{10,... | collective-permute-start | bytes 399368 | tf_op jit(solution)/shard_map/ppermute | solution.py:22
  148.1 4.0 %collective-permute-done.1 = f32[520,64]{0,1:T(8,128)S(1)} collective-permute-done((f32[520,64]{0,1:T(8,128)S(1)}, f32[520,64]{0,1:T(8,128)S(1)}, u32[]{:S(2)}, u32[]{:S(2)}) %collective-permute-start.1) | collective-permute-done | bytes 133152 | tf_op jit(solution)/shard_map/ppermute | solution.py:22
  152.1 0.9 collective-permute-start.2
  153.0 7.0 %all-to-all-start = ((bf16[8,64,1024]{2,1,0:T(8,128)(2,1)}), bf16[8,64,1024]{2,1,0:T(8,128)(2,1)S(1)}, u32[]{:S(2)}, u32[]{:S(2)}) async-start(bf16[8,64,1024]{2,1,0:T(8,128)(2,1)} %bitcast.17), calls=%async_computation | async-start | bytes 2097152 | tf_op jit(solution)/shard_map/all_to_all | solution.py:63
  160.0 0.0 collective-permute-done.2
  160.0 0.9 add.63
  160.9 1.5 fusion
  162.5 0.5 slice.18
  163.0 0.7 concatenate.7
  163.7 0.1 collective-permute-start.3
  163.8 0.4 fusion.4
  164.1 1.5 collective-permute-start.7
  165.6 0.0 collective-permute-done.3
  165.6 0.7 pad_add_fusion.1
  166.3 0.1 collective-permute-start.4
  166.4 10.6 %collective-permute-done.7 = f32[64,1024]{1,0:T(8,128)S(1)} collective-permute-done((f32[64,1024]{1,0:T(8,128)S(1)}, f32[64,1024]{1,0:T(8,128)S(1)}, u32[]{:S(2)}, u32[]{:S(2)}) %collective-permute-start.7) | collective-permute-done | bytes 262176 | tf_op jit(solution)/shard_map/ppermute | solution.py:22
  177.0 2.8 %collective-permute-start.8 = (f32[64,1024]{1,0:T(8,128)S(1)}, f32[64,1024]{1,0:T(8,128)S(1)}, u32[]{:S(2)}, u32[]{:S(2)}) collective-permute-start(f32[64,1024]{1,0:T(8,128)S(1)} %add.68), channel_id=1, source_target_pairs={{0,96},{8,104},{16,112},{24,120},{32,64},{40,72},{48,80},{56,88},{... | collective-permute-start | bytes 786440 | tf_op jit(solution)/shard_map/ppermute | solution.py:22
  179.9 0.6 collective-permute-start.5
  180.5 6.3 %collective-permute-done.8 = f32[64,1024]{1,0:T(8,128)S(1)} collective-permute-done((f32[64,1024]{1,0:T(8,128)S(1)}, f32[64,1024]{1,0:T(8,128)S(1)}, u32[]{:S(2)}, u32[]{:S(2)}) %collective-permute-start.8) | collective-permute-done | bytes 262176 | tf_op jit(solution)/shard_map/ppermute | solution.py:22
  186.9 0.1 collective-permute-start.9
  186.9 3.0 %collective-permute-done.5 = f32[1032,64]{0,1:T(8,128)S(1)} collective-permute-done((f32[1032,64]{0,1:T(8,128)S(1)}, f32[1032,64]{0,1:T(8,128)S(1)}, u32[]{:S(2)}, u32[]{:S(2)}) %collective-permute-start.5) | collective-permute-done | bytes 264224 | tf_op jit(solution)/shard_map/ppermute | solution.py:22
  190.0 0.9 collective-permute-start.6
  190.9 2.4 %collective-permute-done.9 = f32[64,1024]{1,0:T(8,128)S(1)} collective-permute-done((f32[64,1024]{1,0:T(8,128)S(1)}, f32[64,1024]{1,0:T(8,128)S(1)}, u32[]{:S(2)}, u32[]{:S(2)}) %collective-permute-start.9) | collective-permute-done | bytes 262176 | tf_op jit(solution)/shard_map/ppermute | solution.py:22
  193.3 0.1 collective-permute-start.10
  193.4 1.1 copy.13
  194.5 0.5 collective-permute-done.10
  195.0 0.7 add.71
  195.7 1.1 collective-permute-done.6
  196.9 0.7 slice.19
  197.6 0.5 slice.20
  (19 shorter events, 0.3 us)
Async XLA Ops:
  7.2 115.9 %copy-start = (bf16[64,1024]{1,0:T(8,128)(2,1)S(1)}, bf16[64,1024]{1,0:T(8,128)(2,1)}, u32[]{:S(2)}) copy-start(bf16[64,1024]{1,0:T(8,128)(2,1)} %param.11) | copy-start | bytes 393220
  7.2 2.4 %copy-start.1 = (f32[8192]{0:T(1024)S(1)}, f32[8192]{0:T(1024)}, u32[]{:S(2)}) copy-start(f32[8192]{0:T(1024)} %param.13) | copy-start | bytes 98308
  7.2 3.7 %copy-start.2 = (s32[512]{0:T(512)S(1)}, s32[512]{0:T(512)}, u32[]{:S(2)}) copy-start(s32[512]{0:T(512)} %param.12) | copy-start | bytes 6148
  7.2 100.9 %all-gather.3.cloned.1.call-start = ((), (), s32[]{:S(2)}) async-start(), calls=%async_computation.1 | async-start | bytes 17825792 | tf_op jit(solution)/shard_map/all_gather | solution.py:41
  108.1 16.4 %copy-start.3 = (bf16[8192,1024]{1,0:T(8,128)(2,1)S(1)}, bf16[8192,1024]{1,0:T(8,128)(2,1)}, u32[]{:S(2)}) copy-start(bf16[8192,1024]{1,0:T(8,128)(2,1)} %all-gather.3.cloned.1.call-done) | copy-start | bytes 50331652
  138.2 6.4 %collective-permute-start = (f32[520,64]{0,1:T(8,128)S(1)}, f32[520,64]{0,1:T(8,128)S(1)}, u32[]{:S(2)}, u32[]{:S(2)}) collective-permute-start(f32[520,64]{0,1:T(8,128)S(1)} %concatenate.6), channel_id=1, source_target_pairs={{0,2},{1,3},{2,0},{3,1},{4,6},{5,7},{6,4},{7,5},{8,10},{9,11},{10,... | collective-permute-start | bytes 399368 | tf_op jit(solution)/shard_map/ppermute | solution.py:22
  145.3 6.8 %collective-permute-start.1 = (f32[520,64]{0,1:T(8,128)S(1)}, f32[520,64]{0,1:T(8,128)S(1)}, u32[]{:S(2)}, u32[]{:S(2)}) collective-permute-start(f32[520,64]{0,1:T(8,128)S(1)} %pad_add_fusion), channel_id=1, source_target_pairs={{0,6},{1,7},{2,4},{3,5},{4,2},{5,3},{6,0},{7,1},{8,14},{9,15},{10,... | collective-permute-start | bytes 399368 | tf_op jit(solution)/shard_map/ppermute | solution.py:22
  152.1 7.9 %collective-permute-start.2 = (f32[520,64]{0,1:T(8,128)S(1)}, f32[520,64]{0,1:T(8,128)}, u32[]{:S(2)}, u32[]{:S(2)}) collective-permute-start(f32[520,64]{0,1:T(8,128)S(1)} %add.62), channel_id=1, source_target_pairs={{0,1},{1,0},{2,3},{3,2},{4,5},{5,4},{6,7},{7,6},{8,9},{9,8},{10,11... | collective-permute-start | bytes 399368 | tf_op jit(solution)/shard_map/ppermute | solution.py:22
  153.0 40.4 %all-to-all-start = ((bf16[8,64,1024]{2,1,0:T(8,128)(2,1)}), bf16[8,64,1024]{2,1,0:T(8,128)(2,1)S(1)}, u32[]{:S(2)}, u32[]{:S(2)}) async-start(bf16[8,64,1024]{2,1,0:T(8,128)(2,1)} %bitcast.17), calls=%async_computation | async-start | bytes 2097152 | tf_op jit(solution)/shard_map/all_to_all | solution.py:63
  163.7 2.0 collective-permute-start.3
  164.1 12.9 %collective-permute-start.7 = (f32[64,1024]{1,0:T(8,128)S(1)}, f32[64,1024]{1,0:T(8,128)S(1)}, u32[]{:S(2)}, u32[]{:S(2)}) collective-permute-start(f32[64,1024]{1,0:T(8,128)S(1)} %fusion.4), channel_id=1, source_target_pairs={{0,16},{8,24},{16,0},{24,8},{32,48},{40,56},{48,32},{56,40},{64,80... | collective-permute-start | bytes 786440 | tf_op jit(solution)/shard_map/ppermute | solution.py:22
  166.3 13.5 %collective-permute-start.4 = (f32[1032,64]{0,1:T(8,128)S(1)}, f32[1032,64]{0,1:T(8,128)S(1)}, u32[]{:S(2)}, u32[]{:S(2)}) collective-permute-start(f32[1032,64]{0,1:T(8,128)S(1)} %pad_add_fusion.1), channel_id=1, source_target_pairs={{0,32},{8,40},{16,48},{24,56},{32,0},{40,8},{48,16},{56,24},{64,96... | collective-permute-start | bytes 792584 | tf_op jit(solution)/shard_map/ppermute | solution.py:22
  177.0 9.8 %collective-permute-start.8 = (f32[64,1024]{1,0:T(8,128)S(1)}, f32[64,1024]{1,0:T(8,128)S(1)}, u32[]{:S(2)}, u32[]{:S(2)}) collective-permute-start(f32[64,1024]{1,0:T(8,128)S(1)} %add.68), channel_id=1, source_target_pairs={{0,96},{8,104},{16,112},{24,120},{32,64},{40,72},{48,80},{56,88},{... | collective-permute-start | bytes 786440 | tf_op jit(solution)/shard_map/ppermute | solution.py:22
  179.9 10.1 %collective-permute-start.5 = (f32[1032,64]{0,1:T(8,128)S(1)}, f32[1032,64]{0,1:T(8,128)S(1)}, u32[]{:S(2)}, u32[]{:S(2)}) collective-permute-start(f32[1032,64]{0,1:T(8,128)S(1)} %add.65), channel_id=1, source_target_pairs={{0,96},{8,104},{16,112},{24,120},{32,64},{40,72},{48,80},{56,88},{... | collective-permute-start | bytes 792584 | tf_op jit(solution)/shard_map/ppermute | solution.py:22
  186.9 6.5 %collective-permute-start.9 = (f32[64,1024]{1,0:T(8,128)S(1)}, f32[64,1024]{1,0:T(8,128)S(1)}, u32[]{:S(2)}, u32[]{:S(2)}) collective-permute-start(f32[64,1024]{1,0:T(8,128)S(1)} %add.69), channel_id=1, source_target_pairs={{0,32},{8,40},{16,48},{24,56},{32,0},{40,8},{48,16},{56,24},{64,96... | collective-permute-start | bytes 786440 | tf_op jit(solution)/shard_map/ppermute | solution.py:22
  190.0 6.8 %collective-permute-start.6 = (f32[1032,64]{0,1:T(8,128)S(1)}, f32[1032,64]{0,1:T(8,128)S(1)}, u32[]{:S(2)}, u32[]{:S(2)}) collective-permute-start(f32[1032,64]{0,1:T(8,128)S(1)} %add.66), channel_id=1, source_target_pairs={{0,16},{8,24},{16,0},{24,8},{32,48},{40,56},{48,32},{56,40},{64,80... | collective-permute-start | bytes 792584 | tf_op jit(solution)/shard_map/ppermute | solution.py:22
  193.3 1.6 collective-permute-start.10
Sparse Core Ops, SparseCore 0:
  9.7 98.3 all-gather.2

commit v11 on v10

--- a/solution.py
+++ b/solution.py
@@ -80,7 +80,7 @@
     middle_gradient = packed[:group].astype(jnp.bfloat16)
     loss_mp = packed[group, 0]
 
-    up_part = butterfly_sum(up_grad, "dp", (2, 12, 4, 1))
+    up_part = butterfly_sum(up_grad, "dp", (4, 12, 2, 1))
     down_grad = jnp.dot(my_rows.T, middle_gradient, preferred_element_type=jnp.float32)
     packed2 = jnp.concatenate([down_grad, jnp.broadcast_to(loss_mp, (8, rank))], axis=0)
     packed2 = butterfly_sum(packed2, "dp")

time: 205 us -> 206 us (level)
  starting transfers between devices: 18.4 us -> 22.4 us
  waiting for transfers between devices: 64.7 us -> 61.2 us
    ppermute x11, starting transfers between devices: 11.4 us -> 15.4 us  [butterfly_sum(): x = x + lax.ppermute(x, axis, [(i, i ^ mask) for i in range(n)])]
    ppermute x11, waiting for transfers between devices: 32.8 us -> 29.3 us  [butterfly_sum(): x = x + lax.ppermute(x, axis, [(i, i ^ mask) for i in range(n)])]
where the time goes in v11:
time: 206 us; the launch traced here: 205 us
  blocking collectives  64.6 us (31%)
  waiting for transfers between devices  61.2 us (30%)
  matrix products  32.3 us (16%)
  starting transfers between devices  22.4 us (11%)
  between operations  15.6 us (8%)
  other arithmetic  5.16 us (3%)
  local copies, waits for them, and re-layouts  4.16 us (2%)
    psum x1, blocking collectives, per_device(): rank_projection = lax.psum(low_part, 'mp').astype(jnp.bfloat16)  43.5 us
    all_gather x1, waiting for transfers between devices, per_device(): gathered = lax.all_gather(weight, 'dp', axis=0, tiled=True)  31.2 us
    ppermute x11, waiting for transfers between devices, butterfly_sum(): x = x + lax.ppermute(x, axis, [(i, i ^ mask) for i in range(n)])  29.3 us
    dot_general x2, matrix products, row_adder(): return jnp.dot(source, piece, preferred_element_type=jnp.float32)  26.8 us
    all_gather x1, blocking collectives, per_device(): all_flags = lax.all_gather(flags, 'dp', axis=0, tiled=True)  21.1 us
    ppermute x11, starting transfers between devices, butterfly_sum(): x = x + lax.ppermute(x, axis, [(i, i ^ mask) for i in range(n)])  15.4 us
    all_to_all x1, starting transfers between devices, per_device(): lax.all_to_all(updated_output.astype(jnp.bfloat16), 'mp', split_axis=0, c...  6.97 us
  transfers between devices with their start and end apart: 13, of which 9 were waited for; matrix products, arithmetic and copies ran while one was open for 5% of the time, Pallas kernels for 0%

profile of v11, /device:TPU:4, one launch (start us, length us, event | category | flops | bytes accessed | tf_op | source)
XLA Modules:
  0.0 205.4 jit_solution(18271727702532128318)
XLA Ops:
  7.2 0.0 copy-start
  7.2 0.0 all-gather.3.cloned.1.call-start
  7.2 0.7 all-gather.3.cloned.1.call-update
  7.9 1.7 fusion.2
  9.6 0.6 multiply_reduce_fusion.1
  10.9 21.1 %all-gather = s32[16,1,512]{2,1,0:T(1,128)S(1)} all-gather(s32[1,1,512]{2,1,0:T(1,128)S(1)} %bitcast.19), channel_id=1, replica_groups=mesh['dp'=16,'mp'=8] {'dp'}, dimensions={0}, use_global_device_ids=true | all-gather | bytes 34816 | tf_op jit(solution)/shard_map/all_gather | solution.py:47
  32.0 0.7 reduce_sum.36
  33.4 43.5 %all-reduce.3 = bf16[512,64]{0,1:T(8,128)(2,1)S(1)} all-reduce(f32[512,64]{0,1:T(8,128)S(1)} %fusion.2), channel_id=1, replica_groups=mesh['dp'=16,'mp'=8] {'mp'}, use_global_device_ids=true, to_apply=%region_0.0 | all-reduce | flops 32768 | bytes 196608 | tf_op jit(solution)/shard_map/psum | solution.py:45
  76.9 31.2 %all-gather.3.cloned.1.call-done = bf16[8192,1024]{1,0:T(8,128)(2,1)} async-done(((bf16[512,1024]{1,0:T(8,128)(2,1)}), bf16[8192,1024]{1,0:T(8,128)(2,1)}) %all-gather.3.cloned.1.call-update) | async-done | bytes 16777232 | tf_op jit(solution)/shard_map/all_gather | solution.py:41
  108.1 14.9 %convolution_convert_fusion.1 = bf16[512,1024]{1,0:T(8,128)(2,1)S(1)} fusion(bf16[512,8192]{1,0:T(8,128)(2,1)} %param.8, bf16[8192,1024]{1,0:T(8,128)(2,1)} %all-gather.3.cloned.1.call-done), kind=kOutput, calls=%fused_computation.5 | convolution fusion | flops 8590458880 | bytes 26214400 | tf_op jit(solution)/shard_map/dot_general | solution.py:13
  123.1 1.4 fusion.10
  124.5 11.9 %multiply_reduce_fusion = (f32[512]{0:T(512)S(1)}, f32[512,1024]{1,0:T(8,128)S(1)}) fusion(f32[512,1024]{1,0:T(8,128)S(1)} %get-tuple-element.9, bf16[512,8192]{1,0:T(8,128)(2,1)} %param.7, bf16[8192,1024]{1,0:T(8,128)(2,1)S(1)} %copy-done.3, f32[512]{0:T(512)S(1)} %get-tuple-element.7, f32[1024]{0:T(1024)S(1)} %dynamic-slice_multiply_fusion, ...), kind=kOutput, calls=%fused_computation | convolution fusion | flops 8594128896 | bytes 29370368 | tf_op jit(solution)/shard_map/dot_general | solution.py:13
  136.4 0.6 multiply_reduce_fusion.2
  137.0 0.5 fusion.9
  137.5 0.7 concatenate.6
  138.2 1.6 collective-permute-start
  139.8 4.9 %collective-permute-done = f32[520,64]{0,1:T(8,128)S(1)} collective-permute-done((f32[520,64]{0,1:T(8,128)S(1)}, f32[520,64]{0,1:T(8,128)S(1)}, u32[]{:S(2)}, u32[]{:S(2)}) %collective-permute-start) | collective-permute-done | bytes 133152 | tf_op jit(solution)/shard_map/ppermute | solution.py:22
  144.6 0.7 pad_add_fusion
  145.3 2.8 %collective-permute-start.1 = (f32[520,64]{0,1:T(8,128)S(1)}, f32[520,64]{0,1:T(8,128)S(1)}, u32[]{:S(2)}, u32[]{:S(2)}) collective-permute-start(f32[520,64]{0,1:T(8,128)S(1)} %pad_add_fusion), channel_id=1, source_target_pairs={{0,6},{1,7},{2,4},{3,5},{4,2},{5,3},{6,0},{7,1},{8,14},{9,15},{10,... | collective-permute-start | bytes 399368 | tf_op jit(solution)/shard_map/ppermute | solution.py:22
  148.1 4.0 %collective-permute-done.1 = f32[520,64]{0,1:T(8,128)S(1)} collective-permute-done((f32[520,64]{0,1:T(8,128)S(1)}, f32[520,64]{0,1:T(8,128)S(1)}, u32[]{:S(2)}, u32[]{:S(2)}) %collective-permute-start.1) | collective-permute-done | bytes 133152 | tf_op jit(solution)/shard_map/ppermute | solution.py:22
  152.1 0.9 collective-permute-start.2
  153.0 7.0 %all-to-all-start = ((bf16[8,64,1024]{2,1,0:T(8,128)(2,1)}), bf16[8,64,1024]{2,1,0:T(8,128)(2,1)S(1)}, u32[]{:S(2)}, u32[]{:S(2)}) async-start(bf16[8,64,1024]{2,1,0:T(8,128)(2,1)} %bitcast.17), calls=%async_computation | async-start | bytes 2097152 | tf_op jit(solution)/shard_map/all_to_all | solution.py:63
  160.0 0.0 collective-permute-done.2
  160.0 0.9 add.63
  160.9 1.5 fusion
  162.5 0.5 slice.18
  163.0 0.7 concatenate.7
  163.7 0.1 collective-permute-start.3
  163.8 0.4 fusion.4
  164.1 0.1 collective-permute-start.7
  164.2 1.1 collective-permute-done.3
  165.3 0.7 pad_add_fusion.1
  166.0 1.0 collective-permute-start.4
  167.0 6.4 %collective-permute-done.7 = f32[64,1024]{1,0:T(8,128)S(1)} collective-permute-done((f32[64,1024]{1,0:T(8,128)S(1)}, f32[64,1024]{1,0:T(8,128)S(1)}, u32[]{:S(2)}, u32[]{:S(2)}) %collective-permute-start.7) | collective-permute-done | bytes 262176 | tf_op jit(solution)/shard_map/ppermute | solution.py:22
  173.4 3.2 %collective-permute-start.8 = (f32[64,1024]{1,0:T(8,128)S(1)}, f32[64,1024]{1,0:T(8,128)S(1)}, u32[]{:S(2)}, u32[]{:S(2)}) collective-permute-start(f32[64,1024]{1,0:T(8,128)S(1)} %add.68), channel_id=1, source_target_pairs={{0,96},{8,104},{16,112},{24,120},{32,64},{40,72},{48,80},{56,88},{... | collective-permute-start | bytes 786440 | tf_op jit(solution)/shard_map/ppermute | solution.py:22
  176.7 2.6 %collective-permute-done.4 = f32[1032,64]{0,1:T(8,128)S(1)} collective-permute-done((f32[1032,64]{0,1:T(8,128)S(1)}, f32[1032,64]{0,1:T(8,128)S(1)}, u32[]{:S(2)}, u32[]{:S(2)}) %collective-permute-start.4) | collective-permute-done | bytes 264224 | tf_op jit(solution)/shard_map/ppermute | solution.py:22
  179.3 3.2 %collective-permute-start.5 = (f32[1032,64]{0,1:T(8,128)S(1)}, f32[1032,64]{0,1:T(8,128)S(1)}, u32[]{:S(2)}, u32[]{:S(2)}) collective-permute-start(f32[1032,64]{0,1:T(8,128)S(1)} %add.65), channel_id=1, source_target_pairs={{0,96},{8,104},{16,112},{24,120},{32,64},{40,72},{48,80},{56,88},{... | collective-permute-start | bytes 792584 | tf_op jit(solution)/shard_map/ppermute | solution.py:22
  182.5 0.0 collective-permute-done.8
  182.5 1.1 collective-permute-start.9
  183.6 5.7 %collective-permute-done.5 = f32[1032,64]{0,1:T(8,128)S(1)} collective-permute-done((f32[1032,64]{0,1:T(8,128)S(1)}, f32[1032,64]{0,1:T(8,128)S(1)}, u32[]{:S(2)}, u32[]{:S(2)}) %collective-permute-start.5) | collective-permute-done | bytes 264224 | tf_op jit(solution)/shard_map/ppermute | solution.py:22
  189.3 1.3 collective-permute-start.6
  190.7 0.1 collective-permute-start.10
  190.8 1.1 copy.13
  191.8 0.5 collective-permute-done.10
  192.3 0.7 add.71
  193.0 4.3 %collective-permute-done.6 = f32[1032,64]{0,1:T(8,128)S(1)} collective-permute-done((f32[1032,64]{0,1:T(8,128)S(1)}, f32[1032,64]{0,1:T(8,128)S(1)}, u32[]{:S(2)}, u32[]{:S(2)}) %collective-permute-start.6) | collective-permute-done | bytes 264224 | tf_op jit(solution)/shard_map/ppermute | solution.py:22
  197.3 0.7 slice.19
  198.1 0.5 slice.20
  (19 shorter events, 0.3 us)
Async XLA Ops:
  7.2 115.9 %copy-start = (bf16[64,1024]{1,0:T(8,128)(2,1)S(1)}, bf16[64,1024]{1,0:T(8,128)(2,1)}, u32[]{:S(2)}) copy-start(bf16[64,1024]{1,0:T(8,128)(2,1)} %param.11) | copy-start | bytes 393220
  7.2 2.4 %copy-start.1 = (f32[8192]{0:T(1024)S(1)}, f32[8192]{0:T(1024)}, u32[]{:S(2)}) copy-start(f32[8192]{0:T(1024)} %param.13) | copy-start | bytes 98308
  7.2 3.7 %copy-start.2 = (s32[512]{0:T(512)S(1)}, s32[512]{0:T(512)}, u32[]{:S(2)}) copy-start(s32[512]{0:T(512)} %param.12) | copy-start | bytes 6148
  7.2 100.9 %all-gather.3.cloned.1.call-start = ((), (), s32[]{:S(2)}) async-start(), calls=%async_computation.1 | async-start | bytes 17825792 | tf_op jit(solution)/shard_map/all_gather | solution.py:41
  108.1 16.4 %copy-start.3 = (bf16[8192,1024]{1,0:T(8,128)(2,1)S(1)}, bf16[8192,1024]{1,0:T(8,128)(2,1)}, u32[]{:S(2)}) copy-start(bf16[8192,1024]{1,0:T(8,128)(2,1)} %all-gather.3.cloned.1.call-done) | copy-start | bytes 50331652
  138.2 6.4 %collective-permute-start = (f32[520,64]{0,1:T(8,128)S(1)}, f32[520,64]{0,1:T(8,128)S(1)}, u32[]{:S(2)}, u32[]{:S(2)}) collective-permute-start(f32[520,64]{0,1:T(8,128)S(1)} %concatenate.6), channel_id=1, source_target_pairs={{0,2},{1,3},{2,0},{3,1},{4,6},{5,7},{6,4},{7,5},{8,10},{9,11},{10,... | collective-permute-start | bytes 399368 | tf_op jit(solution)/shard_map/ppermute | solution.py:22
  145.3 6.8 %collective-permute-start.1 = (f32[520,64]{0,1:T(8,128)S(1)}, f32[520,64]{0,1:T(8,128)S(1)}, u32[]{:S(2)}, u32[]{:S(2)}) collective-permute-start(f32[520,64]{0,1:T(8,128)S(1)} %pad_add_fusion), channel_id=1, source_target_pairs={{0,6},{1,7},{2,4},{3,5},{4,2},{5,3},{6,0},{7,1},{8,14},{9,15},{10,... | collective-permute-start | bytes 399368 | tf_op jit(solution)/shard_map/ppermute | solution.py:22
  152.1 7.9 %collective-permute-start.2 = (f32[520,64]{0,1:T(8,128)S(1)}, f32[520,64]{0,1:T(8,128)}, u32[]{:S(2)}, u32[]{:S(2)}) collective-permute-start(f32[520,64]{0,1:T(8,128)S(1)} %add.62), channel_id=1, source_target_pairs={{0,1},{1,0},{2,3},{3,2},{4,5},{5,4},{6,7},{7,6},{8,9},{9,8},{10,11... | collective-permute-start | bytes 399368 | tf_op jit(solution)/shard_map/ppermute | solution.py:22
  153.0 37.7 %all-to-all-start = ((bf16[8,64,1024]{2,1,0:T(8,128)(2,1)}), bf16[8,64,1024]{2,1,0:T(8,128)(2,1)S(1)}, u32[]{:S(2)}, u32[]{:S(2)}) async-start(bf16[8,64,1024]{2,1,0:T(8,128)(2,1)} %bitcast.17), calls=%async_computation | async-start | bytes 2097152 | tf_op jit(solution)/shard_map/all_to_all | solution.py:63
  163.7 1.7 collective-permute-start.3
  164.1 9.3 %collective-permute-start.7 = (f32[64,1024]{1,0:T(8,128)S(1)}, f32[64,1024]{1,0:T(8,128)S(1)}, u32[]{:S(2)}, u32[]{:S(2)}) collective-permute-start(f32[64,1024]{1,0:T(8,128)S(1)} %fusion.4), channel_id=1, source_target_pairs={{0,32},{8,40},{16,48},{24,56},{32,0},{40,8},{48,16},{56,24},{64,96... | collective-permute-start | bytes 786440 | tf_op jit(solution)/shard_map/ppermute | solution.py:22
  166.0 13.2 %collective-permute-start.4 = (f32[1032,64]{0,1:T(8,128)S(1)}, f32[1032,64]{0,1:T(8,128)S(1)}, u32[]{:S(2)}, u32[]{:S(2)}) collective-permute-start(f32[1032,64]{0,1:T(8,128)S(1)} %pad_add_fusion.1), channel_id=1, source_target_pairs={{0,32},{8,40},{16,48},{24,56},{32,0},{40,8},{48,16},{56,24},{64,96... | collective-permute-start | bytes 792584 | tf_op jit(solution)/shard_map/ppermute | solution.py:22
  173.4 9.1 %collective-permute-start.8 = (f32[64,1024]{1,0:T(8,128)S(1)}, f32[64,1024]{1,0:T(8,128)S(1)}, u32[]{:S(2)}, u32[]{:S(2)}) collective-permute-start(f32[64,1024]{1,0:T(8,128)S(1)} %add.68), channel_id=1, source_target_pairs={{0,96},{8,104},{16,112},{24,120},{32,64},{40,72},{48,80},{56,88},{... | collective-permute-start | bytes 786440 | tf_op jit(solution)/shard_map/ppermute | solution.py:22
  179.3 10.0 %collective-permute-start.5 = (f32[1032,64]{0,1:T(8,128)S(1)}, f32[1032,64]{0,1:T(8,128)S(1)}, u32[]{:S(2)}, u32[]{:S(2)}) collective-permute-start(f32[1032,64]{0,1:T(8,128)S(1)} %add.65), channel_id=1, source_target_pairs={{0,96},{8,104},{16,112},{24,120},{32,64},{40,72},{48,80},{56,88},{... | collective-permute-start | bytes 792584 | tf_op jit(solution)/shard_map/ppermute | solution.py:22
  182.5 8.1 %collective-permute-start.9 = (f32[64,1024]{1,0:T(8,128)S(1)}, f32[64,1024]{1,0:T(8,128)S(1)}, u32[]{:S(2)}, u32[]{:S(2)}) collective-permute-start(f32[64,1024]{1,0:T(8,128)S(1)} %add.69), channel_id=1, source_target_pairs={{0,16},{8,24},{16,0},{24,8},{32,48},{40,56},{48,32},{56,40},{64,80... | collective-permute-start | bytes 786440 | tf_op jit(solution)/shard_map/ppermute | solution.py:22
  189.3 8.0 %collective-permute-start.6 = (f32[1032,64]{0,1:T(8,128)S(1)}, f32[1032,64]{0,1:T(8,128)S(1)}, u32[]{:S(2)}, u32[]{:S(2)}) collective-permute-start(f32[1032,64]{0,1:T(8,128)S(1)} %add.66), channel_id=1, source_target_pairs={{0,16},{8,24},{16,0},{24,8},{32,48},{40,56},{48,32},{56,40},{64,80... | collective-permute-start | bytes 792584 | tf_op jit(solution)/shard_map/ppermute | solution.py:22
  190.7 1.6 collective-permute-start.10
Sparse Core Ops, SparseCore 0:
  9.7 98.3 all-gather.2
